TPU v7x, 1024 devices: a whole 4x8x16 slice. The times are simulated.
1024 devices in a mesh: ctx: 32 (over z_lo, x, core), exp: 8 (over y), dp: 4 (over z_hi).
Axes of the slice: x: 4, y: 8, z: 16 (z_hi: 4, z_lo: 4; z = z_hi * 4 + z_lo), core: 2. Of those that a mesh axis runs over, the one named last changes fastest.
Arguments:
- queries: bfloat16 [4, 8192, 6144], P('dp', 'ctx', 'exp'), may hold values from -4 to 4
- key_rows: bfloat16 [4, 8192, 1024], P('dp', 'ctx', 'exp'), may hold values from -4 to 4
- value_rows: bfloat16 [4, 8192, 1024], P('dp', 'ctx', 'exp'), may hold values from -6 to 6
- out_grad: bfloat16 [4, 8192, 6144], P('dp', 'ctx', 'exp'), may hold values from -6 to 6
- log_norm: float32 [4, 48, 8192], P('dp', 'exp', 'ctx'), may hold values from 1 to 3
- row_delta: float32 [4, 48, 8192], P('dp', 'exp', 'ctx'), may hold values from -16 to 16
- tok_grad: bfloat16 [4, 8192, 6144], P('dp', ('ctx', 'exp')), may hold values from -6 to 6
- router_prob: float32 [4, 8192, 2], P('dp', ('ctx', 'exp')), may hold values from 0.2 to 1
- expert_ids: int32 [4, 8192, 2], P('dp', ('ctx', 'exp')), may hold values from 0 to 7, all different within a row; in each aligned block of 32 rows (0 to 31, 32 to 63, ..., all dimensions but the last counted through in order) at most 16 rows name the same one
- saved_pre: bfloat16 [8, 32, 4, 128, 256], P('exp', 'ctx', 'dp'), may hold values from -4 to 4
- w_down: bfloat16 [8, 128, 6144], P('exp'), may hold values from -0.078125 to 0.078125
Outputs:
- query_grad: bfloat16 [4, 8192, 6144], P('dp', 'ctx', 'exp')
- key_grad: bfloat16 [4, 8192, 1024], P('dp', 'ctx', 'exp')
- value_grad: bfloat16 [4, 8192, 1024], P('dp', 'ctx', 'exp')
- pre_grad: bfloat16 [8, 32, 4, 128, 256], P('exp', 'ctx', 'dp')
- weight_grad: float32 [8, 6144, 128], P('exp', ('ctx', 'dp'))
Inputs may be any that keep to these rules, and one draw needn't show every extreme that they name: `expert_ids`: the two experts of a token differ; among the 32 tokens of one device each expert is named by at most 16 tokens, a bound that some block reaches.
All inputs are finite; a program needn't handle non-finite values.
Results may differ from a plain program's by a relative error of at most 0.0068.
Values may be sent and summed in bfloat16 or wider, within the bound.
No kernel may reach another device: no remote copies, remote signals or barrier semaphores. Data moves between devices by JAX's collectives and lax.ppermute only.
A program may use at most 32 MiB of HBM per device.

v0:
```python
import jax
import jax.numpy as jnp
from jax import lax
from jax.sharding import PartitionSpec as P

HEADS = 48
KV_HEADS = 8
HEAD_DIM = 128


def passed_along(value, axis, by):
    size = lax.axis_size(axis)
    pairs = [(i, i + by) for i in range(size) if 0 <= i + by < size]
    return lax.ppermute(value, axis, pairs)


def from_behind(block, axis, distance):
    devices = range(lax.axis_size(axis))
    route = [((i - distance) % len(devices), i) for i in devices]
    return lax.ppermute(block, axis, route)


def pair_grads(query_rows, grad_rows, norm_rows, delta_rows, both_block):
    head_sets = query_rows.shape[0]
    length = both_block.shape[1]
    factor = HEAD_DIM ** (-0.5)
    key_part = both_block[0].reshape(length, head_sets, HEAD_DIM).transpose(1, 0, 2)
    value_part = both_block[1].reshape(length, head_sets, HEAD_DIM).transpose(1, 0, 2)
    scores = (
        jnp.einsum("kqd,kud->kqu", query_rows, key_part, preferred_element_type=jnp.float32)
        * factor
    )
    weights = jnp.exp(scores - norm_rows[:, :, None])
    weights_low = weights.astype(jnp.bfloat16)
    prob_grad = jnp.einsum(
        "kqd,kud->kqu", grad_rows, value_part, preferred_element_type=jnp.float32
    )
    score_grad = (weights * (prob_grad - delta_rows[:, :, None])).astype(jnp.bfloat16)
    query_out = (
        jnp.einsum("kqu,kud->kqd", score_grad, key_part, preferred_element_type=jnp.float32)
        * factor
    )
    key_out = (
        jnp.einsum("kqu,kqd->kud", score_grad, query_rows, preferred_element_type=jnp.float32)
        * factor
    )
    value_out = jnp.einsum(
        "kqu,kqd->kud", weights_low, grad_rows, preferred_element_type=jnp.float32
    )
    return (query_out, key_out, value_out)


def body(
    queries,
    key_rows,
    value_rows,
    out_grad,
    log_norm,
    row_delta,
    tok_grad,
    router_prob,
    expert_ids,
    saved_pre,
    w_down,
):
    length = queries.shape[1]
    head_sets = key_rows.shape[2] // HEAD_DIM
    group_size = HEADS // KV_HEADS
    position = lax.axis_index("ctx")

    def by_head(array):
        shaped = array[0].reshape(length, head_sets, group_size, HEAD_DIM).transpose(1, 2, 0, 3)
        return shaped.reshape(head_sets, group_size * length, HEAD_DIM)

    query_rows = by_head(queries)
    grad_rows = by_head(out_grad)
    norm_rows = log_norm[0].reshape(head_sets, group_size * length)
    delta_rows = row_delta[0].reshape(head_sets, group_size * length)
    both_local = jnp.stack([key_rows[0], value_rows[0]])
    carried_blocks = []
    current = both_local
    for repeat in range(2):
        current = passed_along(current, "ctx", 1)
        carried_blocks.append(current)
    nearer = carried_blocks[0]
    farther = carried_blocks[1]
    near_mask = (position >= 1).astype(jnp.float32)
    far_mask = (position >= 2).astype(jnp.float32)
    query_near, key_near, value_near = pair_grads(
        query_rows, grad_rows, norm_rows, delta_rows, nearer
    )
    outgoing = (jnp.stack([key_near, value_near]) * near_mask).astype(jnp.bfloat16)
    arrived = from_behind(outgoing, "ctx", 1)
    query_far, key_far, value_far = pair_grads(
        query_rows, grad_rows, norm_rows, delta_rows, farther
    )
    query_total = query_near * near_mask + query_far * far_mask
    query_grad = query_total.reshape(head_sets, group_size, length, HEAD_DIM).transpose(2, 0, 1, 3)
    query_grad = query_grad.reshape(1, length, head_sets * group_size * HEAD_DIM).astype(
        jnp.bfloat16
    )
    both_total = (arrived.astype(jnp.float32) + jnp.stack([key_far, value_far]) * far_mask).astype(
        jnp.bfloat16
    )
    key_grad = both_total[0].transpose(1, 0, 2).reshape(1, length, head_sets * HEAD_DIM)
    value_grad = both_total[1].transpose(1, 0, 2).reshape(1, length, head_sets * HEAD_DIM)
    expert_count = lax.axis_size("exp")
    capacity = saved_pre.shape[3] // expert_count
    model_width = tok_grad.shape[2]
    pair_count = tok_grad.shape[1] * 2
    routed = (router_prob[0][:, :, None] * tok_grad[0].astype(jnp.float32)[:, None, :]).astype(
        jnp.bfloat16
    )
    routed = routed.reshape(pair_count, model_width)
    flat_ids = expert_ids[0].reshape(pair_count)
    matches = (flat_ids[:, None] == jnp.arange(expert_count, dtype=jnp.int32)[None, :]).astype(
        jnp.int32
    )
    earlier = jnp.cumsum(matches, axis=0) - matches
    place = jnp.sum(earlier * matches, axis=1)
    slot_index = flat_ids * capacity + place
    table = (
        jnp.arange(expert_count * capacity, dtype=jnp.int32)[:, None] == slot_index[None, :]
    ).astype(jnp.bfloat16)
    outbound = jnp.dot(table, routed, preferred_element_type=jnp.float32).astype(jnp.bfloat16)
    incoming_block = lax.all_to_all(outbound, "exp", split_axis=0, concat_axis=0, tiled=True)
    saved = saved_pre[0, 0, 0].astype(jnp.float32)
    hidden_units = saved.shape[1] // 2
    gate = saved[:, :hidden_units]
    upward = saved[:, hidden_units:]
    sigma = jax.nn.sigmoid(gate)
    active = gate * sigma
    hidden_state = (active * upward).astype(jnp.bfloat16)
    hidden_gradient = jnp.einsum(
        "rd,fd->rf", incoming_block, w_down[0], preferred_element_type=jnp.float32
    )
    gate_grad = hidden_gradient * upward * sigma * (1.0 + gate * (1.0 - sigma))
    up_grad = hidden_gradient * active
    pre_grad = jnp.concatenate([gate_grad, up_grad], axis=-1).astype(jnp.bfloat16)[None, None, None]
    ctx_count = lax.axis_size("ctx")
    data_count = lax.axis_size("dp")
    averaging = 1.0 / (ctx_count * data_count)
    summed = lax.psum_scatter(
        jnp.einsum("rc,rf->cf", incoming_block, hidden_state, preferred_element_type=jnp.float32),
        ("ctx", "dp"),
        scatter_dimension=0,
        tiled=True,
    )
    weight_grad = (summed * averaging)[None]
    return (query_grad, key_grad, value_grad, pre_grad, weight_grad)


def solution(mesh):
    placed = (
        P("dp", "ctx", "exp"),
        P("dp", "ctx", "exp"),
        P("dp", "ctx", "exp"),
        P("dp", "ctx", "exp"),
        P("dp", "exp", "ctx"),
        P("dp", "exp", "ctx"),
        P("dp", ("ctx", "exp"), None),
        P("dp", ("ctx", "exp"), None),
        P("dp", ("ctx", "exp"), None),
        P("exp", "ctx", "dp", None, None),
        P("exp", None, None),
    )
    return jax.shard_map(
        body,
        mesh=mesh,
        in_specs=placed,
        out_specs=(
            P("dp", "ctx", "exp"),
            P("dp", "ctx", "exp"),
            P("dp", "ctx", "exp"),
            P("exp", "ctx", "dp", None, None),
            P("exp", ("ctx", "dp"), None),
        ),
        check_vma=False,
    )
```

profile of v0, /device:TPU:64, one launch (start us, length us, event | category | flops | bytes accessed | tf_op | source)
XLA Modules:
  0.0 827.2 jit_solution(11760120661079209610)
XLA Ops:
  7.2 0.9 copy.26
  8.1 0.1 reshape_squeeze.11
  8.2 0.1 fusion.24
  8.2 0.1 reduce_window_sum.11
  8.3 0.2 select_reduce_fusion
  8.5 1.1 bitcast_convert_fusion
  9.6 2.0 mul.161
  11.6 2.4 mul.162
  14.0 0.1 copy.27
  14.1 0.1 mul.159
  14.2 1.8 convolution_convert_fusion
  16.0 7.2 all-to-all-start
  23.3 0.1 copy.28
  23.4 39.8 %all-to-all-done = bf16[8,16,6144]{2,1,0:T(8,128)(2,1)S(1)} async-done(((bf16[8,16,6144]{2,1,0:T(8,128)(2,1)}), bf16[8,16,6144]{2,1,0:T(8,128)(2,1)S(1)}, u32[]{:S(2)}, u32[]{:S(2)}) %all-to-all-start) | async-done | bytes 1572896 | tf_op jit(solution)/shard_map/all_to_all | solution.py:126
  63.2 2.3 fusion.22
  65.5 0.8 copy-done.9
  66.3 0.7 pad_maximum_fusion
  67.0 1.9 collective-permute-start
  68.9 1.2 copy.21
  70.1 0.9 copy.22
  71.1 1.9 copy.23
  73.0 1.2 copy.24
  74.2 0.6 reduce.1
  74.9 0.7 sub.49
  75.6 0.1 collective-permute-done
  75.7 1.4 fusion.4
  77.1 1.3 fusion.6
  78.4 0.4 fusion.13
  78.8 0.4 convolution_bitcast_fusion.1
  79.1 0.7 fusion.17
  79.8 3.3 collective-permute-start.2
  83.1 1.9 collective-permute-start.1
  85.1 1.3 convolution_multiply_fusion.3
  86.3 5.4 collective-permute-done.1
  91.8 0.4 fusion.5
  92.1 0.4 fusion.7
  92.5 1.1 copy-done.4
  93.6 1.2 fusion.9
  94.8 1.9 copy.25
  96.7 1.9 copy.29
  98.6 1.9 convolution_bitcast_fusion
  100.5 0.4 fusion.12
  100.9 0.9 fusion.19
  101.8 0.7 slice_bitcast_fusion
  102.5 0.6 fusion.25
  103.1 0.7 copy.30
  103.8 715.1 %reduce-scatter.2.cloned.1.call-done = f32[48,128]{1,0:T(8,128)} async-done(((f32[6144,128]{1,0:T(8,128)}), f32[48,128]{1,0:T(8,128)}) %reduce-scatter.2.cloned.1.call-update) | async-done | bytes 24592 | tf_op jit(solution)/shard_map/reduce_scatter | solution.py:143
  819.0 1.3 multiply_bitcast_fusion
  (34 shorter events, 0.2 us)
Async XLA Ops:
  7.2 95.3 %copy-start = (bf16[1,128,6144]{2,1,0:T(8,128)(2,1)S(1)}, bf16[1,128,6144]{2,1,0:T(8,128)(2,1)}, u32[]{:S(2)}) copy-start(bf16[1,128,6144]{2,1,0:T(8,128)(2,1)} %param.21) | copy-start | bytes 4718596
  11.6 2.4 copy-start.13
  16.0 7.3 copy-start.8
  16.0 47.2 %all-to-all-start = ((bf16[8,16,6144]{2,1,0:T(8,128)(2,1)}), bf16[8,16,6144]{2,1,0:T(8,128)(2,1)S(1)}, u32[]{:S(2)}, u32[]{:S(2)}) async-start(bf16[8,16,6144]{2,1,0:T(8,128)(2,1)} %bitcast.81), calls=%async_computation | async-start | bytes 3145728 | tf_op jit(solution)/shard_map/all_to_all | solution.py:126
  23.2 795.7 %reduce-scatter.2.cloned.1.call-start = ((), (), s32[]{:S(2)}) async-start(), calls=%async_computation.2 | async-start | bytes 3170304 | tf_op jit(solution)/shard_map/reduce_scatter | solution.py:143
  23.4 42.0 %copy-start.6 = (f32[128,256]{0,1:T(8,128)}, f32[128,256]{0,1:T(8,128)S(1)}, u32[]{:S(2)}) copy-start(f32[128,256]{0,1:T(8,128)S(1)} %bitcast_convert_fusion.1) | copy-start | bytes 393220
  65.5 0.8 copy-start.9
  65.5 0.9 copy-start.10
  66.3 4.7 copy-start.11
  67.0 8.7 %collective-permute-start = (bf16[2,256,128]{2,1,0:T(8,128)(2,1)}, bf16[2,256,128]{2,1,0:T(8,128)(2,1)}, u32[]{:S(2)}, u32[]{:S(2)}) collective-permute-start(bf16[2,256,128]{2,1,0:T(8,128)(2,1)} %pad_maximum_fusion), channel_id=1, source_target_pairs={{0,32},{32,64},{64,96},{96,128},{128,160},{160,192},{192,224},{224... | collective-permute-start | bytes 393224 | tf_op jit(solution)/shard_map/ppermute | solution.py:14
  68.9 5.3 copy-start.12
  77.1 1.3 copy-start.2
  79.8 21.1 %collective-permute-start.2 = (bf16[2,1,256,128]{3,2,1,0:T(8,128)(2,1)}, bf16[2,1,256,128]{3,2,1,0:T(8,128)(2,1)}, u32[]{:S(2)}, u32[]{:S(2)}) collective-permute-start(bf16[2,1,256,128]{3,2,1,0:T(8,128)(2,1)} %fusion.17), channel_id=1, source_target_pairs={{992,0},{0,32},{32,64},{64,96},{96,128},{128,160},{160,192},{192,2... | collective-permute-start | bytes 393224 | tf_op jit(solution)/shard_map/ppermute | solution.py:20
  83.1 8.6 %collective-permute-start.1 = (bf16[2,256,128]{2,1,0:T(8,128)(2,1)}, bf16[2,256,128]{2,1,0:T(8,128)(2,1)S(1)}, u32[]{:S(2)}, u32[]{:S(2)}) collective-permute-start(bf16[2,256,128]{2,1,0:T(8,128)(2,1)} %collective-permute-done), channel_id=1, source_target_pairs={{0,32},{32,64},{64,96},{96,128},{128,160},{160,192},{192,224},{224... | collective-permute-start | bytes 393224 | tf_op jit(solution)/shard_map/ppermute | solution.py:14
  92.1 2.7 copy-start.1
  92.5 1.1 copy-start.4
  98.6 1.9 copy-start.3
  98.6 1.9 copy-start.5
  100.5 2.0 copy-start.7
Sparse Core Ops, SparseCore 0:
  65.6 753.3 reduce-scatter.1
where the time goes:
time: 828 us; the launch traced here: 827 us
  waiting for transfers between devices  760 us (92%)
  local copies, waits for them, and re-layouts  18.9 us (2%)
  starting transfers between devices  14.4 us (2%)
  between operations  14.3 us (2%)
  matrix products  13.4 us (2%)
    reduce_scatter x1, waiting for transfers between devices, body(): lax.psum_scatter(jnp.einsum('rc,rf->cf', incoming_block, hidden_state, pr...  715 us
    all_to_all x1, waiting for transfers between devices, body(): lax.all_to_all(outbound, 'exp', split_axis=0, concat_axis=0, tiled=True)  39.8 us
  transfers between devices with their start and end apart: 5, of which 4 were waited for; matrix products, arithmetic and copies ran while one was open for 3% of the time, Pallas kernels for 0%

commit v1 on v0

--- a/solution.py
+++ b/solution.py
@@ -1,11 +1,13 @@
 import jax
 import jax.numpy as jnp
 from jax import lax
-from jax.sharding import PartitionSpec as P
+from jax.sharding import Mesh, PartitionSpec as P
 
 HEADS = 48
 KV_HEADS = 8
 HEAD_DIM = 128
+CTX = ("zl", "xx", "core")
+ROW_AXES = ("zl", "xx", "core", "dp")
 
 
 def passed_along(value, axis, by):
@@ -50,6 +52,16 @@
     return (query_out, key_out, value_out)
 
 
+def staged_reduce_scatter(partial):
+    rows, width = partial.shape
+    sizes = [lax.axis_size(name) for name in ROW_AXES]
+    block = rows // (sizes[0] * sizes[1] * sizes[2] * sizes[3])
+    pieces = partial.reshape(*sizes, block, width).transpose(2, 1, 0, 3, 4, 5)
+    for name in ("core", "xx", "zl", "dp"):
+        pieces = lax.all_to_all(pieces, name, 0, 0, tiled=True).sum(0)
+    return pieces.reshape(block, width)
+
+
 def body(
     queries,
     key_rows,
@@ -66,7 +78,7 @@
     length = queries.shape[1]
     head_sets = key_rows.shape[2] // HEAD_DIM
     group_size = HEADS // KV_HEADS
-    position = lax.axis_index("ctx")
+    position = lax.axis_index(CTX)
 
     def by_head(array):
         shaped = array[0].reshape(length, head_sets, group_size, HEAD_DIM).transpose(1, 2, 0, 3)
@@ -80,7 +92,7 @@
     carried_blocks = []
     current = both_local
     for repeat in range(2):
-        current = passed_along(current, "ctx", 1)
+        current = passed_along(current, CTX, 1)
         carried_blocks.append(current)
     nearer = carried_blocks[0]
     farther = carried_blocks[1]
@@ -90,7 +102,7 @@
         query_rows, grad_rows, norm_rows, delta_rows, nearer
     )
     outgoing = (jnp.stack([key_near, value_near]) * near_mask).astype(jnp.bfloat16)
-    arrived = from_behind(outgoing, "ctx", 1)
+    arrived = from_behind(outgoing, CTX, 1)
     query_far, key_far, value_far = pair_grads(
         query_rows, grad_rows, norm_rows, delta_rows, farther
     )
@@ -137,43 +149,41 @@
     gate_grad = hidden_gradient * upward * sigma * (1.0 + gate * (1.0 - sigma))
     up_grad = hidden_gradient * active
     pre_grad = jnp.concatenate([gate_grad, up_grad], axis=-1).astype(jnp.bfloat16)[None, None, None]
-    ctx_count = lax.axis_size("ctx")
-    data_count = lax.axis_size("dp")
-    averaging = 1.0 / (ctx_count * data_count)
-    summed = lax.psum_scatter(
-        jnp.einsum("rc,rf->cf", incoming_block, hidden_state, preferred_element_type=jnp.float32),
-        ("ctx", "dp"),
-        scatter_dimension=0,
-        tiled=True,
-    )
+    averaging = 1.0 / lax.axis_size(ROW_AXES)
+    partial = jnp.einsum("rc,rf->cf", incoming_block, hidden_state, preferred_element_type=jnp.float32)
+    summed = staged_reduce_scatter(partial)
     weight_grad = (summed * averaging)[None]
     return (query_grad, key_grad, value_grad, pre_grad, weight_grad)
 
 
 def solution(mesh):
     placed = (
-        P("dp", "ctx", "exp"),
-        P("dp", "ctx", "exp"),
-        P("dp", "ctx", "exp"),
-        P("dp", "ctx", "exp"),
-        P("dp", "exp", "ctx"),
-        P("dp", "exp", "ctx"),
-        P("dp", ("ctx", "exp"), None),
-        P("dp", ("ctx", "exp"), None),
-        P("dp", ("ctx", "exp"), None),
-        P("exp", "ctx", "dp", None, None),
+        P("dp", CTX, "exp"),
+        P("dp", CTX, "exp"),
+        P("dp", CTX, "exp"),
+        P("dp", CTX, "exp"),
+        P("dp", "exp", CTX),
+        P("dp", "exp", CTX),
+        P("dp", CTX + ("exp",), None),
+        P("dp", CTX + ("exp",), None),
+        P("dp", CTX + ("exp",), None),
+        P("exp", CTX, "dp", None, None),
         P("exp", None, None),
+    )
+    ctx_size, exp_size, dp_size = mesh.devices.shape
+    split = Mesh(
+        mesh.devices.reshape(ctx_size // 8, 4, 2, exp_size, dp_size), ("zl", "xx", "core", "exp", "dp")
     )
     return jax.shard_map(
         body,
-        mesh=mesh,
+        mesh=split,
         in_specs=placed,
         out_specs=(
-            P("dp", "ctx", "exp"),
-            P("dp", "ctx", "exp"),
-            P("dp", "ctx", "exp"),
-            P("exp", "ctx", "dp", None, None),
-            P("exp", ("ctx", "dp"), None),
+            P("dp", CTX, "exp"),
+            P("dp", CTX, "exp"),
+            P("dp", CTX, "exp"),
+            P("exp", CTX, "dp", None, None),
+            P("exp", ROW_AXES, None),
         ),
         check_vma=False,
     )

time: 828 us -> 159 us (0.19)
  the two profiles are of different devices: /device:TPU:64 before, /device:TPU:4 now
where the time goes in v1:
time: 159 us; the launch traced here: 157 us
  waiting for transfers between devices  49.1 us (31%)
  starting transfers between devices  42.3 us (27%)
  local copies, waits for them, and re-layouts  24.6 us (15%)
  matrix products  18.6 us (12%)
  other arithmetic  14.5 us (9%)
  blocking collectives  7.22 us (5%)
    all_to_all x3, starting transfers between devices, staged_reduce_scatter(): pieces = lax.all_to_all(pieces, name, 0, 0, tiled=True).sum(0)  28.1 us
    all_to_all x1, waiting for transfers between devices, body(): lax.all_to_all(outbound, 'exp', split_axis=0, concat_axis=0, tiled=True)  24.4 us
    all_to_all x3, waiting for transfers between devices, staged_reduce_scatter(): pieces = lax.all_to_all(pieces, name, 0, 0, tiled=True).sum(0)  14.2 us
    ppermute x2, waiting for transfers between devices, passed_along(): return lax.ppermute(value, axis, pairs)  10.5 us
    unnamed x35, local copies, waits for them, and re-layouts  9.9 us
    reduce_sum x4, other arithmetic, staged_reduce_scatter(): pieces = lax.all_to_all(pieces, name, 0, 0, tiled=True).sum(0)  7.41 us
    all_to_all x1, starting transfers between devices, body(): lax.all_to_all(outbound, 'exp', split_axis=0, concat_axis=0, tiled=True)  7.23 us
    all_to_all x1, blocking collectives, staged_reduce_scatter(): pieces = lax.all_to_all(pieces, name, 0, 0, tiled=True).sum(0)  7.22 us
  transfers between devices with their start and end apart: 7, of which 4 were waited for; matrix products, arithmetic and copies ran while one was open for 22% of the time, Pallas kernels for 0%

profile of v1, /device:TPU:4, one launch (start us, length us, event | category | flops | bytes accessed | tf_op | source)
XLA Modules:
  0.0 157.3 jit_solution(16703870841150451167)
XLA Ops:
  0.6 0.9 copy.69
  2.0 1.1 bitcast_convert_fusion
  3.1 2.0 %mul.179 = f32[32,2,6144]{2,1,0:T(2,128)} broadcast(f32[32,6144]{1,0:T(8,128)S(1)} %bitcast_convert_fusion), dimensions={0,2} | broadcast | bytes 2359296 | tf_op jit(solution)/shard_map/mul | solution.py:123
  5.1 2.4 %mul.180 = f32[64,6144]{1,0:T(8,128)S(1)} reshape(f32[32,2,6144]{2,1,0:T(2,128)} %mul.179) | data formatting | bytes 3145728 | tf_op jit(solution)/shard_map/mul | solution.py:123
  7.7 1.8 %convolution_convert_fusion = bf16[128,6144]{1,0:T(8,128)(2,1)} fusion(f32[64,6144]{1,0:T(8,128)S(1)} %mul.180, f32[64]{0:T(128)S(1)} %mul.177, s32[64]{0:T(128)S(1)} %multiply_add_fusion), kind=kOutput, calls=%fused_computation | convolution fusion | flops 102244352 | bytes 3146240 | tf_op jit(solution)/shard_map/dot_general | solution.py:137
  9.5 7.2 %all-to-all-start = ((bf16[8,16,6144]{2,1,0:T(8,128)(2,1)}), bf16[8,16,6144]{2,1,0:T(8,128)(2,1)S(1)}, u32[]{:S(2)}, u32[]{:S(2)}) async-start(bf16[8,16,6144]{2,1,0:T(8,128)(2,1)} %bitcast.90), calls=%async_computation | async-start | bytes 3145728 | tf_op jit(solution)/shard_map/all_to_all | solution.py:138
  16.8 0.7 pad_maximum_fusion
  17.4 1.9 %collective-permute-start = (bf16[2,256,128]{2,1,0:T(8,128)(2,1)}, bf16[2,256,128]{2,1,0:T(8,128)(2,1)}, u32[]{:S(2)}, u32[]{:S(2)}) collective-permute-start(bf16[2,256,128]{2,1,0:T(8,128)(2,1)} %pad_maximum_fusion), channel_id=1, source_target_pairs={{0,32},{32,64},{64,96},{96,128},{128,160},{160,192},{192,224},{224... | collective-permute-start | bytes 393224 | tf_op jit(solution)/shard_map/ppermute | solution.py:16
  19.4 1.2 copy.64
  20.5 0.9 copy.65
  21.5 1.9 %copy.66 = bf16[1,256,768]{1,2,0:T(8,128)(2,1)} copy(bf16[1,256,768]{2,1,0:T(8,128)(2,1)} %param.14) | data formatting | bytes 786432 | tf_op args[3]
  23.4 1.2 copy.67
  24.6 1.3 reduce.1
  25.9 0.7 sub.49
  26.6 1.6 copy.71
  28.2 1.5 bitcast_convert_fusion.1
  29.7 2.6 %fusion.4 = f32[256,1536]{1,0:T(8,128)} fusion(bf16[1536,128]{1,0:T(8,128)(2,1)} %bitcast.86, f32[1536]{0:T(1024)S(1)} %sub.46, bf16[2,256,128]{2,1,0:T(8,128)(2,1)} %collective-permute-done), kind=kOutput, calls=%fused_computation.9 | convolution fusion | flops 101449728 | bytes 2037760 | tf_op jit(solution)/shard_map/kqd,kud->kqu/dot_general | solution.py:32
  32.3 24.4 %all-to-all-done = bf16[8,16,6144]{2,1,0:T(8,128)(2,1)S(1)} async-done(((bf16[8,16,6144]{2,1,0:T(8,128)(2,1)}), bf16[8,16,6144]{2,1,0:T(8,128)(2,1)S(1)}, u32[]{:S(2)}, u32[]{:S(2)}) %all-to-all-start) | async-done | bytes 1572896 | tf_op jit(solution)/shard_map/all_to_all | solution.py:138
  56.7 1.6 %copy.72 = bf16[128,6144]{0,1:T(8,128)(2,1)} copy(bf16[128,6144]{1,0:T(8,128)(2,1)S(1)} %bitcast.79) | data formatting | bytes 3145728 | tf_op jit(solution)/shard_map/all_to_all | solution.py:138
  58.3 2.0 %convolution_bitcast_fusion = f32[2,4,4,4,48,128]{5,4,3,0,1,2:T(8,128)S(1)} fusion(bf16[4,4,2,4,48,128]{5,4,3,2,1,0:T(8,128)(2,1)} %bitcast.81, f32[128,256]{0,1:T(8,128)} %bitcast_convert_fusion.1), kind=kOutput, calls=%fused_computation.17 | convolution fusion | flops 201424896 | bytes 4849664 | tf_op jit(solution)/shard_map/rc,rf->cf/dot_general | solution.py:153
  60.7 7.2 %all_to_all.32 = f32[2,4,4,4,48,128]{5,4,3,1,2,0:T(8,128)} all-to-all(f32[2,4,4,4,48,128]{5,4,3,1,2,0:T(8,128)S(1)} %copy.74), channel_id=1, replica_groups=mesh['zl'=4,'xx'=4,'core'=2,'exp'=8,'dp'=4] {'core'}, dimensions={0} | all-to-all | bytes 6291456 | tf_op jit(solution)/shard_map/all_to_all | solution.py:61
  67.9 3.4 %reduce_sum.46 = f32[4,4,4,48,128]{4,3,2,0,1:T(8,128)} reduce(f32[2,4,4,4,48,128]{5,4,3,1,2,0:T(8,128)} %all_to_all.32, f32[]{:T(128)} %constant.37.clone.1), dimensions={0}, to_apply=%region_2.3 | reduce | flops 393216 | bytes 4718596 | tf_op jit(solution)/shard_map/reduce_sum | solution.py:61
  71.3 2.8 %copy.76 = f32[4,4,4,48,128]{4,3,2,1,0:T(8,128)} copy(f32[4,4,4,48,128]{4,3,2,0,1:T(8,128)} %reduce_sum.46) | data formatting | bytes 3145728 | tf_op jit(solution)/shard_map/reduce_sum | solution.py:61
  74.1 4.9 %all-to-all-start.2 = ((f32[4,4,4,48,128]{4,3,2,1,0:T(8,128)}), f32[4,4,4,48,128]{4,3,2,1,0:T(8,128)}, u32[]{:S(2)}, u32[]{:S(2)}) async-start(f32[4,4,4,48,128]{4,3,2,1,0:T(8,128)} %copy.76), calls=%async_computation.2 | async-start | bytes 3145728 | tf_op jit(solution)/shard_map/all_to_all | solution.py:61
  79.0 1.9 %fusion.6 = bf16[256,1536]{1,0:T(8,128)(2,1)S(1)} fusion(f32[256,1536]{1,0:T(8,128)} %fusion.4, bf16[1536,128]{1,0:T(8,128)(2,1)S(1)} %bitcast.82, f32[1536]{0:T(1024)S(1)} %sub.49, bf16[2,256,128]{2,1,0:T(8,128)(2,1)} %collective-permute-done), kind=kOutput, calls=%fused_computation.11 | convolution fusion | flops 101842944 | bytes 2824192 | tf_op jit(solution)/shard_map/kqd,kud->kqu/dot_general | solution.py:37
  81.7 0.7 fusion.17
  82.3 1.9 %collective-permute-start.2 = (bf16[2,1,256,128]{3,2,1,0:T(8,128)(2,1)}, bf16[2,1,256,128]{3,2,1,0:T(8,128)(2,1)}, u32[]{:S(2)}, u32[]{:S(2)}) collective-permute-start(bf16[2,1,256,128]{3,2,1,0:T(8,128)(2,1)} %fusion.17), channel_id=1, source_target_pairs={{992,0},{0,32},{32,64},{64,96},{96,128},{128,160},{160,192},{192,2... | collective-permute-start | bytes 393224 | tf_op jit(solution)/shard_map/ppermute | solution.py:22
  84.2 3.2 %collective-permute-start.1 = (bf16[2,256,128]{2,1,0:T(8,128)(2,1)}, bf16[2,256,128]{2,1,0:T(8,128)(2,1)S(1)}, u32[]{:S(2)}, u32[]{:S(2)}) collective-permute-start(bf16[2,256,128]{2,1,0:T(8,128)(2,1)} %collective-permute-done), channel_id=1, source_target_pairs={{0,32},{32,64},{64,96},{96,128},{128,160},{160,192},{192,224},{224... | collective-permute-start | bytes 393224 | tf_op jit(solution)/shard_map/ppermute | solution.py:16
  87.4 2.2 %convolution_multiply_fusion.3 = f32[1536,128]{1,0:T(8,128)} fusion(bf16[256,1536]{1,0:T(8,128)(2,1)S(1)} %fusion.6, f32[]{:T(128)S(6)} %mul.159, bf16[2,256,128]{2,1,0:T(8,128)(2,1)} %collective-permute-done), kind=kOutput, calls=%fused_computation.14 | convolution fusion | flops 100859904 | bytes 1638404 | tf_op jit(solution)/shard_map/kqu,kud->kqd/dot_general | solution.py:42
  89.6 10.5 %collective-permute-done.1 = bf16[2,256,128]{2,1,0:T(8,128)(2,1)S(1)} collective-permute-done((bf16[2,256,128]{2,1,0:T(8,128)(2,1)}, bf16[2,256,128]{2,1,0:T(8,128)(2,1)S(1)}, u32[]{:S(2)}, u32[]{:S(2)}) %collective-permute-start.1) | collective-permute-done | bytes 131104 | tf_op jit(solution)/shard_map/ppermute | solution.py:16
  100.1 0.7 copy-done.8
  100.8 1.5 fusion.5
  102.3 2.3 %reduce_sum.47 = f32[4,4,48,128]{3,2,1,0:T(8,128)} reduce(f32[4,4,4,48,128]{4,3,2,1,0:T(8,128)} %all-to-all-done.2, f32[]{:T(128)} %constant.37.clone.1), dimensions={0}, to_apply=%region_3.4 | reduce | flops 294912 | bytes 1966084 | tf_op jit(solution)/shard_map/reduce_sum | solution.py:61
  104.6 7.2 %all-to-all-start.3 = ((f32[4,4,48,128]{3,2,1,0:T(8,128)}), f32[4,4,48,128]{3,2,1,0:T(8,128)}, u32[]{:S(2)}, u32[]{:S(2)}) async-start(f32[4,4,48,128]{3,2,1,0:T(8,128)} %reduce_sum.47), calls=%async_computation.3 | async-start | bytes 786432 | tf_op jit(solution)/shard_map/all_to_all | solution.py:61
  111.8 1.9 %fusion.7 = bf16[256,1536]{1,0:T(8,128)(2,1)S(1)} fusion(f32[256,1536]{1,0:T(8,128)} %fusion.5, bf16[1536,128]{1,0:T(8,128)(2,1)S(1)} %bitcast.84, f32[1536]{0:T(1024)S(1)} %sub.49, bf16[2,256,128]{2,1,0:T(8,128)(2,1)} %copy-done.8), kind=kOutput, calls=%fused_computation.12 | convolution fusion | flops 101842944 | bytes 2824192 | tf_op jit(solution)/shard_map/kqd,kud->kqu/dot_general | solution.py:37
  113.7 0.9 copy-done.4
  114.6 1.2 fusion.9
  115.8 1.9 %copy.68 = bf16[1,6,256,128]{2,3,1,0:T(8,128)(2,1)} copy(bf16[1,6,256,128]{3,2,1,0:T(8,128)(2,1)} %bitcast.91) | data formatting | bytes 786432 | tf_op jit(solution)/shard_map/convert_element_type | solution.py:111
  117.7 1.9 %copy.77 = bf16[1,256,768]{2,1,0:T(8,128)(2,1)} copy(bf16[1,256,768]{1,2,0:T(8,128)(2,1)} %bitcast.92) | data formatting | bytes 786432
  119.6 1.9 %convolution_bitcast_fusion.1 = f32[1,1,256,128]{3,2,1,0:T(8,128)S(1)} fusion(bf16[1536,128]{1,0:T(8,128)(2,1)S(1)} %bitcast.85, f32[256,1536]{1,0:T(8,128)} %fusion.5), kind=kOutput, calls=%fused_computation.21 | convolution fusion | flops 101056512 | bytes 2097152 | tf_op jit(solution)/shard_map/kqu,kqd->kud/dot_general | solution.py:49
  121.9 0.9 fusion.19
  122.8 0.7 slice_bitcast_fusion
  123.8 1.7 %reduce_sum.48 = f32[4,48,128]{2,1,0:T(8,128)} reduce(f32[4,4,48,128]{3,2,1,0:T(8,128)} %all-to-all-done.3, f32[]{:T(128)} %constant.37.clone.1), dimensions={0}, to_apply=%region_4.5 | reduce | flops 73728 | bytes 491524 | tf_op jit(solution)/shard_map/reduce_sum | solution.py:61
  125.5 16.0 %all-to-all-start.4 = ((f32[4,48,128]{2,1,0:T(8,128)}), f32[4,48,128]{2,1,0:T(8,128)S(1)}, u32[]{:S(2)}, u32[]{:S(2)}) async-start(f32[4,48,128]{2,1,0:T(8,128)} %reduce_sum.48), calls=%async_computation.4 | async-start | bytes 196608 | tf_op jit(solution)/shard_map/all_to_all | solution.py:61
  141.5 0.6 fusion.26
  142.1 0.7 copy.78
  142.8 13.9 %all-to-all-done.4 = f32[4,48,128]{2,1,0:T(8,128)S(1)} async-done(((f32[4,48,128]{2,1,0:T(8,128)}), f32[4,48,128]{2,1,0:T(8,128)S(1)}, u32[]{:S(2)}, u32[]{:S(2)}) %all-to-all-start.4) | async-done | bytes 98336 | tf_op jit(solution)/shard_map/all_to_all | solution.py:61
  156.7 0.6 multiply_bitcast_fusion
  (45 shorter events, 2.5 us)
Async XLA Ops:
  0.6 140.9 %copy-start = (bf16[1,128,6144]{2,1,0:T(8,128)(2,1)S(1)}, bf16[1,128,6144]{2,1,0:T(8,128)(2,1)}, u32[]{:S(2)}) copy-start(bf16[1,128,6144]{2,1,0:T(8,128)(2,1)} %param.21) | copy-start | bytes 4718596
  5.1 2.4 %copy-start.13 = (f32[1,32,2]{1,2,0:T(2,128)S(1)}, f32[1,32,2]{1,2,0:T(2,128)}, u32[]{:S(2)}) copy-start(f32[1,32,2]{1,2,0:T(2,128)} %param.18) | copy-start | bytes 772
  9.5 7.2 %copy-start.10 = (bf16[1,256,128]{2,1,0:T(8,128)(2,1)S(1)}, bf16[1,256,128]{2,1,0:T(8,128)(2,1)}, u32[]{:S(2)}) copy-start(bf16[1,256,128]{2,1,0:T(8,128)(2,1)} %param.13) | copy-start | bytes 196612
  9.5 7.2 %copy-start.11 = (bf16[1,256,128]{2,1,0:T(8,128)(2,1)S(1)}, bf16[1,256,128]{2,1,0:T(8,128)(2,1)}, u32[]{:S(2)}) copy-start(bf16[1,256,128]{2,1,0:T(8,128)(2,1)} %param.12) | copy-start | bytes 196612
  9.5 47.2 %all-to-all-start = ((bf16[8,16,6144]{2,1,0:T(8,128)(2,1)}), bf16[8,16,6144]{2,1,0:T(8,128)(2,1)S(1)}, u32[]{:S(2)}, u32[]{:S(2)}) async-start(bf16[8,16,6144]{2,1,0:T(8,128)(2,1)} %bitcast.90), calls=%async_computation | async-start | bytes 3145728 | tf_op jit(solution)/shard_map/all_to_all | solution.py:138
  16.8 4.7 %copy-start.12 = (f32[1,6,256]{2,0,1:T(1,128)S(1)}, f32[1,6,256]{2,0,1:T(1,128)}, u32[]{:S(2)}) copy-start(f32[1,6,256]{2,0,1:T(1,128)} %param.15) | copy-start | bytes 18436
  17.4 12.3 %collective-permute-start = (bf16[2,256,128]{2,1,0:T(8,128)(2,1)}, bf16[2,256,128]{2,1,0:T(8,128)(2,1)}, u32[]{:S(2)}, u32[]{:S(2)}) collective-permute-start(bf16[2,256,128]{2,1,0:T(8,128)(2,1)} %pad_maximum_fusion), channel_id=1, source_target_pairs={{0,32},{32,64},{64,96},{96,128},{128,160},{160,192},{192,224},{224... | collective-permute-start | bytes 393224 | tf_op jit(solution)/shard_map/ppermute | solution.py:16
  74.1 28.2 %all-to-all-start.2 = ((f32[4,4,4,48,128]{4,3,2,1,0:T(8,128)}), f32[4,4,4,48,128]{4,3,2,1,0:T(8,128)}, u32[]{:S(2)}, u32[]{:S(2)}) async-start(f32[4,4,4,48,128]{4,3,2,1,0:T(8,128)} %copy.76), calls=%async_computation.2 | async-start | bytes 3145728 | tf_op jit(solution)/shard_map/all_to_all | solution.py:61
  79.0 2.0 %copy-start.2 = (bf16[1,6,256,128]{3,2,1,0:T(8,128)(2,1)S(1)}, bf16[1,6,256,128]{3,2,1,0:T(8,128)(2,1)}, u32[]{:S(2)}) copy-start(bf16[1,6,256,128]{3,2,1,0:T(8,128)(2,1)} %copy.65) | copy-start | bytes 1179652
  79.0 2.3 %copy-start.1 = (f32[256,1536]{1,0:T(8,128)S(1)}, f32[256,1536]{1,0:T(8,128)}, u32[]{:S(2)}) copy-start(f32[256,1536]{1,0:T(8,128)} %fusion.4) | copy-start | bytes 4718596
  82.3 39.5 %collective-permute-start.2 = (bf16[2,1,256,128]{3,2,1,0:T(8,128)(2,1)}, bf16[2,1,256,128]{3,2,1,0:T(8,128)(2,1)}, u32[]{:S(2)}, u32[]{:S(2)}) collective-permute-start(bf16[2,1,256,128]{3,2,1,0:T(8,128)(2,1)} %fusion.17), channel_id=1, source_target_pairs={{992,0},{0,32},{32,64},{64,96},{96,128},{128,160},{160,192},{192,2... | collective-permute-start | bytes 393224 | tf_op jit(solution)/shard_map/ppermute | solution.py:22
  84.2 15.9 %collective-permute-start.1 = (bf16[2,256,128]{2,1,0:T(8,128)(2,1)}, bf16[2,256,128]{2,1,0:T(8,128)(2,1)S(1)}, u32[]{:S(2)}, u32[]{:S(2)}) collective-permute-start(bf16[2,256,128]{2,1,0:T(8,128)(2,1)} %collective-permute-done), channel_id=1, source_target_pairs={{0,32},{32,64},{64,96},{96,128},{128,160},{160,192},{192,224},{224... | collective-permute-start | bytes 393224 | tf_op jit(solution)/shard_map/ppermute | solution.py:16
  100.1 0.7 copy-start.8
  104.6 19.2 %all-to-all-start.3 = ((f32[4,4,48,128]{3,2,1,0:T(8,128)}), f32[4,4,48,128]{3,2,1,0:T(8,128)}, u32[]{:S(2)}, u32[]{:S(2)}) async-start(f32[4,4,48,128]{3,2,1,0:T(8,128)} %reduce_sum.47), calls=%async_computation.3 | async-start | bytes 786432 | tf_op jit(solution)/shard_map/all_to_all | solution.py:61
  111.8 2.8 %copy-start.6 = (f32[1536,128]{1,0:T(8,128)S(1)}, f32[1536,128]{1,0:T(8,128)}, u32[]{:S(2)}) copy-start(f32[1536,128]{1,0:T(8,128)} %convolution_multiply_fusion.3) | copy-start | bytes 2359300
  111.8 2.8 %copy-start.9 = (bf16[2,256,128]{2,1,0:T(8,128)(2,1)S(1)}, bf16[2,256,128]{2,1,0:T(8,128)(2,1)}, u32[]{:S(2)}) copy-start(bf16[2,256,128]{2,1,0:T(8,128)(2,1)} %copy-done.8) | copy-start | bytes 393220
  113.7 0.9 copy-start.4
  119.6 1.9 %copy-start.3 = (bf16[1,6,256,128]{3,2,1,0:T(8,128)(2,1)S(1)}, bf16[1,6,256,128]{3,2,1,0:T(8,128)(2,1)}, u32[]{:S(2)}) copy-start(bf16[1,6,256,128]{3,2,1,0:T(8,128)(2,1)} %copy.65) | copy-start | bytes 1179652
  119.6 1.9 %copy-start.5 = (bf16[256,1536]{1,0:T(8,128)(2,1)S(1)}, bf16[256,1536]{1,0:T(8,128)(2,1)}, u32[]{:S(2)}) copy-start(bf16[256,1536]{1,0:T(8,128)(2,1)} %copy-done.4) | copy-start | bytes 2359300
  121.5 20.0 %copy-start.7 = (f32[128,256]{0,1:T(8,128)S(1)}, f32[128,256]{0,1:T(8,128)}, u32[]{:S(2)}) copy-start(f32[128,256]{0,1:T(8,128)} %bitcast_convert_fusion.1) | copy-start | bytes 393220
  125.5 31.2 %all-to-all-start.4 = ((f32[4,48,128]{2,1,0:T(8,128)}), f32[4,48,128]{2,1,0:T(8,128)S(1)}, u32[]{:S(2)}, u32[]{:S(2)}) async-start(f32[4,48,128]{2,1,0:T(8,128)} %reduce_sum.48), calls=%async_computation.4 | async-start | bytes 196608 | tf_op jit(solution)/shard_map/all_to_all | solution.py:61

commit v2 on v1

--- a/solution.py
+++ b/solution.py
@@ -52,14 +52,24 @@
     return (query_out, key_out, value_out)
 
 
-def staged_reduce_scatter(partial):
-    rows, width = partial.shape
-    sizes = [lax.axis_size(name) for name in ROW_AXES]
-    block = rows // (sizes[0] * sizes[1] * sizes[2] * sizes[3])
-    pieces = partial.reshape(*sizes, block, width).transpose(2, 1, 0, 3, 4, 5)
-    for name in ("core", "xx", "zl", "dp"):
-        pieces = lax.all_to_all(pieces, name, 0, 0, tiled=True).sum(0)
-    return pieces.reshape(block, width)
+def weight_partial_sums(incoming_block, hidden_state):
+    slots, width = incoming_block.shape
+    zl, xx, core, dp = (lax.axis_size(name) for name in ROW_AXES)
+    block = width // (zl * xx * core * dp)
+    columns = incoming_block.reshape(slots, zl, xx, core, dp, block)
+    here = lax.axis_index("core")
+    swap = [(i, (i + 1) % core) for i in range(core)]
+    mine = lax.dynamic_index_in_dim(columns, here, 3, keepdims=False)
+    other = lax.dynamic_index_in_dim(columns, 1 - here, 3, keepdims=False)
+    rows_in = jnp.concatenate([mine, lax.ppermute(other, "core", swap)], axis=0)
+    hidden_in = jnp.concatenate([hidden_state, lax.ppermute(hidden_state, "core", swap)], axis=0)
+    pieces = jnp.einsum(
+        "rzxdq,rf->xzdqf", rows_in, hidden_in, preferred_element_type=jnp.float32
+    )
+    pieces = lax.all_to_all(pieces, "xx", 0, 0, tiled=True).sum(0)
+    pieces = pieces.reshape(zl * dp, block, hidden_state.shape[1])
+    pieces = lax.all_to_all(pieces, ("zl", "dp"), 0, 0, tiled=True).sum(0)
+    return pieces
 
 
 def body(
@@ -150,8 +160,7 @@
     up_grad = hidden_gradient * active
     pre_grad = jnp.concatenate([gate_grad, up_grad], axis=-1).astype(jnp.bfloat16)[None, None, None]
     averaging = 1.0 / lax.axis_size(ROW_AXES)
-    partial = jnp.einsum("rc,rf->cf", incoming_block, hidden_state, preferred_element_type=jnp.float32)
-    summed = staged_reduce_scatter(partial)
+    summed = weight_partial_sums(incoming_block, hidden_state)
     weight_grad = (summed * averaging)[None]
     return (query_grad, key_grad, value_grad, pre_grad, weight_grad)
 

time: 159 us -> 167 us (1.050)
  the two profiles are of different devices: /device:TPU:4 before, /device:TPU:64 now
where the time goes in v2:
time: 167 us; the launch traced here: 165 us
  waiting for transfers between devices  53.8 us (32%)
  starting transfers between devices  42.2 us (25%)
  local copies, waits for them, and re-layouts  41.6 us (25%)
  matrix products  14.7 us (9%)
  other arithmetic  11.9 us (7%)
    all_to_all x1, waiting for transfers between devices, body(): lax.all_to_all(outbound, 'exp', split_axis=0, concat_axis=0, tiled=True)  28.5 us
    all_to_all x1, starting transfers between devices, weight_partial_sums(): pieces = lax.all_to_all(pieces, ('zl', 'dp'), 0, 0, tiled=True).sum(0)  18.4 us
    all_to_all x1, waiting for transfers between devices, weight_partial_sums(): pieces = lax.all_to_all(pieces, ('zl', 'dp'), 0, 0, tiled=True).sum(0)  13.3 us
    dynamic_slice x2, local copies, waits for them, and re-layouts, weight_partial_sums(): mine = lax.dynamic_index_in_dim(columns, here, 3, keepdims=False)  10.6 us
    unnamed x41, local copies, waits for them, and re-layouts  10 us
    all_to_all x1, waiting for transfers between devices, weight_partial_sums(): pieces = lax.all_to_all(pieces, 'xx', 0, 0, tiled=True).sum(0)  8.69 us
    all_to_all x1, starting transfers between devices, body(): lax.all_to_all(outbound, 'exp', split_axis=0, concat_axis=0, tiled=True)  7.23 us
    ppermute x2, starting transfers between devices, passed_along(): return lax.ppermute(value, axis, pairs)  5.88 us
  transfers between devices with their start and end apart: 8, of which 4 were waited for; matrix products, arithmetic and copies ran while one was open for 33% of the time, Pallas kernels for 0%

profile of v2, /device:TPU:64, one launch (start us, length us, event | category | flops | bytes accessed | tf_op | source)
XLA Modules:
  0.0 165.2 jit_solution(6471180832356479995)
XLA Ops:
  0.6 1.2 bitcast_convert_fusion
  1.8 2.0 %mul.179 = f32[32,2,6144]{2,1,0:T(2,128)} broadcast(f32[32,6144]{1,0:T(8,128)S(1)} %bitcast_convert_fusion), dimensions={0,2} | broadcast | bytes 2359296 | tf_op jit(solution)/shard_map/mul | solution.py:133
  3.8 2.4 %mul.180 = f32[64,6144]{1,0:T(8,128)S(1)} reshape(f32[32,2,6144]{2,1,0:T(2,128)} %mul.179) | data formatting | bytes 3145728 | tf_op jit(solution)/shard_map/mul | solution.py:133
  7.1 1.8 %convolution_convert_fusion = bf16[128,6144]{1,0:T(8,128)(2,1)} fusion(f32[64,6144]{1,0:T(8,128)S(1)} %mul.180, f32[64]{0:T(128)S(1)} %mul.177, s32[64]{0:T(128)S(1)} %multiply_add_fusion), kind=kOutput, calls=%fused_computation | convolution fusion | flops 102244352 | bytes 3146240 | tf_op jit(solution)/shard_map/dot_general | solution.py:147
  8.9 7.2 %all-to-all-start = ((bf16[8,16,6144]{2,1,0:T(8,128)(2,1)}), bf16[8,16,6144]{2,1,0:T(8,128)(2,1)S(1)}, u32[]{:S(2)}, u32[]{:S(2)}) async-start(bf16[8,16,6144]{2,1,0:T(8,128)(2,1)} %bitcast.87), calls=%async_computation | async-start | bytes 3145728 | tf_op jit(solution)/shard_map/all_to_all | solution.py:148
  16.1 0.7 pad_maximum_fusion.1
  16.8 1.9 %collective-permute-start = (bf16[2,256,128]{2,1,0:T(8,128)(2,1)}, bf16[2,256,128]{2,1,0:T(8,128)(2,1)}, u32[]{:S(2)}, u32[]{:S(2)}) collective-permute-start(bf16[2,256,128]{2,1,0:T(8,128)(2,1)} %pad_maximum_fusion.1), channel_id=1, source_target_pairs={{0,32},{32,64},{64,96},{96,128},{128,160},{160,192},{192,224},{224... | collective-permute-start | bytes 393224 | tf_op jit(solution)/shard_map/ppermute | solution.py:16
  18.7 1.2 copy.51
  19.9 0.9 copy.52
  20.9 1.9 %copy.53 = bf16[1,256,768]{1,2,0:T(8,128)(2,1)} copy(bf16[1,256,768]{2,1,0:T(8,128)(2,1)} %param.14) | data formatting | bytes 786432 | tf_op args[3]
  22.8 1.2 copy.54
  24.0 1.3 reduce.1
  25.3 0.7 sub.52
  26.0 1.6 copy.58
  27.6 28.5 %all-to-all-done = bf16[8,16,6144]{2,1,0:T(8,128)(2,1)S(1)} async-done(((bf16[8,16,6144]{2,1,0:T(8,128)(2,1)}), bf16[8,16,6144]{2,1,0:T(8,128)(2,1)S(1)}, u32[]{:S(2)}, u32[]{:S(2)}) %all-to-all-start) | async-done | bytes 1572896 | tf_op jit(solution)/shard_map/all_to_all | solution.py:148
  56.1 5.3 %reshape.268 = bf16[128,4,4,2,4,48]{5,4,3,2,1,0:T(4,128)(2,1)} reshape(bf16[8,16,6144]{2,1,0:T(8,128)(2,1)S(1)} %all-to-all-done) | data formatting | bytes 3145728 | tf_op jit(solution)/shard_map/reshape | solution.py:59
  61.4 6.3 %constant_dynamic-slice_fusion = (bf16[128,4,4,1,4,48]{5,4,3,2,1,0:T(4,128)(2,1)}, bf16[128,4,4,1,4,48]{5,4,3,2,1,0:T(4,128)(2,1)}) fusion(bf16[128,4,4,2,4,48]{5,4,3,2,1,0:T(4,128)(2,1)} %reshape.268, s32[]{:T(128)S(6)} %select_n.7, s32[]{:T(128)S(6)} %select_n.8), kind=kLoop, calls=%fused_computation.62 | loop fusion | bytes 3145736 | tf_op jit(solution)/shard_map/jit(dynamic_index_in_dim)/dynamic_slice | solution.py:62
  67.7 4.3 %copy.60 = bf16[128,4,4,1,4,48]{0,5,4,2,1,3:T(8,128)(2,1)} copy(bf16[128,4,4,1,4,48]{5,4,3,2,1,0:T(4,128)(2,1)} %get-tuple-element.26) | data formatting | bytes 1572864 | tf_op jit(solution)/shard_map/jit(dynamic_index_in_dim)/dynamic_slice | solution.py:63
  72.0 1.9 %collective-permute-start.4 = (bf16[128,4,4,4,48]{0,4,3,2,1:T(8,128)(2,1)}, bf16[128,4,4,4,48]{0,4,3,2,1:T(8,128)(2,1)}, u32[]{:S(2)}, u32[]{:S(2)}) collective-permute-start(bf16[128,4,4,4,48]{0,4,3,2,1:T(8,128)(2,1)} %bitcast.96), channel_id=1, source_target_pairs={{0,32},{32,0},{1,33},{33,1},{2,34},{34,2},{3,35},{35,3},{4,36},{36... | collective-permute-start | bytes 2359304 | tf_op jit(solution)/shard_map/ppermute | solution.py:64
  73.9 1.5 bitcast_convert_fusion.1
  75.4 2.6 %fusion.4 = f32[256,1536]{1,0:T(8,128)} fusion(bf16[1536,128]{1,0:T(8,128)(2,1)} %bitcast.83, f32[1536]{0:T(1024)S(1)} %sub.49, bf16[2,256,128]{2,1,0:T(8,128)(2,1)} %collective-permute-done), kind=kOutput, calls=%fused_computation.9 | convolution fusion | flops 101449728 | bytes 2037760 | tf_op jit(solution)/shard_map/kqd,kud->kqu/dot_general | solution.py:32
  78.0 4.3 %copy.59 = bf16[128,4,4,1,4,48]{0,5,4,2,1,3:T(8,128)(2,1)} copy(bf16[128,4,4,1,4,48]{5,4,3,2,1,0:T(4,128)(2,1)} %get-tuple-element.25) | data formatting | bytes 1572864 | tf_op jit(solution)/shard_map/jit(dynamic_index_in_dim)/dynamic_slice | solution.py:62
  82.3 2.1 %fusion.28 = (bf16[1,1,1,128,128]{3,4,2,1,0:T(8,128)(2,1)}, bf16[1,1,1,128,128]{3,4,2,1,0:T(8,128)(2,1)}, bf16[128,128]{0,1:T(8,128)(2,1)S(1)}) fusion(f32[128,256]{0,1:T(8,128)} %bitcast_convert_fusion.1, bf16[128,6144]{1,0:T(8,128)(2,1)S(1)} %bitcast.78, bf16[1,128,6144]{2,1,0:T(8,128)(2,1)S(1)} %copy-done), kind=kOutput, calls=%fused_computation.60 | convolution fusion | flops 201572352 | bytes 3375104 | tf_op jit(solution)/shard_map/rd,fd->rf/dot_general | solution.py:156
  84.4 2.4 %collective-permute-start.3 = (bf16[128,128]{0,1:T(8,128)(2,1)S(1)}, bf16[128,128]{0,1:T(8,128)(2,1)S(1)}, u32[]{:S(2)}, u32[]{:S(2)}) collective-permute-start(bf16[128,128]{0,1:T(8,128)(2,1)S(1)} %get-tuple-element.29), channel_id=1, source_target_pairs={{0,32},{32,0},{1,33},{33,1},{2,34},{34,2},{3,35},{35,3},{4,36},{36... | collective-permute-start | bytes 98312 | tf_op jit(solution)/shard_map/ppermute | solution.py:65
  86.9 1.3 pad_maximum_fusion
  88.8 1.3 copy.62
  90.1 4.5 %all-to-all-start.1 = ((f32[4,4,4,48,128]{4,3,2,1,0:T(8,128)}), f32[4,4,4,48,128]{4,3,2,1,0:T(8,128)}, u32[]{:S(2)}, u32[]{:S(2)}) async-start(f32[4,4,4,48,128]{4,3,2,1,0:T(8,128)} %copy.62), calls=%async_computation.1 | async-start | bytes 3145728 | tf_op jit(solution)/shard_map/all_to_all | solution.py:69
  94.6 1.3 fusion.6
  96.6 0.7 fusion.17
  97.3 1.9 %collective-permute-start.2 = (bf16[2,1,256,128]{3,2,1,0:T(8,128)(2,1)}, bf16[2,1,256,128]{3,2,1,0:T(8,128)(2,1)}, u32[]{:S(2)}, u32[]{:S(2)}) collective-permute-start(bf16[2,1,256,128]{3,2,1,0:T(8,128)(2,1)} %fusion.17), channel_id=1, source_target_pairs={{992,0},{0,32},{32,64},{64,96},{96,128},{128,160},{160,192},{192,2... | collective-permute-start | bytes 393224 | tf_op jit(solution)/shard_map/ppermute | solution.py:22
  99.2 4.0 %collective-permute-start.1 = (bf16[2,256,128]{2,1,0:T(8,128)(2,1)}, bf16[2,256,128]{2,1,0:T(8,128)(2,1)S(1)}, u32[]{:S(2)}, u32[]{:S(2)}) collective-permute-start(bf16[2,256,128]{2,1,0:T(8,128)(2,1)} %collective-permute-done), channel_id=1, source_target_pairs={{0,32},{32,64},{64,96},{96,128},{128,160},{160,192},{192,224},{224... | collective-permute-start | bytes 393224 | tf_op jit(solution)/shard_map/ppermute | solution.py:16
  103.2 2.2 %convolution_multiply_fusion.3 = f32[1536,128]{1,0:T(8,128)} fusion(bf16[256,1536]{1,0:T(8,128)(2,1)S(1)} %fusion.6, f32[]{:T(128)S(6)} %mul.159, bf16[2,256,128]{2,1,0:T(8,128)(2,1)} %collective-permute-done), kind=kOutput, calls=%fused_computation.14 | convolution fusion | flops 100859904 | bytes 1638404 | tf_op jit(solution)/shard_map/kqu,kud->kqd/dot_general | solution.py:42
  105.3 3.3 %collective-permute-done.1 = bf16[2,256,128]{2,1,0:T(8,128)(2,1)S(1)} collective-permute-done((bf16[2,256,128]{2,1,0:T(8,128)(2,1)}, bf16[2,256,128]{2,1,0:T(8,128)(2,1)S(1)}, u32[]{:S(2)}, u32[]{:S(2)}) %collective-permute-start.1) | collective-permute-done | bytes 131104 | tf_op jit(solution)/shard_map/ppermute | solution.py:16
  108.6 0.7 copy-done.8
  109.6 8.7 %all-to-all-done.1 = f32[4,4,4,48,128]{4,3,2,1,0:T(8,128)} async-done(((f32[4,4,4,48,128]{4,3,2,1,0:T(8,128)}), f32[4,4,4,48,128]{4,3,2,1,0:T(8,128)}, u32[]{:S(2)}, u32[]{:S(2)}) %all-to-all-start.1) | async-done | bytes 1572896 | tf_op jit(solution)/shard_map/all_to_all | solution.py:69
  118.3 2.3 %reduce_sum.28 = f32[4,4,48,128]{3,2,1,0:T(8,128)} reduce(f32[4,4,4,48,128]{4,3,2,1,0:T(8,128)} %all-to-all-done.1, f32[]{:T(128)} %constant.44.clone.1), dimensions={0}, to_apply=%region_2.3 | reduce | flops 294912 | bytes 1966084 | tf_op jit(solution)/shard_map/reduce_sum | solution.py:69
  120.6 18.4 %all-to-all-start.2 = ((f32[16,48,128]{2,1,0:T(8,128)}), f32[16,48,128]{2,1,0:T(8,128)}, u32[]{:S(2)}, u32[]{:S(2)}) async-start(f32[16,48,128]{2,1,0:T(8,128)} %bitcast.95), calls=%async_computation.2 | async-start | bytes 786432 | tf_op jit(solution)/shard_map/all_to_all | solution.py:71
  139.1 1.3 fusion.7
  140.4 0.9 copy-done.4
  141.3 1.2 fusion.9
  142.4 1.9 %copy.55 = bf16[1,6,256,128]{2,3,1,0:T(8,128)(2,1)} copy(bf16[1,6,256,128]{3,2,1,0:T(8,128)(2,1)} %bitcast.91) | data formatting | bytes 786432 | tf_op jit(solution)/shard_map/convert_element_type | solution.py:121
  144.3 1.9 %copy.63 = bf16[1,256,768]{2,1,0:T(8,128)(2,1)} copy(bf16[1,256,768]{1,2,0:T(8,128)(2,1)} %bitcast.92) | data formatting | bytes 786432
  146.6 0.6 copy-done.3
  147.9 0.9 fusion.19
  148.8 0.7 slice_bitcast_fusion
  149.5 0.7 copy.64
  150.3 13.3 %all-to-all-done.2 = f32[16,48,128]{2,1,0:T(8,128)} async-done(((f32[16,48,128]{2,1,0:T(8,128)}), f32[16,48,128]{2,1,0:T(8,128)}, u32[]{:S(2)}, u32[]{:S(2)}) %all-to-all-start.2) | async-done | bytes 393248 | tf_op jit(solution)/shard_map/all_to_all | solution.py:71
  163.6 1.0 reduce_sum.29
  (53 shorter events, 4.1 us)
Async XLA Ops:
  0.6 81.7 %copy-start = (bf16[1,128,6144]{2,1,0:T(8,128)(2,1)S(1)}, bf16[1,128,6144]{2,1,0:T(8,128)(2,1)}, u32[]{:S(2)}) copy-start(bf16[1,128,6144]{2,1,0:T(8,128)(2,1)} %param.21) | copy-start | bytes 4718596
  3.8 2.4 %copy-start.15 = (f32[1,32,2]{1,2,0:T(2,128)S(1)}, f32[1,32,2]{1,2,0:T(2,128)}, u32[]{:S(2)}) copy-start(f32[1,32,2]{1,2,0:T(2,128)} %param.18) | copy-start | bytes 772
  3.8 2.6 %copy-start.16 = (s32[1,32,2]{1,2,0:T(2,128)S(1)}, s32[1,32,2]{1,2,0:T(2,128)}, u32[]{:S(2)}) copy-start(s32[1,32,2]{1,2,0:T(2,128)} %param.19) | copy-start | bytes 772
  8.8 7.2 %copy-start.12 = (bf16[1,256,128]{2,1,0:T(8,128)(2,1)S(1)}, bf16[1,256,128]{2,1,0:T(8,128)(2,1)}, u32[]{:S(2)}) copy-start(bf16[1,256,128]{2,1,0:T(8,128)(2,1)} %param.13) | copy-start | bytes 196612
  8.9 7.2 %copy-start.13 = (bf16[1,256,128]{2,1,0:T(8,128)(2,1)S(1)}, bf16[1,256,128]{2,1,0:T(8,128)(2,1)}, u32[]{:S(2)}) copy-start(bf16[1,256,128]{2,1,0:T(8,128)(2,1)} %param.12) | copy-start | bytes 196612
  8.9 47.2 %all-to-all-start = ((bf16[8,16,6144]{2,1,0:T(8,128)(2,1)}), bf16[8,16,6144]{2,1,0:T(8,128)(2,1)S(1)}, u32[]{:S(2)}, u32[]{:S(2)}) async-start(bf16[8,16,6144]{2,1,0:T(8,128)(2,1)} %bitcast.87), calls=%async_computation | async-start | bytes 3145728 | tf_op jit(solution)/shard_map/all_to_all | solution.py:148
  16.1 4.7 %copy-start.14 = (f32[1,6,256]{2,0,1:T(1,128)S(1)}, f32[1,6,256]{2,0,1:T(1,128)}, u32[]{:S(2)}) copy-start(f32[1,6,256]{2,0,1:T(1,128)} %param.15) | copy-start | bytes 18436
  16.8 58.6 %collective-permute-start = (bf16[2,256,128]{2,1,0:T(8,128)(2,1)}, bf16[2,256,128]{2,1,0:T(8,128)(2,1)}, u32[]{:S(2)}, u32[]{:S(2)}) collective-permute-start(bf16[2,256,128]{2,1,0:T(8,128)(2,1)} %pad_maximum_fusion.1), channel_id=1, source_target_pairs={{0,32},{32,64},{64,96},{96,128},{128,160},{160,192},{192,224},{224... | collective-permute-start | bytes 393224 | tf_op jit(solution)/shard_map/ppermute | solution.py:16
  72.0 14.9 %collective-permute-start.4 = (bf16[128,4,4,4,48]{0,4,3,2,1:T(8,128)(2,1)}, bf16[128,4,4,4,48]{0,4,3,2,1:T(8,128)(2,1)}, u32[]{:S(2)}, u32[]{:S(2)}) collective-permute-start(bf16[128,4,4,4,48]{0,4,3,2,1:T(8,128)(2,1)} %bitcast.96), channel_id=1, source_target_pairs={{0,32},{32,0},{1,33},{33,1},{2,34},{34,2},{3,35},{35,3},{4,36},{36... | collective-permute-start | bytes 2359304 | tf_op jit(solution)/shard_map/ppermute | solution.py:64
  82.3 4.6 %copy-start.7 = (bf16[128,4,4,1,4,48]{0,5,4,2,1,3:T(8,128)(2,1)S(1)}, bf16[128,4,4,1,4,48]{0,5,4,2,1,3:T(8,128)(2,1)}, u32[]{:S(2)}) copy-start(bf16[128,4,4,1,4,48]{0,5,4,2,1,3:T(8,128)(2,1)} %copy.59) | copy-start | bytes 2359300
  84.4 3.8 %collective-permute-start.3 = (bf16[128,128]{0,1:T(8,128)(2,1)S(1)}, bf16[128,128]{0,1:T(8,128)(2,1)S(1)}, u32[]{:S(2)}, u32[]{:S(2)}) collective-permute-start(bf16[128,128]{0,1:T(8,128)(2,1)S(1)} %get-tuple-element.29), channel_id=1, source_target_pairs={{0,32},{32,0},{1,33},{33,1},{2,34},{34,2},{3,35},{35,3},{4,36},{36... | collective-permute-start | bytes 98312 | tf_op jit(solution)/shard_map/ppermute | solution.py:65
  90.1 4.5 %copy-start.1 = (f32[256,1536]{1,0:T(8,128)S(1)}, f32[256,1536]{1,0:T(8,128)}, u32[]{:S(2)}) copy-start(f32[256,1536]{1,0:T(8,128)} %fusion.4) | copy-start | bytes 4718596
  90.1 28.2 %all-to-all-start.1 = ((f32[4,4,4,48,128]{4,3,2,1,0:T(8,128)}), f32[4,4,4,48,128]{4,3,2,1,0:T(8,128)}, u32[]{:S(2)}, u32[]{:S(2)}) async-start(f32[4,4,4,48,128]{4,3,2,1,0:T(8,128)} %copy.62), calls=%async_computation.1 | async-start | bytes 3145728 | tf_op jit(solution)/shard_map/all_to_all | solution.py:69
  94.6 1.3 copy-start.2
  97.3 50.6 %collective-permute-start.2 = (bf16[2,1,256,128]{3,2,1,0:T(8,128)(2,1)}, bf16[2,1,256,128]{3,2,1,0:T(8,128)(2,1)}, u32[]{:S(2)}, u32[]{:S(2)}) collective-permute-start(bf16[2,1,256,128]{3,2,1,0:T(8,128)(2,1)} %fusion.17), channel_id=1, source_target_pairs={{992,0},{0,32},{32,64},{64,96},{96,128},{128,160},{160,192},{192,2... | collective-permute-start | bytes 393224 | tf_op jit(solution)/shard_map/ppermute | solution.py:22
  99.2 9.4 %collective-permute-start.1 = (bf16[2,256,128]{2,1,0:T(8,128)(2,1)}, bf16[2,256,128]{2,1,0:T(8,128)(2,1)S(1)}, u32[]{:S(2)}, u32[]{:S(2)}) collective-permute-start(bf16[2,256,128]{2,1,0:T(8,128)(2,1)} %collective-permute-done), channel_id=1, source_target_pairs={{0,32},{32,64},{64,96},{96,128},{128,160},{160,192},{192,224},{224... | collective-permute-start | bytes 393224 | tf_op jit(solution)/shard_map/ppermute | solution.py:16
  108.6 0.7 copy-start.8
  120.6 43.0 %all-to-all-start.2 = ((f32[16,48,128]{2,1,0:T(8,128)}), f32[16,48,128]{2,1,0:T(8,128)}, u32[]{:S(2)}, u32[]{:S(2)}) async-start(f32[16,48,128]{2,1,0:T(8,128)} %bitcast.95), calls=%async_computation.2 | async-start | bytes 786432 | tf_op jit(solution)/shard_map/all_to_all | solution.py:71
  139.0 2.2 %copy-start.6 = (f32[1536,128]{1,0:T(8,128)S(1)}, f32[1536,128]{1,0:T(8,128)}, u32[]{:S(2)}) copy-start(f32[1536,128]{1,0:T(8,128)} %convolution_multiply_fusion.3) | copy-start | bytes 2359300
  139.0 2.2 %copy-start.9 = (bf16[2,256,128]{2,1,0:T(8,128)(2,1)S(1)}, bf16[2,256,128]{2,1,0:T(8,128)(2,1)}, u32[]{:S(2)}) copy-start(bf16[2,256,128]{2,1,0:T(8,128)(2,1)} %copy-done.8) | copy-start | bytes 393220
  140.3 0.9 copy-start.4
  146.3 1.0 copy-start.3
  146.3 1.3 copy-start.5
  147.5 2.0 %copy-start.10 = (bf16[1,1,1,128,128]{3,4,2,1,0:T(8,128)(2,1)S(1)}, bf16[1,1,1,128,128]{3,4,2,1,0:T(8,128)(2,1)}, u32[]{:S(2)}) copy-start(bf16[1,1,1,128,128]{3,4,2,1,0:T(8,128)(2,1)} %get-tuple-element.27) | copy-start | bytes 98308
  147.5 2.0 %copy-start.11 = (bf16[1,1,1,128,128]{3,4,2,1,0:T(8,128)(2,1)S(1)}, bf16[1,1,1,128,128]{3,4,2,1,0:T(8,128)(2,1)}, u32[]{:S(2)}) copy-start(bf16[1,1,1,128,128]{3,4,2,1,0:T(8,128)(2,1)} %get-tuple-element.28) | copy-start | bytes 98308

commit v3 on v1

--- a/solution.py
+++ b/solution.py
@@ -54,12 +54,16 @@
 
 def staged_reduce_scatter(partial):
     rows, width = partial.shape
-    sizes = [lax.axis_size(name) for name in ROW_AXES]
-    block = rows // (sizes[0] * sizes[1] * sizes[2] * sizes[3])
-    pieces = partial.reshape(*sizes, block, width).transpose(2, 1, 0, 3, 4, 5)
-    for name in ("core", "xx", "zl", "dp"):
-        pieces = lax.all_to_all(pieces, name, 0, 0, tiled=True).sum(0)
-    return pieces.reshape(block, width)
+    zl, xx, core, dp = (lax.axis_size(name) for name in ROW_AXES)
+    block = rows // (zl * xx * core * dp)
+    pieces = partial.reshape(zl, xx, core, dp, block, width).transpose(2, 1, 0, 3, 4, 5)
+    here = lax.axis_index("core")
+    mine = lax.dynamic_index_in_dim(pieces, here, 0, keepdims=False)
+    other = lax.dynamic_index_in_dim(pieces, 1 - here, 0, keepdims=False)
+    pieces = mine + lax.ppermute(other, "core", [(i, (i + 1) % core) for i in range(core)])
+    pieces = lax.all_to_all(pieces, "xx", 0, 0, tiled=True).sum(0)
+    pieces = pieces.reshape(zl * dp, block, width)
+    return lax.all_to_all(pieces, ("zl", "dp"), 0, 0, tiled=True).sum(0)
 
 
 def body(

time: 159 us -> 160 us (level)
  the two profiles are of different devices: /device:TPU:4 before, /device:TPU:68 now
where the time goes in v3:
time: 160 us; the launch traced here: 159 us
  waiting for transfers between devices  64.2 us (40%)
  starting transfers between devices  40.1 us (25%)
  local copies, waits for them, and re-layouts  23.8 us (15%)
  matrix products  20.1 us (13%)
  other arithmetic  9.99 us (6%)
    all_to_all x1, waiting for transfers between devices, body(): lax.all_to_all(outbound, 'exp', split_axis=0, concat_axis=0, tiled=True)  39.8 us
    all_to_all x1, starting transfers between devices, staged_reduce_scatter(): return lax.all_to_all(pieces, ('zl', 'dp'), 0, 0, tiled=True).sum(0)  18.6 us
    all_to_all x1, waiting for transfers between devices, staged_reduce_scatter(): return lax.all_to_all(pieces, ('zl', 'dp'), 0, 0, tiled=True).sum(0)  13.8 us
    ppermute x2, waiting for transfers between devices, passed_along(): return lax.ppermute(value, axis, pairs)  10.6 us
    unnamed x45, local copies, waits for them, and re-layouts  9.46 us
    all_to_all x1, starting transfers between devices, body(): lax.all_to_all(outbound, 'exp', split_axis=0, concat_axis=0, tiled=True)  7.23 us
    all_to_all x1, starting transfers between devices, staged_reduce_scatter(): pieces = lax.all_to_all(pieces, 'xx', 0, 0, tiled=True).sum(0)  4.8 us
    dot_general x2, matrix products, pair_grads(): jnp.einsum('kqu,kud->kqd', score_grad, key_part, preferred_element_type=j...  4.72 us
  transfers between devices with their start and end apart: 7, of which 3 were waited for; matrix products, arithmetic and copies ran while one was open for 21% of the time, Pallas kernels for 0%

profile of v3, /device:TPU:68, one launch (start us, length us, event | category | flops | bytes accessed | tf_op | source)
XLA Modules:
  0.0 159.2 jit_solution(9856485674878391073)
XLA Ops:
  0.6 1.2 bitcast_convert_fusion
  1.8 2.0 %mul.179 = f32[32,2,6144]{2,1,0:T(2,128)} broadcast(f32[32,6144]{1,0:T(8,128)S(1)} %bitcast_convert_fusion), dimensions={0,2} | broadcast | bytes 2359296 | tf_op jit(solution)/shard_map/mul | solution.py:127
  3.8 2.4 %mul.180 = f32[64,6144]{1,0:T(8,128)S(1)} reshape(f32[32,2,6144]{2,1,0:T(2,128)} %mul.179) | data formatting | bytes 3145728 | tf_op jit(solution)/shard_map/mul | solution.py:127
  7.1 1.8 %convolution_convert_fusion = bf16[128,6144]{1,0:T(8,128)(2,1)} fusion(f32[64,6144]{1,0:T(8,128)S(1)} %mul.180, f32[64]{0:T(128)S(1)} %mul.177, s32[64]{0:T(128)S(1)} %multiply_add_fusion), kind=kOutput, calls=%fused_computation | convolution fusion | flops 102244352 | bytes 3146240 | tf_op jit(solution)/shard_map/dot_general | solution.py:141
  8.9 7.2 %all-to-all-start = ((bf16[8,16,6144]{2,1,0:T(8,128)(2,1)}), bf16[8,16,6144]{2,1,0:T(8,128)(2,1)S(1)}, u32[]{:S(2)}, u32[]{:S(2)}) async-start(bf16[8,16,6144]{2,1,0:T(8,128)(2,1)} %bitcast.99), calls=%async_computation | async-start | bytes 3145728 | tf_op jit(solution)/shard_map/all_to_all | solution.py:142
  16.2 39.8 %all-to-all-done = bf16[8,16,6144]{2,1,0:T(8,128)(2,1)S(1)} async-done(((bf16[8,16,6144]{2,1,0:T(8,128)(2,1)}), bf16[8,16,6144]{2,1,0:T(8,128)(2,1)S(1)}, u32[]{:S(2)}, u32[]{:S(2)}) %all-to-all-start) | async-done | bytes 1572896 | tf_op jit(solution)/shard_map/all_to_all | solution.py:142
  56.1 1.6 %copy.59 = bf16[128,6144]{0,1:T(8,128)(2,1)} copy(bf16[128,6144]{1,0:T(8,128)(2,1)S(1)} %bitcast.88) | data formatting | bytes 3145728 | tf_op jit(solution)/shard_map/all_to_all | solution.py:142
  57.6 2.0 %fusion.23 = f32[4,4,2,4,48,128]{5,4,3,2,1,0:T(8,128)S(1)} fusion(bf16[4,4,2,4,48,128]{5,4,3,2,1,0:T(8,128)(2,1)} %bitcast.90, f32[128,256]{0,1:T(8,128)S(1)} %bitcast_convert_fusion.1), kind=kOutput, calls=%fused_computation.54 | convolution fusion | flops 201424896 | bytes 4849664 | tf_op jit(solution)/shard_map/rc,rf->cf/dot_general | solution.py:157
  59.7 1.3 dynamic-slice_bitcast_fusion
  61.0 0.8 copy-done.1
  61.8 2.0 %collective-permute-start.3 = (f32[4,4,4,48,128]{4,3,2,0,1:T(8,128)}, f32[4,4,4,48,128]{4,3,2,0,1:T(8,128)}, u32[]{:S(2)}, u32[]{:S(2)}) collective-permute-start(f32[4,4,4,48,128]{4,3,2,0,1:T(8,128)} %dynamic-slice_bitcast_fusion), channel_id=1, source_target_pairs={{0,32},{32,0},{1,33},{33,1},{2,34},{34,2},{3,35},{35,3},{4,36},{36... | collective-permute-start | bytes 4718600 | tf_op jit(solution)/shard_map/ppermute | solution.py:63
  63.9 0.7 pad_maximum_fusion
  64.5 2.4 %collective-permute-start = (bf16[2,256,128]{2,1,0:T(8,128)(2,1)}, bf16[2,256,128]{2,1,0:T(8,128)(2,1)}, u32[]{:S(2)}, u32[]{:S(2)}) collective-permute-start(bf16[2,256,128]{2,1,0:T(8,128)(2,1)} %pad_maximum_fusion), channel_id=1, source_target_pairs={{0,32},{32,64},{64,96},{96,128},{128,160},{160,192},{192,224},{224... | collective-permute-start | bytes 393224 | tf_op jit(solution)/shard_map/ppermute | solution.py:16
  67.0 1.2 copy.51
  68.1 1.0 copy.52
  69.1 1.9 %copy.53 = bf16[1,256,768]{1,2,0:T(8,128)(2,1)} copy(bf16[1,256,768]{2,1,0:T(8,128)(2,1)} %param.14) | data formatting | bytes 786432 | tf_op args[3]
  71.1 1.2 copy.54
  72.3 0.6 reduce.1
  72.9 0.7 sub.52
  73.6 1.6 fusion.4
  75.2 1.1 copy-done.4
  76.3 2.2 %fusion.6 = bf16[256,1536]{1,0:T(8,128)(2,1)} fusion(f32[256,1536]{1,0:T(8,128)S(1)} %fusion.4, bf16[1536,128]{1,0:T(8,128)(2,1)S(1)} %bitcast.91, f32[1536]{0:T(1024)S(1)} %sub.52, bf16[2,256,128]{2,1,0:T(8,128)(2,1)} %collective-permute-done), kind=kOutput, calls=%fused_computation.11 | convolution fusion | flops 101842944 | bytes 2824192 | tf_op jit(solution)/shard_map/kqd,kud->kqu/dot_general | solution.py:37
  78.5 1.6 %bitcast_add_fusion = f32[4,4,4,48,128]{4,3,2,0,1:T(8,128)S(1)} fusion(f32[4,4,4,48,128]{4,3,2,0,1:T(8,128)} %collective-permute-done.3, f32[4,4,2,4,48,128]{5,4,3,2,1,0:T(8,128)S(1)} %copy-done.2, s32[]{:T(128)S(6)} %select_n.7), kind=kLoop, calls=%fused_computation.17 | loop fusion | flops 393216 | bytes 4718596 | tf_op jit(solution)/shard_map/add | solution.py:63
  80.2 1.3 copy.62
  81.4 4.8 %all-to-all-start.1 = ((f32[4,4,4,48,128]{4,3,2,1,0:T(8,128)}), f32[4,4,4,48,128]{4,3,2,1,0:T(8,128)}, u32[]{:S(2)}, u32[]{:S(2)}) async-start(f32[4,4,4,48,128]{4,3,2,1,0:T(8,128)} %copy.62), calls=%async_computation.1 | async-start | bytes 3145728 | tf_op jit(solution)/shard_map/all_to_all | solution.py:64
  86.2 1.6 fusion.13
  87.8 1.9 %convolution_bitcast_fusion.1 = f32[1,1,256,128]{3,2,1,0:T(8,128)S(1)} fusion(bf16[1536,128]{1,0:T(8,128)(2,1)S(1)} %bitcast.92, f32[256,1536]{1,0:T(8,128)} %copy-done.4), kind=kOutput, calls=%fused_computation.25 | convolution fusion | flops 101056512 | bytes 2097152 | tf_op jit(solution)/shard_map/kqu,kqd->kud/dot_general | solution.py:49
  89.7 0.7 fusion.17
  90.3 3.0 %collective-permute-start.2 = (bf16[2,1,256,128]{3,2,1,0:T(8,128)(2,1)}, bf16[2,1,256,128]{3,2,1,0:T(8,128)(2,1)}, u32[]{:S(2)}, u32[]{:S(2)}) collective-permute-start(bf16[2,1,256,128]{3,2,1,0:T(8,128)(2,1)} %fusion.17), channel_id=1, source_target_pairs={{992,0},{0,32},{32,64},{64,96},{96,128},{128,160},{160,192},{192,2... | collective-permute-start | bytes 393224 | tf_op jit(solution)/shard_map/ppermute | solution.py:22
  93.3 2.1 %collective-permute-start.1 = (bf16[2,256,128]{2,1,0:T(8,128)(2,1)}, bf16[2,256,128]{2,1,0:T(8,128)(2,1)S(1)}, u32[]{:S(2)}, u32[]{:S(2)}) collective-permute-start(bf16[2,256,128]{2,1,0:T(8,128)(2,1)} %collective-permute-done), channel_id=1, source_target_pairs={{0,32},{32,64},{64,96},{96,128},{128,160},{160,192},{192,224},{224... | collective-permute-start | bytes 393224 | tf_op jit(solution)/shard_map/ppermute | solution.py:16
  95.5 2.1 %convolution_multiply_fusion.3 = f32[1536,128]{1,0:T(8,128)} fusion(bf16[256,1536]{1,0:T(8,128)(2,1)S(1)} %copy-done.7, f32[]{:T(128)S(6)} %mul.159, bf16[2,256,128]{2,1,0:T(8,128)(2,1)} %collective-permute-done), kind=kOutput, calls=%fused_computation.14 | convolution fusion | flops 100859904 | bytes 1638404 | tf_op jit(solution)/shard_map/kqu,kud->kqd/dot_general | solution.py:42
  97.6 10.6 %collective-permute-done.1 = bf16[2,256,128]{2,1,0:T(8,128)(2,1)S(1)} collective-permute-done((bf16[2,256,128]{2,1,0:T(8,128)(2,1)}, bf16[2,256,128]{2,1,0:T(8,128)(2,1)S(1)}, u32[]{:S(2)}, u32[]{:S(2)}) %collective-permute-start.1) | collective-permute-done | bytes 131104 | tf_op jit(solution)/shard_map/ppermute | solution.py:16
  108.2 0.4 fusion.5
  108.8 1.2 copy-done.3
  110.0 1.3 fusion.7
  111.3 2.3 %reduce_sum.28 = f32[4,4,48,128]{3,2,1,0:T(8,128)} reduce(f32[4,4,4,48,128]{4,3,2,1,0:T(8,128)} %all-to-all-done.1, f32[]{:T(128)} %constant.44.clone.1), dimensions={0}, to_apply=%region_2.3 | reduce | flops 294912 | bytes 1966084 | tf_op jit(solution)/shard_map/reduce_sum | solution.py:64
  113.6 18.6 %all-to-all-start.2 = ((f32[16,48,128]{2,1,0:T(8,128)}), f32[16,48,128]{2,1,0:T(8,128)}, u32[]{:S(2)}, u32[]{:S(2)}) async-start(f32[16,48,128]{2,1,0:T(8,128)} %bitcast.104), calls=%async_computation.2 | async-start | bytes 786432 | tf_op jit(solution)/shard_map/all_to_all | solution.py:66
  132.1 2.6 %fusion.9 = bf16[1536,128]{1,0:T(8,128)(2,1)} fusion(f32[1536,128]{1,0:T(8,128)} %convolution_multiply_fusion.3, bf16[256,1536]{1,0:T(8,128)(2,1)} %fusion.7, f32[]{:T(128)S(6)} %mul.165, bf16[2,256,128]{2,1,0:T(8,128)(2,1)} %copy-done.11), kind=kOutput, calls=%fused_computation.16 | convolution fusion | flops 101253120 | bytes 2031620 | tf_op jit(solution)/shard_map/kqu,kud->kqd/dot_general | solution.py:42
  134.7 1.9 %copy.55 = bf16[1,6,256,128]{2,3,1,0:T(8,128)(2,1)} copy(bf16[1,6,256,128]{3,2,1,0:T(8,128)(2,1)} %bitcast.100) | data formatting | bytes 786432 | tf_op jit(solution)/shard_map/convert_element_type | solution.py:115
  136.6 1.9 %copy.63 = bf16[1,256,768]{2,1,0:T(8,128)(2,1)} copy(bf16[1,256,768]{1,2,0:T(8,128)(2,1)} %bitcast.101) | data formatting | bytes 786432
  138.5 1.9 %convolution_bitcast_fusion = f32[1,1,256,128]{3,2,1,0:T(8,128)S(1)} fusion(bf16[1536,128]{1,0:T(8,128)(2,1)S(1)} %bitcast.94, f32[256,1536]{1,0:T(8,128)} %copy-done.3), kind=kOutput, calls=%fused_computation.22 | convolution fusion | flops 101056512 | bytes 2097152 | tf_op jit(solution)/shard_map/kqu,kqd->kud/dot_general | solution.py:49
  140.8 0.9 fusion.19
  141.7 0.7 slice_bitcast_fusion
  142.4 0.6 fusion.27
  143.0 0.7 copy.64
  143.7 13.8 %all-to-all-done.2 = f32[16,48,128]{2,1,0:T(8,128)} async-done(((f32[16,48,128]{2,1,0:T(8,128)}), f32[16,48,128]{2,1,0:T(8,128)}, u32[]{:S(2)}, u32[]{:S(2)}) %all-to-all-start.2) | async-done | bytes 393248 | tf_op jit(solution)/shard_map/all_to_all | solution.py:66
  157.6 1.0 reduce_sum.29
  158.6 0.6 multiply_bitcast_fusion
  (53 shorter events, 1.6 us)
Async XLA Ops:
  0.6 141.8 %copy-start = (bf16[1,128,6144]{2,1,0:T(8,128)(2,1)S(1)}, bf16[1,128,6144]{2,1,0:T(8,128)(2,1)}, u32[]{:S(2)}) copy-start(bf16[1,128,6144]{2,1,0:T(8,128)(2,1)} %param.21) | copy-start | bytes 4718596
  3.8 2.4 %copy-start.17 = (f32[1,32,2]{1,2,0:T(2,128)S(1)}, f32[1,32,2]{1,2,0:T(2,128)}, u32[]{:S(2)}) copy-start(f32[1,32,2]{1,2,0:T(2,128)} %param.18) | copy-start | bytes 772
  3.8 2.6 %copy-start.18 = (s32[1,32,2]{1,2,0:T(2,128)S(1)}, s32[1,32,2]{1,2,0:T(2,128)}, u32[]{:S(2)}) copy-start(s32[1,32,2]{1,2,0:T(2,128)} %param.19) | copy-start | bytes 772
  8.9 7.2 %copy-start.12 = (bf16[1,1,1,128,256]{4,3,2,1,0:T(8,128)(2,1)S(1)}, bf16[1,1,1,128,256]{4,3,2,1,0:T(8,128)(2,1)}, u32[]{:S(2)}) copy-start(bf16[1,1,1,128,256]{4,3,2,1,0:T(8,128)(2,1)} %param.20) | copy-start | bytes 196612
  8.9 47.2 %all-to-all-start = ((bf16[8,16,6144]{2,1,0:T(8,128)(2,1)}), bf16[8,16,6144]{2,1,0:T(8,128)(2,1)S(1)}, u32[]{:S(2)}, u32[]{:S(2)}) async-start(bf16[8,16,6144]{2,1,0:T(8,128)(2,1)} %bitcast.99), calls=%async_computation | async-start | bytes 3145728 | tf_op jit(solution)/shard_map/all_to_all | solution.py:142
  16.2 41.4 %copy-start.9 = (f32[128,256]{0,1:T(8,128)}, f32[128,256]{0,1:T(8,128)S(1)}, u32[]{:S(2)}) copy-start(f32[128,256]{0,1:T(8,128)S(1)} %bitcast_convert_fusion.1) | copy-start | bytes 393220
  59.6 2.2 %copy-start.1 = (f32[4,4,2,4,48,128]{5,4,3,2,1,0:T(8,128)}, f32[4,4,2,4,48,128]{5,4,3,2,1,0:T(8,128)S(1)}, u32[]{:S(2)}) copy-start(f32[4,4,2,4,48,128]{5,4,3,2,1,0:T(8,128)S(1)} %fusion.23) | copy-start | bytes 9437188
  59.7 4.2 %copy-start.13 = (bf16[1,256,128]{2,1,0:T(8,128)(2,1)S(1)}, bf16[1,256,128]{2,1,0:T(8,128)(2,1)}, u32[]{:S(2)}) copy-start(bf16[1,256,128]{2,1,0:T(8,128)(2,1)} %param.13) | copy-start | bytes 196612
  59.7 4.2 %copy-start.14 = (bf16[1,256,128]{2,1,0:T(8,128)(2,1)S(1)}, bf16[1,256,128]{2,1,0:T(8,128)(2,1)}, u32[]{:S(2)}) copy-start(bf16[1,256,128]{2,1,0:T(8,128)(2,1)} %param.12) | copy-start | bytes 196612
  61.8 7.3 %copy-start.15 = (f32[1,6,256]{2,0,1:T(1,128)S(1)}, f32[1,6,256]{2,0,1:T(1,128)}, u32[]{:S(2)}) copy-start(f32[1,6,256]{2,0,1:T(1,128)} %param.15) | copy-start | bytes 18436
  61.8 16.7 %collective-permute-start.3 = (f32[4,4,4,48,128]{4,3,2,0,1:T(8,128)}, f32[4,4,4,48,128]{4,3,2,0,1:T(8,128)}, u32[]{:S(2)}, u32[]{:S(2)}) collective-permute-start(f32[4,4,4,48,128]{4,3,2,0,1:T(8,128)} %dynamic-slice_bitcast_fusion), channel_id=1, source_target_pairs={{0,32},{32,0},{1,33},{33,1},{2,34},{34,2},{3,35},{35,3},{4,36},{36... | collective-permute-start | bytes 4718600 | tf_op jit(solution)/shard_map/ppermute | solution.py:63
  64.5 9.1 %collective-permute-start = (bf16[2,256,128]{2,1,0:T(8,128)(2,1)}, bf16[2,256,128]{2,1,0:T(8,128)(2,1)}, u32[]{:S(2)}, u32[]{:S(2)}) collective-permute-start(bf16[2,256,128]{2,1,0:T(8,128)(2,1)} %pad_maximum_fusion), channel_id=1, source_target_pairs={{0,32},{32,64},{64,96},{96,128},{128,160},{160,192},{192,224},{224... | collective-permute-start | bytes 393224 | tf_op jit(solution)/shard_map/ppermute | solution.py:16
  67.0 5.3 %copy-start.16 = (f32[1,6,256]{2,0,1:T(1,128)S(1)}, f32[1,6,256]{2,0,1:T(1,128)}, u32[]{:S(2)}) copy-start(f32[1,6,256]{2,0,1:T(1,128)} %param.16) | copy-start | bytes 18436
  73.6 4.9 %copy-start.2 = (f32[4,4,2,4,48,128]{5,4,3,2,1,0:T(8,128)S(1)}, f32[4,4,2,4,48,128]{5,4,3,2,1,0:T(8,128)}, u32[]{:S(2)}) copy-start(f32[4,4,2,4,48,128]{5,4,3,2,1,0:T(8,128)} %copy-done.1) | copy-start | bytes 9437188
  75.2 1.1 copy-start.4
  81.4 29.9 %all-to-all-start.1 = ((f32[4,4,4,48,128]{4,3,2,1,0:T(8,128)}), f32[4,4,4,48,128]{4,3,2,1,0:T(8,128)}, u32[]{:S(2)}, u32[]{:S(2)}) async-start(f32[4,4,4,48,128]{4,3,2,1,0:T(8,128)} %copy.62), calls=%async_computation.1 | async-start | bytes 3145728 | tf_op jit(solution)/shard_map/all_to_all | solution.py:64
  87.8 7.7 %copy-start.7 = (bf16[256,1536]{1,0:T(8,128)(2,1)S(1)}, bf16[256,1536]{1,0:T(8,128)(2,1)}, u32[]{:S(2)}) copy-start(bf16[256,1536]{1,0:T(8,128)(2,1)} %fusion.6) | copy-start | bytes 2359300
  87.8 20.4 %copy-start.5 = (bf16[1,6,256,128]{3,2,1,0:T(8,128)(2,1)S(1)}, bf16[1,6,256,128]{3,2,1,0:T(8,128)(2,1)}, u32[]{:S(2)}) copy-start(bf16[1,6,256,128]{3,2,1,0:T(8,128)(2,1)} %copy.52) | copy-start | bytes 1179652
  90.3 50.4 %collective-permute-start.2 = (bf16[2,1,256,128]{3,2,1,0:T(8,128)(2,1)}, bf16[2,1,256,128]{3,2,1,0:T(8,128)(2,1)}, u32[]{:S(2)}, u32[]{:S(2)}) collective-permute-start(bf16[2,1,256,128]{3,2,1,0:T(8,128)(2,1)} %fusion.17), channel_id=1, source_target_pairs={{992,0},{0,32},{32,64},{64,96},{96,128},{128,160},{160,192},{192,2... | collective-permute-start | bytes 393224 | tf_op jit(solution)/shard_map/ppermute | solution.py:22
  93.3 14.8 %collective-permute-start.1 = (bf16[2,256,128]{2,1,0:T(8,128)(2,1)}, bf16[2,256,128]{2,1,0:T(8,128)(2,1)S(1)}, u32[]{:S(2)}, u32[]{:S(2)}) collective-permute-start(bf16[2,256,128]{2,1,0:T(8,128)(2,1)} %collective-permute-done), channel_id=1, source_target_pairs={{0,32},{32,64},{64,96},{96,128},{128,160},{160,192},{192,224},{224... | collective-permute-start | bytes 393224 | tf_op jit(solution)/shard_map/ppermute | solution.py:16
  108.2 0.7 copy-start.11
  108.8 1.2 copy-start.3
  113.6 44.0 %all-to-all-start.2 = ((f32[16,48,128]{2,1,0:T(8,128)}), f32[16,48,128]{2,1,0:T(8,128)}, u32[]{:S(2)}, u32[]{:S(2)}) async-start(f32[16,48,128]{2,1,0:T(8,128)} %bitcast.104), calls=%async_computation.2 | async-start | bytes 786432 | tf_op jit(solution)/shard_map/all_to_all | solution.py:66
  138.5 1.9 %copy-start.6 = (bf16[1,6,256,128]{3,2,1,0:T(8,128)(2,1)S(1)}, bf16[1,6,256,128]{3,2,1,0:T(8,128)(2,1)}, u32[]{:S(2)}) copy-start(bf16[1,6,256,128]{3,2,1,0:T(8,128)(2,1)} %copy.52) | copy-start | bytes 1179652
  138.5 1.9 %copy-start.8 = (bf16[256,1536]{1,0:T(8,128)(2,1)S(1)}, bf16[256,1536]{1,0:T(8,128)(2,1)}, u32[]{:S(2)}) copy-start(bf16[256,1536]{1,0:T(8,128)(2,1)} %fusion.7) | copy-start | bytes 2359300
  140.4 2.0 %copy-start.10 = (f32[128,256]{0,1:T(8,128)S(1)}, f32[128,256]{0,1:T(8,128)}, u32[]{:S(2)}) copy-start(f32[128,256]{0,1:T(8,128)} %copy-done.9) | copy-start | bytes 393220

commit v4 on v3

--- a/solution.py
+++ b/solution.py
@@ -61,9 +61,10 @@
     mine = lax.dynamic_index_in_dim(pieces, here, 0, keepdims=False)
     other = lax.dynamic_index_in_dim(pieces, 1 - here, 0, keepdims=False)
     pieces = mine + lax.ppermute(other, "core", [(i, (i + 1) % core) for i in range(core)])
-    pieces = lax.all_to_all(pieces, "xx", 0, 0, tiled=True).sum(0)
-    pieces = pieces.reshape(zl * dp, block, width)
-    return lax.all_to_all(pieces, ("zl", "dp"), 0, 0, tiled=True).sum(0)
+    pieces = lax.all_to_all(pieces.astype(jnp.bfloat16), "xx", 0, 0, tiled=True)
+    pieces = pieces.astype(jnp.float32).sum(0).reshape(zl * dp, block, width)
+    pieces = lax.all_to_all(pieces.astype(jnp.bfloat16), ("zl", "dp"), 0, 0, tiled=True)
+    return pieces.astype(jnp.float32).sum(0)
 
 
 def body(

time: 160 us -> 131 us (0.82)
  the two profiles are of different devices: /device:TPU:68 before, /device:TPU:64 now
where the time goes in v4:
time: 131 us; the launch traced here: 130 us
  waiting for transfers between devices  41.4 us (32%)
  starting transfers between devices  38.9 us (30%)
  local copies, waits for them, and re-layouts  21.4 us (16%)
  matrix products  18.8 us (14%)
  other arithmetic  8.93 us (7%)
    all_to_all x1, waiting for transfers between devices, body(): lax.all_to_all(outbound, 'exp', split_axis=0, concat_axis=0, tiled=True)  25 us
    all_to_all x1, starting transfers between devices, staged_reduce_scatter(): lax.all_to_all(pieces.astype(jnp.bfloat16), ('zl', 'dp'), 0, 0, tiled=True)  18 us
    all_to_all x1, waiting for transfers between devices, staged_reduce_scatter(): lax.all_to_all(pieces.astype(jnp.bfloat16), ('zl', 'dp'), 0, 0, tiled=True)  12.6 us
    unnamed x35, local copies, waits for them, and re-layouts  8.69 us
    all_to_all x1, starting transfers between devices, body(): lax.all_to_all(outbound, 'exp', split_axis=0, concat_axis=0, tiled=True)  7.23 us
    ppermute x2, starting transfers between devices, passed_along(): return lax.ppermute(value, axis, pairs)  4.93 us
    dot_general x2, matrix products, pair_grads(): jnp.einsum('kqu,kud->kqd', score_grad, key_part, preferred_element_type=j...  4.76 us
    mul x3, local copies, waits for them, and re-layouts, body(): router_prob[0][:, :, None] * tok_grad[0].astype(jnp.float32)[:, None, :]  4.54 us
  transfers between devices with their start and end apart: 7, of which 4 were waited for; matrix products, arithmetic and copies ran while one was open for 27% of the time, Pallas kernels for 0%

profile of v4, /device:TPU:64, one launch (start us, length us, event | category | flops | bytes accessed | tf_op | source)
XLA Modules:
  0.0 130.4 jit_solution(17674327990934778490)
XLA Ops:
  0.6 1.2 bitcast_convert_fusion
  1.8 2.0 %mul.179 = f32[32,2,6144]{2,1,0:T(2,128)} broadcast(f32[32,6144]{1,0:T(8,128)S(1)} %bitcast_convert_fusion), dimensions={0,2} | broadcast | bytes 2359296 | tf_op jit(solution)/shard_map/mul | solution.py:128
  3.8 2.4 %mul.180 = f32[64,6144]{1,0:T(8,128)S(1)} reshape(f32[32,2,6144]{2,1,0:T(2,128)} %mul.179) | data formatting | bytes 3145728 | tf_op jit(solution)/shard_map/mul | solution.py:128
  7.0 1.8 %convolution_convert_fusion = bf16[128,6144]{1,0:T(8,128)(2,1)} fusion(f32[64,6144]{1,0:T(8,128)S(1)} %mul.180, f32[64]{0:T(128)S(1)} %mul.177, s32[64]{0:T(128)S(1)} %multiply_add_fusion), kind=kOutput, calls=%fused_computation | convolution fusion | flops 102244352 | bytes 3146240 | tf_op jit(solution)/shard_map/dot_general | solution.py:142
  8.8 7.2 %all-to-all-start = ((bf16[8,16,6144]{2,1,0:T(8,128)(2,1)}), bf16[8,16,6144]{2,1,0:T(8,128)(2,1)S(1)}, u32[]{:S(2)}, u32[]{:S(2)}) async-start(bf16[8,16,6144]{2,1,0:T(8,128)(2,1)} %bitcast.101), calls=%async_computation | async-start | bytes 3145728 | tf_op jit(solution)/shard_map/all_to_all | solution.py:143
  16.1 0.7 pad_maximum_fusion
  16.8 1.9 %collective-permute-start = (bf16[2,256,128]{2,1,0:T(8,128)(2,1)}, bf16[2,256,128]{2,1,0:T(8,128)(2,1)}, u32[]{:S(2)}, u32[]{:S(2)}) collective-permute-start(bf16[2,256,128]{2,1,0:T(8,128)(2,1)} %pad_maximum_fusion), channel_id=1, source_target_pairs={{0,32},{32,64},{64,96},{96,128},{128,160},{160,192},{192,224},{224... | collective-permute-start | bytes 393224 | tf_op jit(solution)/shard_map/ppermute | solution.py:16
  18.7 1.2 copy.51
  19.9 0.9 copy.52
  20.9 1.9 %copy.53 = bf16[1,256,768]{1,2,0:T(8,128)(2,1)} copy(bf16[1,256,768]{2,1,0:T(8,128)(2,1)} %param.14) | data formatting | bytes 786432 | tf_op args[3]
  22.8 1.2 copy.54
  24.0 0.6 reduce.2
  24.7 0.7 sub.52
  25.4 1.6 %copy.58 = bf16[1,1,1,128,256]{3,4,2,1,0:T(8,128)(2,1)} copy(bf16[1,1,1,128,256]{4,3,2,1,0:T(8,128)(2,1)} %param.20) | data formatting | bytes 131072 | tf_op args[9]
  26.9 1.5 %bitcast_convert_fusion.1 = f32[128,256]{0,1:T(8,128)} fusion(bf16[1,1,1,128,256]{3,4,2,1,0:T(8,128)(2,1)} %copy.58), kind=kLoop, calls=%fused_computation.47 | loop fusion | flops 32768 | bytes 196608 | tf_op jit(solution)/shard_map/convert_element_type | solution.py:144
  28.4 2.6 %fusion.4 = f32[256,1536]{1,0:T(8,128)} fusion(bf16[1536,128]{1,0:T(8,128)(2,1)} %bitcast.97, f32[1536]{0:T(1024)S(1)} %sub.49, bf16[2,256,128]{2,1,0:T(8,128)(2,1)} %collective-permute-done), kind=kOutput, calls=%fused_computation.9 | convolution fusion | flops 101449728 | bytes 2037760 | tf_op jit(solution)/shard_map/kqd,kud->kqu/dot_general | solution.py:32
  31.0 25.0 %all-to-all-done = bf16[8,16,6144]{2,1,0:T(8,128)(2,1)S(1)} async-done(((bf16[8,16,6144]{2,1,0:T(8,128)(2,1)}), bf16[8,16,6144]{2,1,0:T(8,128)(2,1)S(1)}, u32[]{:S(2)}, u32[]{:S(2)}) %all-to-all-start) | async-done | bytes 1572896 | tf_op jit(solution)/shard_map/all_to_all | solution.py:143
  56.0 1.6 %copy.59 = bf16[128,6144]{0,1:T(8,128)(2,1)} copy(bf16[128,6144]{1,0:T(8,128)(2,1)S(1)} %bitcast.90) | data formatting | bytes 3145728 | tf_op jit(solution)/shard_map/all_to_all | solution.py:143
  57.6 2.0 %fusion.24 = f32[4,4,2,4,48,128]{5,4,3,2,1,0:T(8,128)S(1)} fusion(bf16[4,4,2,4,48,128]{5,4,3,2,1,0:T(8,128)(2,1)} %bitcast.92, f32[128,256]{0,1:T(8,128)} %bitcast_convert_fusion.1), kind=kOutput, calls=%fused_computation.56 | convolution fusion | flops 201424896 | bytes 4849664 | tf_op jit(solution)/shard_map/rc,rf->cf/dot_general | solution.py:158
  59.8 2.1 %collective-permute-start.3 = (f32[4,4,4,48,128]{4,3,2,0,1:T(8,128)S(1)}, f32[4,4,4,48,128]{4,3,2,0,1:T(8,128)S(1)}, u32[]{:S(2)}, u32[]{:S(2)}) collective-permute-start(f32[4,4,4,48,128]{4,3,2,0,1:T(8,128)S(1)} %dynamic-slice_bitcast_fusion), channel_id=1, source_target_pairs={{0,32},{32,0},{1,33},{33,1},{2,34},{34,2},{3,35},{35,3},{4,36},{36... | collective-permute-start | bytes 4718600 | tf_op jit(solution)/shard_map/ppermute | solution.py:63
  61.9 1.2 fusion.6
  63.1 0.4 fusion.14
  63.5 0.4 convolution_bitcast_fusion.1
  63.8 0.7 fusion.18
  64.5 2.4 %collective-permute-start.2 = (bf16[2,1,256,128]{3,2,1,0:T(8,128)(2,1)}, bf16[2,1,256,128]{3,2,1,0:T(8,128)(2,1)}, u32[]{:S(2)}, u32[]{:S(2)}) collective-permute-start(bf16[2,1,256,128]{3,2,1,0:T(8,128)(2,1)} %fusion.18), channel_id=1, source_target_pairs={{992,0},{0,32},{32,64},{64,96},{96,128},{128,160},{160,192},{192,2... | collective-permute-start | bytes 393224 | tf_op jit(solution)/shard_map/ppermute | solution.py:22
  66.9 3.0 %collective-permute-start.1 = (bf16[2,256,128]{2,1,0:T(8,128)(2,1)}, bf16[2,256,128]{2,1,0:T(8,128)(2,1)S(1)}, u32[]{:S(2)}, u32[]{:S(2)}) collective-permute-start(bf16[2,256,128]{2,1,0:T(8,128)(2,1)} %collective-permute-done), channel_id=1, source_target_pairs={{0,32},{32,64},{64,96},{96,128},{128,160},{160,192},{192,224},{224... | collective-permute-start | bytes 393224 | tf_op jit(solution)/shard_map/ppermute | solution.py:16
  70.0 2.2 %convolution_multiply_fusion.3 = f32[1536,128]{1,0:T(8,128)} fusion(bf16[256,1536]{1,0:T(8,128)(2,1)S(1)} %fusion.6, f32[]{:T(128)S(6)} %mul.159, bf16[2,256,128]{2,1,0:T(8,128)(2,1)} %collective-permute-done), kind=kOutput, calls=%fused_computation.14 | convolution fusion | flops 100859904 | bytes 1638404 | tf_op jit(solution)/shard_map/kqu,kud->kqd/dot_general | solution.py:42
  72.1 3.4 %collective-permute-done.1 = bf16[2,256,128]{2,1,0:T(8,128)(2,1)S(1)} collective-permute-done((bf16[2,256,128]{2,1,0:T(8,128)(2,1)}, bf16[2,256,128]{2,1,0:T(8,128)(2,1)S(1)}, u32[]{:S(2)}, u32[]{:S(2)}) %collective-permute-start.1) | collective-permute-done | bytes 131104 | tf_op jit(solution)/shard_map/ppermute | solution.py:16
  75.5 0.4 fusion.5
  75.9 1.1 copy-done.1
  77.1 1.3 fusion.7
  78.3 0.2 fusion.10
  78.5 0.9 copy.62
  79.5 4.2 %all-to-all-start.1 = ((bf16[4,4,4,48,128]{4,3,2,1,0:T(8,128)(2,1)}), bf16[4,4,4,48,128]{4,3,2,1,0:T(8,128)(2,1)}, u32[]{:S(2)}, u32[]{:S(2)}) async-start(bf16[4,4,4,48,128]{4,3,2,1,0:T(8,128)(2,1)} %copy.62), calls=%async_computation.1 | async-start | bytes 1572864 | tf_op jit(solution)/shard_map/all_to_all | solution.py:64
  83.7 2.6 %fusion.9 = bf16[1536,128]{1,0:T(8,128)(2,1)} fusion(f32[1536,128]{1,0:T(8,128)} %convolution_multiply_fusion.3, bf16[256,1536]{1,0:T(8,128)(2,1)} %fusion.7, f32[]{:T(128)S(6)} %mul.165, bf16[2,256,128]{2,1,0:T(8,128)(2,1)} %copy-done.7), kind=kOutput, calls=%fused_computation.16 | convolution fusion | flops 101253120 | bytes 2031620 | tf_op jit(solution)/shard_map/kqu,kud->kqd/dot_general | solution.py:42
  86.3 1.9 %copy.55 = bf16[1,6,256,128]{2,3,1,0:T(8,128)(2,1)} copy(bf16[1,6,256,128]{3,2,1,0:T(8,128)(2,1)} %bitcast.102) | data formatting | bytes 786432 | tf_op jit(solution)/shard_map/convert_element_type | solution.py:116
  88.2 1.9 %copy.63 = bf16[1,256,768]{2,1,0:T(8,128)(2,1)} copy(bf16[1,256,768]{1,2,0:T(8,128)(2,1)} %bitcast.103) | data formatting | bytes 786432
  90.1 2.5 %convolution_bitcast_fusion = f32[1,1,256,128]{3,2,1,0:T(8,128)} fusion(bf16[1536,128]{1,0:T(8,128)(2,1)S(1)} %bitcast.96, f32[256,1536]{1,0:T(8,128)} %copy-done.1), kind=kOutput, calls=%fused_computation.23 | convolution fusion | flops 101056512 | bytes 2097152 | tf_op jit(solution)/shard_map/kqu,kqd->kud/dot_general | solution.py:49
  92.6 1.0 fusion.13
  93.6 0.4 all-to-all-done.1
  94.0 2.0 %reduce_sum.31 = bf16[4,4,48,128]{3,2,1,0:T(8,128)(2,1)} reduce(bf16[4,4,4,48,128]{4,3,2,1,0:T(8,128)(2,1)} %all-to-all-done.1, bf16[]{:T(256)} %constant.50.clone.1), dimensions={0}, to_apply=%region_2.3 | reduce | flops 294912 | bytes 983042 | tf_op jit(solution)/shard_map/reduce_sum | solution.py:65
  96.0 18.0 %all-to-all-start.2 = ((bf16[16,48,128]{2,1,0:T(8,128)(2,1)}), bf16[16,48,128]{2,1,0:T(8,128)(2,1)S(1)}, u32[]{:S(2)}, u32[]{:S(2)}) async-start(bf16[16,48,128]{2,1,0:T(8,128)(2,1)} %bitcast.34), calls=%async_computation.2 | async-start | bytes 393216 | tf_op jit(solution)/shard_map/all_to_all | solution.py:66
  114.0 1.1 fusion.20
  115.1 0.7 slice_bitcast_fusion
  115.8 0.6 fusion.28
  116.4 0.7 copy.64
  117.1 12.6 %all-to-all-done.2 = bf16[16,48,128]{2,1,0:T(8,128)(2,1)S(1)} async-done(((bf16[16,48,128]{2,1,0:T(8,128)(2,1)}), bf16[16,48,128]{2,1,0:T(8,128)(2,1)S(1)}, u32[]{:S(2)}, u32[]{:S(2)}) %all-to-all-start.2) | async-done | bytes 196640 | tf_op jit(solution)/shard_map/all_to_all | solution.py:66
  129.7 0.6 multiply_bitcast_fusion
  (43 shorter events, 1.0 us)
Async XLA Ops:
  0.6 115.2 %copy-start = (bf16[1,128,6144]{2,1,0:T(8,128)(2,1)S(1)}, bf16[1,128,6144]{2,1,0:T(8,128)(2,1)}, u32[]{:S(2)}) copy-start(bf16[1,128,6144]{2,1,0:T(8,128)(2,1)} %param.21) | copy-start | bytes 4718596
  3.8 2.4 %copy-start.12 = (f32[1,32,2]{1,2,0:T(2,128)S(1)}, f32[1,32,2]{1,2,0:T(2,128)}, u32[]{:S(2)}) copy-start(f32[1,32,2]{1,2,0:T(2,128)} %param.18) | copy-start | bytes 772
  3.8 2.6 %copy-start.13 = (s32[1,32,2]{1,2,0:T(2,128)S(1)}, s32[1,32,2]{1,2,0:T(2,128)}, u32[]{:S(2)}) copy-start(s32[1,32,2]{1,2,0:T(2,128)} %param.19) | copy-start | bytes 772
  8.8 7.2 %copy-start.8 = (bf16[1,256,128]{2,1,0:T(8,128)(2,1)S(1)}, bf16[1,256,128]{2,1,0:T(8,128)(2,1)}, u32[]{:S(2)}) copy-start(bf16[1,256,128]{2,1,0:T(8,128)(2,1)} %param.13) | copy-start | bytes 196612
  8.8 7.2 %copy-start.9 = (bf16[1,256,128]{2,1,0:T(8,128)(2,1)S(1)}, bf16[1,256,128]{2,1,0:T(8,128)(2,1)}, u32[]{:S(2)}) copy-start(bf16[1,256,128]{2,1,0:T(8,128)(2,1)} %param.12) | copy-start | bytes 196612
  8.8 47.2 %all-to-all-start = ((bf16[8,16,6144]{2,1,0:T(8,128)(2,1)}), bf16[8,16,6144]{2,1,0:T(8,128)(2,1)S(1)}, u32[]{:S(2)}, u32[]{:S(2)}) async-start(bf16[8,16,6144]{2,1,0:T(8,128)(2,1)} %bitcast.101), calls=%async_computation | async-start | bytes 3145728 | tf_op jit(solution)/shard_map/all_to_all | solution.py:143
  16.1 4.8 %copy-start.10 = (f32[1,6,256]{2,0,1:T(1,128)S(1)}, f32[1,6,256]{2,0,1:T(1,128)}, u32[]{:S(2)}) copy-start(f32[1,6,256]{2,0,1:T(1,128)} %param.15) | copy-start | bytes 18436
  16.8 11.7 %collective-permute-start = (bf16[2,256,128]{2,1,0:T(8,128)(2,1)}, bf16[2,256,128]{2,1,0:T(8,128)(2,1)}, u32[]{:S(2)}, u32[]{:S(2)}) collective-permute-start(bf16[2,256,128]{2,1,0:T(8,128)(2,1)} %pad_maximum_fusion), channel_id=1, source_target_pairs={{0,32},{32,64},{64,96},{96,128},{128,160},{160,192},{192,224},{224... | collective-permute-start | bytes 393224 | tf_op jit(solution)/shard_map/ppermute | solution.py:16
  18.7 5.3 %copy-start.11 = (f32[1,6,256]{2,0,1:T(1,128)S(1)}, f32[1,6,256]{2,0,1:T(1,128)}, u32[]{:S(2)}) copy-start(f32[1,6,256]{2,0,1:T(1,128)} %param.16) | copy-start | bytes 18436
  59.6 2.2 %copy-start.2 = (f32[256,1536]{1,0:T(8,128)S(1)}, f32[256,1536]{1,0:T(8,128)}, u32[]{:S(2)}) copy-start(f32[256,1536]{1,0:T(8,128)} %fusion.4) | copy-start | bytes 4718596
  59.8 3.3 %copy-start.3 = (bf16[1,6,256,128]{3,2,1,0:T(8,128)(2,1)S(1)}, bf16[1,6,256,128]{3,2,1,0:T(8,128)(2,1)}, u32[]{:S(2)}) copy-start(bf16[1,6,256,128]{3,2,1,0:T(8,128)(2,1)} %copy.52) | copy-start | bytes 1179652
  59.8 18.5 %collective-permute-start.3 = (f32[4,4,4,48,128]{4,3,2,0,1:T(8,128)S(1)}, f32[4,4,4,48,128]{4,3,2,0,1:T(8,128)S(1)}, u32[]{:S(2)}, u32[]{:S(2)}) collective-permute-start(f32[4,4,4,48,128]{4,3,2,0,1:T(8,128)S(1)} %dynamic-slice_bitcast_fusion), channel_id=1, source_target_pairs={{0,32},{32,0},{1,33},{33,1},{2,34},{34,2},{3,35},{35,3},{4,36},{36... | collective-permute-start | bytes 4718600 | tf_op jit(solution)/shard_map/ppermute | solution.py:63
  64.5 49.5 %collective-permute-start.2 = (bf16[2,1,256,128]{3,2,1,0:T(8,128)(2,1)}, bf16[2,1,256,128]{3,2,1,0:T(8,128)(2,1)}, u32[]{:S(2)}, u32[]{:S(2)}) collective-permute-start(bf16[2,1,256,128]{3,2,1,0:T(8,128)(2,1)} %fusion.18), channel_id=1, source_target_pairs={{992,0},{0,32},{32,64},{64,96},{96,128},{128,160},{160,192},{192,2... | collective-permute-start | bytes 393224 | tf_op jit(solution)/shard_map/ppermute | solution.py:22
  66.9 8.6 %collective-permute-start.1 = (bf16[2,256,128]{2,1,0:T(8,128)(2,1)}, bf16[2,256,128]{2,1,0:T(8,128)(2,1)S(1)}, u32[]{:S(2)}, u32[]{:S(2)}) collective-permute-start(bf16[2,256,128]{2,1,0:T(8,128)(2,1)} %collective-permute-done), channel_id=1, source_target_pairs={{0,32},{32,64},{64,96},{96,128},{128,160},{160,192},{192,224},{224... | collective-permute-start | bytes 393224 | tf_op jit(solution)/shard_map/ppermute | solution.py:16
  75.5 2.8 %copy-start.7 = (bf16[2,256,128]{2,1,0:T(8,128)(2,1)}, bf16[2,256,128]{2,1,0:T(8,128)(2,1)S(1)}, u32[]{:S(2)}) copy-start(bf16[2,256,128]{2,1,0:T(8,128)(2,1)S(1)} %collective-permute-done.1) | copy-start | bytes 393220
  75.9 1.1 copy-start.1
  79.5 14.5 %all-to-all-start.1 = ((bf16[4,4,4,48,128]{4,3,2,1,0:T(8,128)(2,1)}), bf16[4,4,4,48,128]{4,3,2,1,0:T(8,128)(2,1)}, u32[]{:S(2)}, u32[]{:S(2)}) async-start(bf16[4,4,4,48,128]{4,3,2,1,0:T(8,128)(2,1)} %copy.62), calls=%async_computation.1 | async-start | bytes 1572864 | tf_op jit(solution)/shard_map/all_to_all | solution.py:64
  90.1 2.5 %copy-start.4 = (bf16[1,6,256,128]{3,2,1,0:T(8,128)(2,1)S(1)}, bf16[1,6,256,128]{3,2,1,0:T(8,128)(2,1)}, u32[]{:S(2)}) copy-start(bf16[1,6,256,128]{3,2,1,0:T(8,128)(2,1)} %copy.52) | copy-start | bytes 1179652
  90.1 2.5 %copy-start.5 = (bf16[256,1536]{1,0:T(8,128)(2,1)S(1)}, bf16[256,1536]{1,0:T(8,128)(2,1)}, u32[]{:S(2)}) copy-start(bf16[256,1536]{1,0:T(8,128)(2,1)} %fusion.7) | copy-start | bytes 2359300
  92.6 23.2 %copy-start.6 = (f32[128,256]{0,1:T(8,128)S(1)}, f32[128,256]{0,1:T(8,128)}, u32[]{:S(2)}) copy-start(f32[128,256]{0,1:T(8,128)} %bitcast_convert_fusion.1) | copy-start | bytes 393220
  96.0 33.7 %all-to-all-start.2 = ((bf16[16,48,128]{2,1,0:T(8,128)(2,1)}), bf16[16,48,128]{2,1,0:T(8,128)(2,1)S(1)}, u32[]{:S(2)}, u32[]{:S(2)}) async-start(bf16[16,48,128]{2,1,0:T(8,128)(2,1)} %bitcast.34), calls=%async_computation.2 | async-start | bytes 393216 | tf_op jit(solution)/shard_map/all_to_all | solution.py:66

commit v5 on v4

--- a/solution.py
+++ b/solution.py
@@ -141,6 +141,9 @@
     ).astype(jnp.bfloat16)
     outbound = jnp.dot(table, routed, preferred_element_type=jnp.float32).astype(jnp.bfloat16)
     incoming_block = lax.all_to_all(outbound, "exp", split_axis=0, concat_axis=0, tiled=True)
+    incoming_block, query_grad, key_grad, value_grad = lax.optimization_barrier(
+        (incoming_block, query_grad, key_grad, value_grad)
+    )
     saved = saved_pre[0, 0, 0].astype(jnp.float32)
     hidden_units = saved.shape[1] // 2
     gate = saved[:, :hidden_units]

time: 131 us -> 125 us (0.954)
  blocking collectives: 0 us -> 17 us
  waiting for transfers between devices: 41.4 us -> 30.7 us
  matrix products: 18.8 us -> 12.6 us
  starting transfers between devices: 38.9 us -> 35 us
  local copies, waits for them, and re-layouts: 21.4 us -> 17.8 us
    all_to_all x0 -> x1, blocking collectives: none -> 17 us  [staged_reduce_scatter(): pieces = lax.all_to_all(pieces.astype(jnp.bfloat16), 'xx', 0, 0, tiled=True)]
    all_to_all x1, waiting for transfers between devices: 25 us -> 9.15 us  [body(): lax.all_to_all(outbound, 'exp', split_axis=0, concat_axis=0, tiled=True)]
    all_to_all x1 -> x0, starting transfers between devices: 4.2 us -> none  [staged_reduce_scatter(): pieces = lax.all_to_all(pieces.astype(jnp.bfloat16), 'xx', 0, 0, tiled=True)]
    ppermute x1, waiting for transfers between devices: 0.01 us -> 3.27 us  [staged_reduce_scatter(): lax.ppermute(other, 'core', [(i, (i + 1) % core) for i in range(core)])]
    dot_general x2, matrix products: 4.76 us -> 2.45 us  [pair_grads(): jnp.einsum('kqu,kud->kqd', score_grad, key_part, preferred_element_type=j...]
    ppermute x2, waiting for transfers between devices: 3.41 us -> 5.14 us  [passed_along(): return lax.ppermute(value, axis, pairs)]
    all_to_all x1 -> x0, local copies, waits for them, and re-layouts: 1.58 us -> none  [body(): lax.all_to_all(outbound, 'exp', split_axis=0, concat_axis=0, tiled=True)]
    dot_general x1, matrix products: 2.03 us -> 0.61 us  [body(): jnp.einsum('rc,rf->cf', incoming_block, hidden_state, preferred_element_t...]
  transfers between devices with their start and end apart: 7 -> 6, of which waited for: 4 -> 4; matrix products, arithmetic and copies ran while one was open for 27% -> 27% of each run, Pallas kernels for 0% -> 0%
where the time goes in v5:
time: 125 us; the launch traced here: 124 us
  starting transfers between devices  35 us (28%)
  waiting for transfers between devices  30.7 us (25%)
  local copies, waits for them, and re-layouts  17.8 us (14%)
  blocking collectives  17 us (14%)
  matrix products  12.6 us (10%)
  other arithmetic  10 us (8%)
    all_to_all x1, starting transfers between devices, staged_reduce_scatter(): lax.all_to_all(pieces.astype(jnp.bfloat16), ('zl', 'dp'), 0, 0, tiled=True)  18.4 us
    all_to_all x1, blocking collectives, staged_reduce_scatter(): pieces = lax.all_to_all(pieces.astype(jnp.bfloat16), 'xx', 0, 0, tiled=True)  17 us
    all_to_all x1, waiting for transfers between devices, staged_reduce_scatter(): lax.all_to_all(pieces.astype(jnp.bfloat16), ('zl', 'dp'), 0, 0, tiled=True)  13.1 us
    all_to_all x1, waiting for transfers between devices, body(): lax.all_to_all(outbound, 'exp', split_axis=0, concat_axis=0, tiled=True)  9.15 us
    unnamed x30, local copies, waits for them, and re-layouts  8.16 us
    all_to_all x1, starting transfers between devices, body(): lax.all_to_all(outbound, 'exp', split_axis=0, concat_axis=0, tiled=True)  7.23 us
    ppermute x2, waiting for transfers between devices, passed_along(): return lax.ppermute(value, axis, pairs)  5.14 us
    mul x3, local copies, waits for them, and re-layouts, body(): router_prob[0][:, :, None] * tok_grad[0].astype(jnp.float32)[:, None, :]  4.53 us
  transfers between devices with their start and end apart: 6, of which 4 were waited for; matrix products, arithmetic and copies ran while one was open for 27% of the time, Pallas kernels for 0%

profile of v5, /device:TPU:64, one launch (start us, length us, event | category | flops | bytes accessed | tf_op | source)
XLA Modules:
  0.0 124.1 jit_solution(17873324849758115621)
XLA Ops:
  0.6 1.7 %pad_maximum_fusion = bf16[2,256,128]{2,1,0:T(8,128)(2,1)} fusion(bf16[1,256,128]{2,1,0:T(8,128)(2,1)} %param.13, bf16[1,256,128]{2,1,0:T(8,128)(2,1)} %param.12), kind=kLoop, calls=%fused_computation.40 | loop fusion | flops 65536 | bytes 262144 | tf_op jit(solution)/shard_map/stack | solution.py:96
  2.3 1.9 %collective-permute-start = (bf16[2,256,128]{2,1,0:T(8,128)(2,1)}, bf16[2,256,128]{2,1,0:T(8,128)(2,1)}, u32[]{:S(2)}, u32[]{:S(2)}) collective-permute-start(bf16[2,256,128]{2,1,0:T(8,128)(2,1)} %pad_maximum_fusion), channel_id=1, source_target_pairs={{0,32},{32,64},{64,96},{96,128},{128,160},{160,192},{192,224},{224... | collective-permute-start | bytes 393224 | tf_op jit(solution)/shard_map/ppermute | solution.py:16
  4.2 0.8 copy.46
  5.1 0.8 copy.45
  6.3 1.1 bitcast_convert_fusion
  7.4 2.0 %mul.159 = f32[32,2,6144]{2,1,0:T(2,128)} broadcast(f32[32,6144]{1,0:T(8,128)S(1)} %bitcast_convert_fusion), dimensions={0,2} | broadcast | bytes 2359296 | tf_op jit(solution)/shard_map/mul | solution.py:128
  9.4 2.4 %mul.160 = f32[64,6144]{1,0:T(8,128)S(1)} reshape(f32[32,2,6144]{2,1,0:T(2,128)} %mul.159) | data formatting | bytes 3145728 | tf_op jit(solution)/shard_map/mul | solution.py:128
  11.8 1.8 %convolution_convert_fusion = bf16[128,6144]{1,0:T(8,128)(2,1)} fusion(f32[64,6144]{1,0:T(8,128)S(1)} %mul.160, f32[64]{0:T(128)S(1)} %mul.157, s32[64]{0:T(128)S(1)} %multiply_add_fusion), kind=kOutput, calls=%fused_computation | convolution fusion | flops 102244352 | bytes 3146240 | tf_op jit(solution)/shard_map/dot_general | solution.py:142
  13.6 7.2 %all-to-all-start = ((bf16[8,16,6144]{2,1,0:T(8,128)(2,1)}), bf16[8,16,6144]{2,1,0:T(8,128)(2,1)S(1)}, u32[]{:S(2)}, u32[]{:S(2)}) async-start(bf16[8,16,6144]{2,1,0:T(8,128)(2,1)} %bitcast.97), calls=%async_computation | async-start | bytes 3145728 | tf_op jit(solution)/shard_map/all_to_all | solution.py:143
  21.0 0.7 copy.52
  21.7 1.2 copy.47
  22.9 0.9 copy.48
  23.8 1.9 %copy.49 = bf16[1,256,768]{1,2,0:T(8,128)(2,1)} copy(bf16[1,256,768]{2,1,0:T(8,128)(2,1)} %param.14) | data formatting | bytes 786432 | tf_op args[3]
  25.7 1.2 copy.50
  26.9 1.5 %bitcast_convert_fusion.1 = f32[128,256]{0,1:T(8,128)} fusion(bf16[1,1,1,128,256]{3,4,2,1,0:T(8,128)(2,1)} %copy.52), kind=kLoop, calls=%fused_computation.48 | loop fusion | flops 32768 | bytes 196608 | tf_op jit(solution)/shard_map/convert_element_type | solution.py:147
  28.4 1.4 %fusion.4 = f32[256,1536]{1,0:T(8,128)S(1)} fusion(bf16[1536,128]{1,0:T(8,128)(2,1)} %bitcast.93, f32[1536]{0:T(1024)S(1)} %sub.50, bf16[2,256,128]{2,1,0:T(8,128)(2,1)} %collective-permute-done), kind=kOutput, calls=%fused_computation.9 | convolution fusion | flops 101449728 | bytes 2037760 | tf_op jit(solution)/shard_map/kqd,kud->kqu/dot_general | solution.py:32
  29.8 1.3 %fusion.6 = bf16[256,1536]{1,0:T(8,128)(2,1)S(1)} fusion(f32[256,1536]{1,0:T(8,128)S(1)} %fusion.4, bf16[1536,128]{1,0:T(8,128)(2,1)S(1)} %bitcast.89, f32[1536]{0:T(1024)S(1)} %sub.53, bf16[2,256,128]{2,1,0:T(8,128)(2,1)} %collective-permute-done), kind=kOutput, calls=%fused_computation.11 | convolution fusion | flops 101842944 | bytes 2824192 | tf_op jit(solution)/shard_map/kqd,kud->kqu/dot_general | solution.py:37
  31.1 0.4 fusion.15
  31.5 0.4 convolution_bitcast_fusion.1
  31.8 0.7 fusion.19
  32.5 3.2 %collective-permute-start.2 = (bf16[2,1,256,128]{3,2,1,0:T(8,128)(2,1)}, bf16[2,1,256,128]{3,2,1,0:T(8,128)(2,1)}, u32[]{:S(2)}, u32[]{:S(2)}) collective-permute-start(bf16[2,1,256,128]{3,2,1,0:T(8,128)(2,1)} %fusion.19), channel_id=1, source_target_pairs={{992,0},{0,32},{32,64},{64,96},{96,128},{128,160},{160,192},{192,2... | collective-permute-start | bytes 393224 | tf_op jit(solution)/shard_map/ppermute | solution.py:22
  35.7 2.2 %collective-permute-start.1 = (bf16[2,256,128]{2,1,0:T(8,128)(2,1)}, bf16[2,256,128]{2,1,0:T(8,128)(2,1)S(1)}, u32[]{:S(2)}, u32[]{:S(2)}) collective-permute-start(bf16[2,256,128]{2,1,0:T(8,128)(2,1)} %collective-permute-done), channel_id=1, source_target_pairs={{0,32},{32,64},{64,96},{96,128},{128,160},{160,192},{192,224},{224... | collective-permute-start | bytes 393224 | tf_op jit(solution)/shard_map/ppermute | solution.py:16
  38.0 1.3 %convolution_multiply_fusion.3 = f32[1536,128]{1,0:T(8,128)S(1)} fusion(bf16[256,1536]{1,0:T(8,128)(2,1)S(1)} %fusion.6, f32[]{:T(128)S(6)} %mul.167, bf16[2,256,128]{2,1,0:T(8,128)(2,1)} %collective-permute-done), kind=kOutput, calls=%fused_computation.14 | convolution fusion | flops 100859904 | bytes 1638404 | tf_op jit(solution)/shard_map/kqu,kud->kqd/dot_general | solution.py:42
  39.2 5.1 %collective-permute-done.1 = bf16[2,256,128]{2,1,0:T(8,128)(2,1)S(1)} collective-permute-done((bf16[2,256,128]{2,1,0:T(8,128)(2,1)}, bf16[2,256,128]{2,1,0:T(8,128)(2,1)S(1)}, u32[]{:S(2)}, u32[]{:S(2)}) %collective-permute-start.1) | collective-permute-done | bytes 131104 | tf_op jit(solution)/shard_map/ppermute | solution.py:16
  44.4 0.4 fusion.5
  44.7 0.4 fusion.7
  45.1 1.0 copy-done.4
  46.1 1.2 fusion.9
  47.3 1.9 %copy.51 = bf16[1,6,256,128]{2,3,1,0:T(8,128)(2,1)} copy(bf16[1,6,256,128]{3,2,1,0:T(8,128)(2,1)} %bitcast.100) | data formatting | bytes 786432 | tf_op jit(solution)/shard_map/convert_element_type | solution.py:116
  49.2 1.9 %convolution_bitcast_fusion = f32[1,1,256,128]{3,2,1,0:T(8,128)S(1)} fusion(bf16[1536,128]{1,0:T(8,128)(2,1)S(1)} %bitcast.92, f32[256,1536]{1,0:T(8,128)} %copy-done.1), kind=kOutput, calls=%fused_computation.24 | convolution fusion | flops 101056512 | bytes 2097152 | tf_op jit(solution)/shard_map/kqu,kqd->kud/dot_general | solution.py:49
  51.1 0.4 fusion.14
  51.5 0.9 fusion.21
  52.4 0.7 slice_bitcast_fusion
  53.1 9.2 %all-to-all-done = bf16[8,16,6144]{2,1,0:T(8,128)(2,1)S(1)} async-done(((bf16[8,16,6144]{2,1,0:T(8,128)(2,1)}), bf16[8,16,6144]{2,1,0:T(8,128)(2,1)S(1)}, u32[]{:S(2)}, u32[]{:S(2)}) %all-to-all-start) | async-done | bytes 1572896 | tf_op jit(solution)/shard_map/all_to_all | solution.py:143
  62.2 0.6 fusion.24
  62.9 0.3 constant_dynamic-slice_fusion
  63.4 2.0 %collective-permute-start.3 = (f32[4,4,4,48,128]{4,3,2,1,0:T(8,128)S(1)}, f32[4,4,4,48,128]{4,3,2,1,0:T(8,128)S(1)}, u32[]{:S(2)}, u32[]{:S(2)}) collective-permute-start(f32[4,4,4,48,128]{4,3,2,1,0:T(8,128)S(1)} %bitcast.98), channel_id=1, source_target_pairs={{0,32},{32,0},{1,33},{33,1},{2,34},{34,2},{3,35},{35,3},{4,36},{36... | collective-permute-start | bytes 4718600 | tf_op jit(solution)/shard_map/ppermute | solution.py:63
  65.4 3.3 %collective-permute-done.3 = f32[4,4,4,48,128]{4,3,2,1,0:T(8,128)S(1)} collective-permute-done((f32[4,4,4,48,128]{4,3,2,1,0:T(8,128)S(1)}, f32[4,4,4,48,128]{4,3,2,1,0:T(8,128)S(1)}, u32[]{:S(2)}, u32[]{:S(2)}) %collective-permute-start.3) | collective-permute-done | bytes 1572896 | tf_op jit(solution)/shard_map/ppermute | solution.py:63
  68.7 0.2 fusion.11
  68.9 17.0 %all_to_all.22 = bf16[4,4,4,48,128]{4,3,2,1,0:T(8,128)(2,1)} all-to-all(bf16[4,4,4,48,128]{4,3,2,1,0:T(8,128)(2,1)S(1)} %fusion.11), channel_id=1, replica_groups=mesh['zl'=4,'xx'=4,'core'=2,'exp'=8,'dp'=4] {'xx'}, dimensions={0} | all-to-all | bytes 1572864 | tf_op jit(solution)/shard_map/all_to_all | solution.py:64
  85.9 2.0 %reduce_sum.31 = bf16[4,4,48,128]{3,2,1,0:T(8,128)(2,1)} reduce(bf16[4,4,4,48,128]{4,3,2,1,0:T(8,128)(2,1)} %all_to_all.22, bf16[]{:T(256)} %constant.50.clone.1), dimensions={0}, to_apply=%region_2.3 | reduce | flops 294912 | bytes 983042 | tf_op jit(solution)/shard_map/reduce_sum | solution.py:65
  87.9 18.4 %all-to-all-start.2 = ((bf16[16,48,128]{2,1,0:T(8,128)(2,1)}), bf16[16,48,128]{2,1,0:T(8,128)(2,1)}, u32[]{:S(2)}, u32[]{:S(2)}) async-start(bf16[16,48,128]{2,1,0:T(8,128)(2,1)} %bitcast.103), calls=%async_computation.2 | async-start | bytes 393216 | tf_op jit(solution)/shard_map/all_to_all | solution.py:66
  106.3 0.9 copy.55
  107.2 1.4 %fusion.27 = (bf16[1,1,1,128,128]{3,4,2,1,0:T(8,128)(2,1)S(1)}, bf16[1,1,1,128,128]{3,4,2,1,0:T(8,128)(2,1)S(1)}) fusion(f32[128,256]{0,1:T(8,128)} %bitcast_convert_fusion.1, bf16[128,6144]{1,0:T(8,128)(2,1)S(1)} %bitcast.88, bf16[1,128,6144]{2,1,0:T(8,128)(2,1)S(1)} %copy-done), kind=kOutput, calls=%fused_computation.61 | convolution fusion | flops 201539584 | bytes 3342336 | tf_op jit(solution)/shard_map/rd,fd->rf/dot_general | solution.py:154
  108.7 0.7 copy.56
  109.4 13.1 %all-to-all-done.2 = bf16[16,48,128]{2,1,0:T(8,128)(2,1)} async-done(((bf16[16,48,128]{2,1,0:T(8,128)(2,1)}), bf16[16,48,128]{2,1,0:T(8,128)(2,1)}, u32[]{:S(2)}, u32[]{:S(2)}) %all-to-all-start.2) | async-done | bytes 196640 | tf_op jit(solution)/shard_map/all_to_all | solution.py:66
  122.5 1.0 convert_reduce_fusion
  123.5 0.6 multiply_bitcast_fusion
  (35 shorter events, 0.8 us)
Async XLA Ops:
  0.6 106.6 %copy-start = (bf16[1,128,6144]{2,1,0:T(8,128)(2,1)S(1)}, bf16[1,128,6144]{2,1,0:T(8,128)(2,1)}, u32[]{:S(2)}) copy-start(bf16[1,128,6144]{2,1,0:T(8,128)(2,1)} %param.21) | copy-start | bytes 4718596
  2.3 26.1 %collective-permute-start = (bf16[2,256,128]{2,1,0:T(8,128)(2,1)}, bf16[2,256,128]{2,1,0:T(8,128)(2,1)}, u32[]{:S(2)}, u32[]{:S(2)}) collective-permute-start(bf16[2,256,128]{2,1,0:T(8,128)(2,1)} %pad_maximum_fusion), channel_id=1, source_target_pairs={{0,32},{32,64},{64,96},{96,128},{128,160},{160,192},{192,224},{224... | collective-permute-start | bytes 393224 | tf_op jit(solution)/shard_map/ppermute | solution.py:16
  13.6 7.2 %copy-start.9 = (f32[1,6,256]{2,0,1:T(1,128)S(1)}, f32[1,6,256]{2,0,1:T(1,128)}, u32[]{:S(2)}) copy-start(f32[1,6,256]{2,0,1:T(1,128)} %param.15) | copy-start | bytes 18436
  13.6 7.3 %copy-start.10 = (f32[1,6,256]{2,0,1:T(1,128)S(1)}, f32[1,6,256]{2,0,1:T(1,128)}, u32[]{:S(2)}) copy-start(f32[1,6,256]{2,0,1:T(1,128)} %param.16) | copy-start | bytes 18436
  13.6 7.3 %copy-start.8 = (bf16[1,1,1,128,256]{4,3,2,1,0:T(8,128)(2,1)S(1)}, bf16[1,1,1,128,256]{4,3,2,1,0:T(8,128)(2,1)}, u32[]{:S(2)}) copy-start(bf16[1,1,1,128,256]{4,3,2,1,0:T(8,128)(2,1)} %param.20) | copy-start | bytes 196612
  13.6 48.6 %all-to-all-start = ((bf16[8,16,6144]{2,1,0:T(8,128)(2,1)}), bf16[8,16,6144]{2,1,0:T(8,128)(2,1)S(1)}, u32[]{:S(2)}, u32[]{:S(2)}) async-start(bf16[8,16,6144]{2,1,0:T(8,128)(2,1)} %bitcast.97), calls=%async_computation | async-start | bytes 3145728 | tf_op jit(solution)/shard_map/all_to_all | solution.py:143
  29.8 1.3 %copy-start.2 = (bf16[1,6,256,128]{3,2,1,0:T(8,128)(2,1)S(1)}, bf16[1,6,256,128]{3,2,1,0:T(8,128)(2,1)}, u32[]{:S(2)}) copy-start(bf16[1,6,256,128]{3,2,1,0:T(8,128)(2,1)} %copy.48) | copy-start | bytes 1179652
  32.5 19.0 %collective-permute-start.2 = (bf16[2,1,256,128]{3,2,1,0:T(8,128)(2,1)}, bf16[2,1,256,128]{3,2,1,0:T(8,128)(2,1)}, u32[]{:S(2)}, u32[]{:S(2)}) collective-permute-start(bf16[2,1,256,128]{3,2,1,0:T(8,128)(2,1)} %fusion.19), channel_id=1, source_target_pairs={{992,0},{0,32},{32,64},{64,96},{96,128},{128,160},{160,192},{192,2... | collective-permute-start | bytes 393224 | tf_op jit(solution)/shard_map/ppermute | solution.py:22
  35.7 8.6 %collective-permute-start.1 = (bf16[2,256,128]{2,1,0:T(8,128)(2,1)}, bf16[2,256,128]{2,1,0:T(8,128)(2,1)S(1)}, u32[]{:S(2)}, u32[]{:S(2)}) collective-permute-start(bf16[2,256,128]{2,1,0:T(8,128)(2,1)} %collective-permute-done), channel_id=1, source_target_pairs={{0,32},{32,64},{64,96},{96,128},{128,160},{160,192},{192,224},{224... | collective-permute-start | bytes 393224 | tf_op jit(solution)/shard_map/ppermute | solution.py:16
  44.7 2.6 %copy-start.1 = (f32[256,1536]{1,0:T(8,128)}, f32[256,1536]{1,0:T(8,128)S(1)}, u32[]{:S(2)}) copy-start(f32[256,1536]{1,0:T(8,128)S(1)} %fusion.5) | copy-start | bytes 4718596
  45.1 1.0 copy-start.4
  49.2 1.9 %copy-start.3 = (bf16[1,6,256,128]{3,2,1,0:T(8,128)(2,1)S(1)}, bf16[1,6,256,128]{3,2,1,0:T(8,128)(2,1)}, u32[]{:S(2)}) copy-start(bf16[1,6,256,128]{3,2,1,0:T(8,128)(2,1)} %copy.48) | copy-start | bytes 1179652
  49.2 1.9 %copy-start.5 = (bf16[256,1536]{1,0:T(8,128)(2,1)S(1)}, bf16[256,1536]{1,0:T(8,128)(2,1)}, u32[]{:S(2)}) copy-start(bf16[256,1536]{1,0:T(8,128)(2,1)} %copy-done.4) | copy-start | bytes 2359300
  51.1 11.1 %copy-start.7 = (f32[128,256]{0,1:T(8,128)S(1)}, f32[128,256]{0,1:T(8,128)}, u32[]{:S(2)}) copy-start(f32[128,256]{0,1:T(8,128)} %bitcast_convert_fusion.1) | copy-start | bytes 393220
  63.4 5.3 %collective-permute-start.3 = (f32[4,4,4,48,128]{4,3,2,1,0:T(8,128)S(1)}, f32[4,4,4,48,128]{4,3,2,1,0:T(8,128)S(1)}, u32[]{:S(2)}, u32[]{:S(2)}) collective-permute-start(f32[4,4,4,48,128]{4,3,2,1,0:T(8,128)S(1)} %bitcast.98), channel_id=1, source_target_pairs={{0,32},{32,0},{1,33},{33,1},{2,34},{34,2},{3,35},{35,3},{4,36},{36... | collective-permute-start | bytes 4718600 | tf_op jit(solution)/shard_map/ppermute | solution.py:63
  68.9 37.4 %copy-start.6 = (bf16[1,6,256,128]{2,3,1,0:T(8,128)(2,1)S(1)}, bf16[1,6,256,128]{2,3,1,0:T(8,128)(2,1)}, u32[]{:S(2)}) copy-start(bf16[1,6,256,128]{2,3,1,0:T(8,128)(2,1)} %copy.51) | copy-start | bytes 1179652
  87.9 34.7 %all-to-all-start.2 = ((bf16[16,48,128]{2,1,0:T(8,128)(2,1)}), bf16[16,48,128]{2,1,0:T(8,128)(2,1)}, u32[]{:S(2)}, u32[]{:S(2)}) async-start(bf16[16,48,128]{2,1,0:T(8,128)(2,1)} %bitcast.103), calls=%async_computation.2 | async-start | bytes 393216 | tf_op jit(solution)/shard_map/all_to_all | solution.py:66

commit v6 on v5

--- a/solution.py
+++ b/solution.py
@@ -60,7 +60,10 @@
     here = lax.axis_index("core")
     mine = lax.dynamic_index_in_dim(pieces, here, 0, keepdims=False)
     other = lax.dynamic_index_in_dim(pieces, 1 - here, 0, keepdims=False)
-    pieces = mine + lax.ppermute(other, "core", [(i, (i + 1) % core) for i in range(core)])
+    swapped = lax.ppermute(
+        other.astype(jnp.bfloat16), "core", [(i, (i + 1) % core) for i in range(core)]
+    )
+    pieces = mine + swapped.astype(jnp.float32)
     pieces = lax.all_to_all(pieces.astype(jnp.bfloat16), "xx", 0, 0, tiled=True)
     pieces = pieces.astype(jnp.float32).sum(0).reshape(zl * dp, block, width)
     pieces = lax.all_to_all(pieces.astype(jnp.bfloat16), ("zl", "dp"), 0, 0, tiled=True)

time: 125 us -> 128 us (1.024)
  local copies, waits for them, and re-layouts: 17.8 us -> 20.1 us
  other arithmetic: 10 us -> 11.7 us
    convert_element_type x1, other arithmetic: 0.21 us -> 1.84 us  [staged_reduce_scatter(): pieces = lax.all_to_all(pieces.astype(jnp.bfloat16), 'xx', 0, 0, tiled=True)]
    unnamed x30 -> x31, local copies, waits for them, and re-layouts: 8.16 us -> 9.66 us
  transfers between devices with their start and end apart: 6 -> 6, of which waited for: 4 -> 4; matrix products, arithmetic and copies ran while one was open for 27% -> 26% of each run, Pallas kernels for 0% -> 0%
where the time goes in v6:
time: 128 us; the launch traced here: 127 us
  starting transfers between devices  35 us (27%)
  waiting for transfers between devices  29.9 us (23%)
  local copies, waits for them, and re-layouts  20.1 us (16%)
  blocking collectives  17 us (13%)
  matrix products  12.6 us (10%)
  other arithmetic  11.7 us (9%)
    all_to_all x1, starting transfers between devices, staged_reduce_scatter(): lax.all_to_all(pieces.astype(jnp.bfloat16), ('zl', 'dp'), 0, 0, tiled=True)  18.4 us
    all_to_all x1, blocking collectives, staged_reduce_scatter(): pieces = lax.all_to_all(pieces.astype(jnp.bfloat16), 'xx', 0, 0, tiled=True)  17 us
    all_to_all x1, waiting for transfers between devices, staged_reduce_scatter(): lax.all_to_all(pieces.astype(jnp.bfloat16), ('zl', 'dp'), 0, 0, tiled=True)  13.1 us
    unnamed x31, local copies, waits for them, and re-layouts  9.66 us
    all_to_all x1, waiting for transfers between devices, body(): lax.all_to_all(outbound, 'exp', split_axis=0, concat_axis=0, tiled=True)  9.12 us
    all_to_all x1, starting transfers between devices, body(): lax.all_to_all(outbound, 'exp', split_axis=0, concat_axis=0, tiled=True)  7.23 us
    ppermute x2, waiting for transfers between devices, passed_along(): return lax.ppermute(value, axis, pairs)  5.13 us
    mul x3, local copies, waits for them, and re-layouts, body(): router_prob[0][:, :, None] * tok_grad[0].astype(jnp.float32)[:, None, :]  4.53 us
  transfers between devices with their start and end apart: 6, of which 4 were waited for; matrix products, arithmetic and copies ran while one was open for 26% of the time, Pallas kernels for 0%

profile of v6, /device:TPU:64, one launch (start us, length us, event | category | flops | bytes accessed | tf_op | source)
XLA Modules:
  0.0 127.1 jit_solution(18024273153904394998)
XLA Ops:
  0.6 1.7 %pad_maximum_fusion = bf16[2,256,128]{2,1,0:T(8,128)(2,1)} fusion(bf16[1,256,128]{2,1,0:T(8,128)(2,1)} %param.13, bf16[1,256,128]{2,1,0:T(8,128)(2,1)} %param.12), kind=kLoop, calls=%fused_computation.41 | loop fusion | flops 65536 | bytes 262144 | tf_op jit(solution)/shard_map/stack | solution.py:99
  2.3 1.9 %collective-permute-start = (bf16[2,256,128]{2,1,0:T(8,128)(2,1)}, bf16[2,256,128]{2,1,0:T(8,128)(2,1)}, u32[]{:S(2)}, u32[]{:S(2)}) collective-permute-start(bf16[2,256,128]{2,1,0:T(8,128)(2,1)} %pad_maximum_fusion), channel_id=1, source_target_pairs={{0,32},{32,64},{64,96},{96,128},{128,160},{160,192},{192,224},{224... | collective-permute-start | bytes 393224 | tf_op jit(solution)/shard_map/ppermute | solution.py:16
  4.2 0.8 copy.46
  5.1 0.8 copy.45
  6.3 1.1 bitcast_convert_fusion
  7.4 2.0 %mul.159 = f32[32,2,6144]{2,1,0:T(2,128)} broadcast(f32[32,6144]{1,0:T(8,128)S(1)} %bitcast_convert_fusion), dimensions={0,2} | broadcast | bytes 2359296 | tf_op jit(solution)/shard_map/mul | solution.py:131
  9.4 2.4 %mul.160 = f32[64,6144]{1,0:T(8,128)S(1)} reshape(f32[32,2,6144]{2,1,0:T(2,128)} %mul.159) | data formatting | bytes 3145728 | tf_op jit(solution)/shard_map/mul | solution.py:131
  11.8 1.8 %convolution_convert_fusion = bf16[128,6144]{1,0:T(8,128)(2,1)} fusion(f32[64,6144]{1,0:T(8,128)S(1)} %mul.160, f32[64]{0:T(128)S(1)} %mul.157, s32[64]{0:T(128)S(1)} %multiply_add_fusion), kind=kOutput, calls=%fused_computation | convolution fusion | flops 102244352 | bytes 3146240 | tf_op jit(solution)/shard_map/dot_general | solution.py:145
  13.6 7.2 %all-to-all-start = ((bf16[8,16,6144]{2,1,0:T(8,128)(2,1)}), bf16[8,16,6144]{2,1,0:T(8,128)(2,1)S(1)}, u32[]{:S(2)}, u32[]{:S(2)}) async-start(bf16[8,16,6144]{2,1,0:T(8,128)(2,1)} %bitcast.97), calls=%async_computation | async-start | bytes 3145728 | tf_op jit(solution)/shard_map/all_to_all | solution.py:146
  21.0 0.7 copy.52
  21.7 1.2 copy.47
  22.9 0.9 copy.48
  23.8 1.9 %copy.49 = bf16[1,256,768]{1,2,0:T(8,128)(2,1)} copy(bf16[1,256,768]{2,1,0:T(8,128)(2,1)} %param.14) | data formatting | bytes 786432 | tf_op args[3]
  25.7 1.2 copy.50
  26.9 1.5 %bitcast_convert_fusion.1 = f32[128,256]{0,1:T(8,128)} fusion(bf16[1,1,1,128,256]{3,4,2,1,0:T(8,128)(2,1)} %copy.52), kind=kLoop, calls=%fused_computation.49 | loop fusion | flops 32768 | bytes 196608 | tf_op jit(solution)/shard_map/convert_element_type | solution.py:150
  28.4 1.4 %fusion.4 = f32[256,1536]{1,0:T(8,128)S(1)} fusion(bf16[1536,128]{1,0:T(8,128)(2,1)} %bitcast.93, f32[1536]{0:T(1024)S(1)} %sub.50, bf16[2,256,128]{2,1,0:T(8,128)(2,1)} %collective-permute-done), kind=kOutput, calls=%fused_computation.9 | convolution fusion | flops 101449728 | bytes 2037760 | tf_op jit(solution)/shard_map/kqd,kud->kqu/dot_general | solution.py:32
  29.9 1.3 fusion.6
  31.2 0.4 fusion.15
  31.5 0.4 convolution_bitcast_fusion.1
  31.9 0.7 fusion.20
  32.5 3.2 %collective-permute-start.2 = (bf16[2,1,256,128]{3,2,1,0:T(8,128)(2,1)}, bf16[2,1,256,128]{3,2,1,0:T(8,128)(2,1)}, u32[]{:S(2)}, u32[]{:S(2)}) collective-permute-start(bf16[2,1,256,128]{3,2,1,0:T(8,128)(2,1)} %fusion.20), channel_id=1, source_target_pairs={{992,0},{0,32},{32,64},{64,96},{96,128},{128,160},{160,192},{192,2... | collective-permute-start | bytes 393224 | tf_op jit(solution)/shard_map/ppermute | solution.py:22
  35.8 2.2 %collective-permute-start.1 = (bf16[2,256,128]{2,1,0:T(8,128)(2,1)}, bf16[2,256,128]{2,1,0:T(8,128)(2,1)S(1)}, u32[]{:S(2)}, u32[]{:S(2)}) collective-permute-start(bf16[2,256,128]{2,1,0:T(8,128)(2,1)} %collective-permute-done), channel_id=1, source_target_pairs={{0,32},{32,64},{64,96},{96,128},{128,160},{160,192},{192,224},{224... | collective-permute-start | bytes 393224 | tf_op jit(solution)/shard_map/ppermute | solution.py:16
  38.0 1.3 convolution_multiply_fusion.3
  39.2 5.1 %collective-permute-done.1 = bf16[2,256,128]{2,1,0:T(8,128)(2,1)S(1)} collective-permute-done((bf16[2,256,128]{2,1,0:T(8,128)(2,1)}, bf16[2,256,128]{2,1,0:T(8,128)(2,1)S(1)}, u32[]{:S(2)}, u32[]{:S(2)}) %collective-permute-start.1) | collective-permute-done | bytes 131104 | tf_op jit(solution)/shard_map/ppermute | solution.py:16
  44.4 0.4 fusion.5
  44.8 0.4 fusion.7
  45.2 1.0 copy-done.5
  46.1 1.2 fusion.9
  47.3 1.9 %copy.51 = bf16[1,6,256,128]{2,3,1,0:T(8,128)(2,1)} copy(bf16[1,6,256,128]{3,2,1,0:T(8,128)(2,1)} %bitcast.99) | data formatting | bytes 786432 | tf_op jit(solution)/shard_map/convert_element_type | solution.py:119
  49.3 1.9 %convolution_bitcast_fusion = f32[1,1,256,128]{3,2,1,0:T(8,128)S(1)} fusion(bf16[1536,128]{1,0:T(8,128)(2,1)S(1)} %bitcast.92, f32[256,1536]{1,0:T(8,128)} %copy-done.2), kind=kOutput, calls=%fused_computation.24 | convolution fusion | flops 101056512 | bytes 2097152 | tf_op jit(solution)/shard_map/kqu,kqd->kud/dot_general | solution.py:49
  51.5 0.9 fusion.22
  52.5 0.7 slice_bitcast_fusion
  53.1 9.1 %all-to-all-done = bf16[8,16,6144]{2,1,0:T(8,128)(2,1)S(1)} async-done(((bf16[8,16,6144]{2,1,0:T(8,128)(2,1)}), bf16[8,16,6144]{2,1,0:T(8,128)(2,1)S(1)}, u32[]{:S(2)}, u32[]{:S(2)}) %all-to-all-start) | async-done | bytes 1572896 | tf_op jit(solution)/shard_map/all_to_all | solution.py:146
  62.2 0.6 fusion.25
  62.9 1.6 %copy-done.1 = f32[6144,128]{1,0:T(8,128)} copy-done((f32[6144,128]{1,0:T(8,128)}, f32[6144,128]{1,0:T(8,128)S(1)}, u32[]{:S(2)}) %copy-start.1) | copy-done | bytes 3145752
  64.5 1.0 fusion.16
  65.5 2.0 %collective-permute-start.3 = (bf16[4,4,4,48,128]{4,3,2,1,0:T(8,128)(2,1)}, bf16[4,4,4,48,128]{4,3,2,1,0:T(8,128)(2,1)}, u32[]{:S(2)}, u32[]{:S(2)}) collective-permute-start(bf16[4,4,4,48,128]{4,3,2,1,0:T(8,128)(2,1)} %fusion.16), channel_id=1, source_target_pairs={{0,32},{32,0},{1,33},{33,1},{2,34},{34,2},{3,35},{35,3},{4,36},{36... | collective-permute-start | bytes 2359304 | tf_op jit(solution)/shard_map/ppermute | solution.py:63
  67.6 2.5 %collective-permute-done.3 = bf16[4,4,4,48,128]{4,3,2,1,0:T(8,128)(2,1)} collective-permute-done((bf16[4,4,4,48,128]{4,3,2,1,0:T(8,128)(2,1)}, bf16[4,4,4,48,128]{4,3,2,1,0:T(8,128)(2,1)}, u32[]{:S(2)}, u32[]{:S(2)}) %collective-permute-start.3) | collective-permute-done | bytes 786464 | tf_op jit(solution)/shard_map/ppermute | solution.py:63
  70.0 1.8 %fusion.11 = bf16[4,4,4,48,128]{4,3,2,1,0:T(8,128)(2,1)S(1)} fusion(bf16[4,4,4,48,128]{4,3,2,1,0:T(8,128)(2,1)} %collective-permute-done.3, f32[4,4,2,4,48,128]{5,4,3,2,1,0:T(8,128)} %bitcast.88, s32[]{:T(128)S(6)} %select_n.7), kind=kLoop, calls=%fused_computation.20 | loop fusion | flops 1179648 | bytes 3145732 | tf_op jit(solution)/shard_map/convert_element_type | solution.py:67
  71.9 17.0 %all_to_all.22 = bf16[4,4,4,48,128]{4,3,2,1,0:T(8,128)(2,1)} all-to-all(bf16[4,4,4,48,128]{4,3,2,1,0:T(8,128)(2,1)S(1)} %fusion.11), channel_id=1, replica_groups=mesh['zl'=4,'xx'=4,'core'=2,'exp'=8,'dp'=4] {'xx'}, dimensions={0} | all-to-all | bytes 1572864 | tf_op jit(solution)/shard_map/all_to_all | solution.py:67
  88.9 2.0 %reduce_sum.31 = bf16[4,4,48,128]{3,2,1,0:T(8,128)(2,1)} reduce(bf16[4,4,4,48,128]{4,3,2,1,0:T(8,128)(2,1)} %all_to_all.22, bf16[]{:T(256)} %constant.50.clone.1), dimensions={0}, to_apply=%region_2.3 | reduce | flops 294912 | bytes 983042 | tf_op jit(solution)/shard_map/reduce_sum | solution.py:68
  90.9 18.4 %all-to-all-start.2 = ((bf16[16,48,128]{2,1,0:T(8,128)(2,1)}), bf16[16,48,128]{2,1,0:T(8,128)(2,1)}, u32[]{:S(2)}, u32[]{:S(2)}) async-start(bf16[16,48,128]{2,1,0:T(8,128)(2,1)} %bitcast.102), calls=%async_computation.2 | async-start | bytes 393216 | tf_op jit(solution)/shard_map/all_to_all | solution.py:69
  109.3 0.9 copy.55
  110.2 1.4 %fusion.28 = (bf16[1,1,1,128,128]{3,4,2,1,0:T(8,128)(2,1)S(1)}, bf16[1,1,1,128,128]{3,4,2,1,0:T(8,128)(2,1)S(1)}) fusion(f32[128,256]{0,1:T(8,128)} %bitcast_convert_fusion.1, bf16[128,6144]{1,0:T(8,128)(2,1)S(1)} %bitcast.86, bf16[1,128,6144]{2,1,0:T(8,128)(2,1)S(1)} %copy-done), kind=kOutput, calls=%fused_computation.62 | convolution fusion | flops 201539584 | bytes 3342336 | tf_op jit(solution)/shard_map/rd,fd->rf/dot_general | solution.py:157
  111.7 0.7 copy.56
  112.4 13.1 %all-to-all-done.2 = bf16[16,48,128]{2,1,0:T(8,128)(2,1)} async-done(((bf16[16,48,128]{2,1,0:T(8,128)(2,1)}), bf16[16,48,128]{2,1,0:T(8,128)(2,1)}, u32[]{:S(2)}, u32[]{:S(2)}) %all-to-all-start.2) | async-done | bytes 196640 | tf_op jit(solution)/shard_map/all_to_all | solution.py:69
  125.6 1.0 convert_reduce_fusion
  126.5 0.6 multiply_bitcast_fusion
  (36 shorter events, 1.0 us)
Async XLA Ops:
  0.6 109.6 %copy-start = (bf16[1,128,6144]{2,1,0:T(8,128)(2,1)S(1)}, bf16[1,128,6144]{2,1,0:T(8,128)(2,1)}, u32[]{:S(2)}) copy-start(bf16[1,128,6144]{2,1,0:T(8,128)(2,1)} %param.21) | copy-start | bytes 4718596
  2.3 26.1 %collective-permute-start = (bf16[2,256,128]{2,1,0:T(8,128)(2,1)}, bf16[2,256,128]{2,1,0:T(8,128)(2,1)}, u32[]{:S(2)}, u32[]{:S(2)}) collective-permute-start(bf16[2,256,128]{2,1,0:T(8,128)(2,1)} %pad_maximum_fusion), channel_id=1, source_target_pairs={{0,32},{32,64},{64,96},{96,128},{128,160},{160,192},{192,224},{224... | collective-permute-start | bytes 393224 | tf_op jit(solution)/shard_map/ppermute | solution.py:16
  13.6 7.2 %copy-start.10 = (f32[1,6,256]{2,0,1:T(1,128)S(1)}, f32[1,6,256]{2,0,1:T(1,128)}, u32[]{:S(2)}) copy-start(f32[1,6,256]{2,0,1:T(1,128)} %param.15) | copy-start | bytes 18436
  13.6 7.3 %copy-start.11 = (f32[1,6,256]{2,0,1:T(1,128)S(1)}, f32[1,6,256]{2,0,1:T(1,128)}, u32[]{:S(2)}) copy-start(f32[1,6,256]{2,0,1:T(1,128)} %param.16) | copy-start | bytes 18436
  13.6 7.3 %copy-start.9 = (bf16[1,1,1,128,256]{4,3,2,1,0:T(8,128)(2,1)S(1)}, bf16[1,1,1,128,256]{4,3,2,1,0:T(8,128)(2,1)}, u32[]{:S(2)}) copy-start(bf16[1,1,1,128,256]{4,3,2,1,0:T(8,128)(2,1)} %param.20) | copy-start | bytes 196612
  13.6 48.6 %all-to-all-start = ((bf16[8,16,6144]{2,1,0:T(8,128)(2,1)}), bf16[8,16,6144]{2,1,0:T(8,128)(2,1)S(1)}, u32[]{:S(2)}, u32[]{:S(2)}) async-start(bf16[8,16,6144]{2,1,0:T(8,128)(2,1)} %bitcast.97), calls=%async_computation | async-start | bytes 3145728 | tf_op jit(solution)/shard_map/all_to_all | solution.py:146
  29.9 1.3 %copy-start.3 = (bf16[1,6,256,128]{3,2,1,0:T(8,128)(2,1)S(1)}, bf16[1,6,256,128]{3,2,1,0:T(8,128)(2,1)}, u32[]{:S(2)}) copy-start(bf16[1,6,256,128]{3,2,1,0:T(8,128)(2,1)} %copy.48) | copy-start | bytes 1179652
  32.5 19.0 %collective-permute-start.2 = (bf16[2,1,256,128]{3,2,1,0:T(8,128)(2,1)}, bf16[2,1,256,128]{3,2,1,0:T(8,128)(2,1)}, u32[]{:S(2)}, u32[]{:S(2)}) collective-permute-start(bf16[2,1,256,128]{3,2,1,0:T(8,128)(2,1)} %fusion.20), channel_id=1, source_target_pairs={{992,0},{0,32},{32,64},{64,96},{96,128},{128,160},{160,192},{192,2... | collective-permute-start | bytes 393224 | tf_op jit(solution)/shard_map/ppermute | solution.py:22
  35.8 8.6 %collective-permute-start.1 = (bf16[2,256,128]{2,1,0:T(8,128)(2,1)}, bf16[2,256,128]{2,1,0:T(8,128)(2,1)S(1)}, u32[]{:S(2)}, u32[]{:S(2)}) collective-permute-start(bf16[2,256,128]{2,1,0:T(8,128)(2,1)} %collective-permute-done), channel_id=1, source_target_pairs={{0,32},{32,64},{64,96},{96,128},{128,160},{160,192},{192,224},{224... | collective-permute-start | bytes 393224 | tf_op jit(solution)/shard_map/ppermute | solution.py:16
  44.8 2.5 %copy-start.2 = (f32[256,1536]{1,0:T(8,128)}, f32[256,1536]{1,0:T(8,128)S(1)}, u32[]{:S(2)}) copy-start(f32[256,1536]{1,0:T(8,128)S(1)} %fusion.5) | copy-start | bytes 4718596
  45.2 1.0 copy-start.5
  49.2 1.9 %copy-start.4 = (bf16[1,6,256,128]{3,2,1,0:T(8,128)(2,1)S(1)}, bf16[1,6,256,128]{3,2,1,0:T(8,128)(2,1)}, u32[]{:S(2)}) copy-start(bf16[1,6,256,128]{3,2,1,0:T(8,128)(2,1)} %copy.48) | copy-start | bytes 1179652
  49.3 1.9 %copy-start.6 = (bf16[256,1536]{1,0:T(8,128)(2,1)S(1)}, bf16[256,1536]{1,0:T(8,128)(2,1)}, u32[]{:S(2)}) copy-start(bf16[256,1536]{1,0:T(8,128)(2,1)} %copy-done.5) | copy-start | bytes 2359300
  51.1 11.1 %copy-start.8 = (f32[128,256]{0,1:T(8,128)S(1)}, f32[128,256]{0,1:T(8,128)}, u32[]{:S(2)}) copy-start(f32[128,256]{0,1:T(8,128)} %bitcast_convert_fusion.1) | copy-start | bytes 393220
  62.9 1.6 %copy-start.1 = (f32[6144,128]{1,0:T(8,128)}, f32[6144,128]{1,0:T(8,128)S(1)}, u32[]{:S(2)}) copy-start(f32[6144,128]{1,0:T(8,128)S(1)} %fusion.25) | copy-start | bytes 9437188
  65.5 4.5 %collective-permute-start.3 = (bf16[4,4,4,48,128]{4,3,2,1,0:T(8,128)(2,1)}, bf16[4,4,4,48,128]{4,3,2,1,0:T(8,128)(2,1)}, u32[]{:S(2)}, u32[]{:S(2)}) collective-permute-start(bf16[4,4,4,48,128]{4,3,2,1,0:T(8,128)(2,1)} %fusion.16), channel_id=1, source_target_pairs={{0,32},{32,0},{1,33},{33,1},{2,34},{34,2},{3,35},{35,3},{4,36},{36... | collective-permute-start | bytes 2359304 | tf_op jit(solution)/shard_map/ppermute | solution.py:63
  71.9 37.4 %copy-start.7 = (bf16[1,6,256,128]{2,3,1,0:T(8,128)(2,1)S(1)}, bf16[1,6,256,128]{2,3,1,0:T(8,128)(2,1)}, u32[]{:S(2)}) copy-start(bf16[1,6,256,128]{2,3,1,0:T(8,128)(2,1)} %copy.51) | copy-start | bytes 1179652
  90.9 34.7 %all-to-all-start.2 = ((bf16[16,48,128]{2,1,0:T(8,128)(2,1)}), bf16[16,48,128]{2,1,0:T(8,128)(2,1)}, u32[]{:S(2)}, u32[]{:S(2)}) async-start(bf16[16,48,128]{2,1,0:T(8,128)(2,1)} %bitcast.102), calls=%async_computation.2 | async-start | bytes 393216 | tf_op jit(solution)/shard_map/all_to_all | solution.py:69

commit v7 on v5

--- a/solution.py
+++ b/solution.py
@@ -125,10 +125,6 @@
     capacity = saved_pre.shape[3] // expert_count
     model_width = tok_grad.shape[2]
     pair_count = tok_grad.shape[1] * 2
-    routed = (router_prob[0][:, :, None] * tok_grad[0].astype(jnp.float32)[:, None, :]).astype(
-        jnp.bfloat16
-    )
-    routed = routed.reshape(pair_count, model_width)
     flat_ids = expert_ids[0].reshape(pair_count)
     matches = (flat_ids[:, None] == jnp.arange(expert_count, dtype=jnp.int32)[None, :]).astype(
         jnp.int32
@@ -136,10 +132,13 @@
     earlier = jnp.cumsum(matches, axis=0) - matches
     place = jnp.sum(earlier * matches, axis=1)
     slot_index = flat_ids * capacity + place
-    table = (
-        jnp.arange(expert_count * capacity, dtype=jnp.int32)[:, None] == slot_index[None, :]
-    ).astype(jnp.bfloat16)
-    outbound = jnp.dot(table, routed, preferred_element_type=jnp.float32).astype(jnp.bfloat16)
+    hit = jnp.arange(expert_count * capacity, dtype=jnp.int32)[:, None] == slot_index[None, :]
+    token_table = hit.reshape(expert_count * capacity, pair_count // 2, 2).any(axis=2)
+    slot_prob = jnp.sum(jnp.where(hit, router_prob[0].reshape(pair_count)[None, :], 0.0), axis=1)
+    picked = jnp.dot(
+        token_table.astype(jnp.bfloat16), tok_grad[0], preferred_element_type=jnp.float32
+    )
+    outbound = (slot_prob[:, None] * picked).astype(jnp.bfloat16)
     incoming_block = lax.all_to_all(outbound, "exp", split_axis=0, concat_axis=0, tiled=True)
     incoming_block, query_grad, key_grad, value_grad = lax.optimization_barrier(
         (incoming_block, query_grad, key_grad, value_grad)

time: 125 us -> 122 us (0.976)
  local copies, waits for them, and re-layouts: 17.8 us -> 13.6 us
    mul x3 -> x0, local copies, waits for them, and re-layouts: 4.53 us -> none  [body(): router_prob[0][:, :, None] * tok_grad[0].astype(jnp.float32)[:, None, :]]
  transfers between devices with their start and end apart: 6 -> 6, of which waited for: 4 -> 4; matrix products, arithmetic and copies ran while one was open for 27% -> 24% of each run, Pallas kernels for 0% -> 0%
where the time goes in v7:
time: 122 us; the launch traced here: 121 us
  starting transfers between devices  35 us (29%)
  waiting for transfers between devices  30.7 us (25%)
  blocking collectives  17 us (14%)
  local copies, waits for them, and re-layouts  13.6 us (11%)
  matrix products  13.6 us (11%)
  other arithmetic  9.82 us (8%)
    all_to_all x1, starting transfers between devices, staged_reduce_scatter(): lax.all_to_all(pieces.astype(jnp.bfloat16), ('zl', 'dp'), 0, 0, tiled=True)  18.4 us
    all_to_all x1, blocking collectives, staged_reduce_scatter(): pieces = lax.all_to_all(pieces.astype(jnp.bfloat16), 'xx', 0, 0, tiled=True)  17 us
    all_to_all x1, waiting for transfers between devices, staged_reduce_scatter(): lax.all_to_all(pieces.astype(jnp.bfloat16), ('zl', 'dp'), 0, 0, tiled=True)  13.1 us
    all_to_all x1, waiting for transfers between devices, body(): lax.all_to_all(outbound, 'exp', split_axis=0, concat_axis=0, tiled=True)  9.16 us
    unnamed x30, local copies, waits for them, and re-layouts  8.19 us
    all_to_all x1, starting transfers between devices, body(): lax.all_to_all(outbound, 'exp', split_axis=0, concat_axis=0, tiled=True)  7.23 us
    ppermute x2, waiting for transfers between devices, passed_along(): return lax.ppermute(value, axis, pairs)  5.13 us
    ppermute x2, starting transfers between devices, passed_along(): return lax.ppermute(value, axis, pairs)  4.11 us
  transfers between devices with their start and end apart: 6, of which 4 were waited for; matrix products, arithmetic and copies ran while one was open for 24% of the time, Pallas kernels for 0%

profile of v7, /device:TPU:64, one launch (start us, length us, event | category | flops | bytes accessed | tf_op | source)
XLA Modules:
  0.0 120.7 jit_solution(10837713076271467268)
XLA Ops:
  0.6 1.7 %pad_maximum_fusion = bf16[2,256,128]{2,1,0:T(8,128)(2,1)} fusion(bf16[1,256,128]{2,1,0:T(8,128)(2,1)} %param.13, bf16[1,256,128]{2,1,0:T(8,128)(2,1)} %param.12), kind=kLoop, calls=%fused_computation.39 | loop fusion | flops 65536 | bytes 262144 | tf_op jit(solution)/shard_map/stack | solution.py:96
  2.3 1.9 %collective-permute-start = (bf16[2,256,128]{2,1,0:T(8,128)(2,1)}, bf16[2,256,128]{2,1,0:T(8,128)(2,1)}, u32[]{:S(2)}, u32[]{:S(2)}) collective-permute-start(bf16[2,256,128]{2,1,0:T(8,128)(2,1)} %pad_maximum_fusion), channel_id=1, source_target_pairs={{0,32},{32,64},{64,96},{96,128},{128,160},{160,192},{192,224},{224... | collective-permute-start | bytes 393224 | tf_op jit(solution)/shard_map/ppermute | solution.py:16
  4.2 0.8 copy.51
  5.3 0.2 select_reduce_fusion.1
  5.6 0.8 copy.52
  6.5 0.7 bitcast_add_fusion
  7.4 2.8 %fusion = bf16[128,6144]{1,0:T(8,128)(2,1)} fusion(pred[128,32]{0,1:T(8,128)(4,1)S(1)} %fusion.27, f32[128]{0:T(128)S(1)} %select_reduce_fusion, bf16[1,32,6144]{2,1,0:T(8,128)(2,1)} %param.17), kind=kOutput, calls=%fused_computation.1 | convolution fusion | flops 51904512 | bytes 1970688 | tf_op jit(solution)/shard_map/dot_general | solution.py:138
  10.2 7.2 %all-to-all-start = ((bf16[8,16,6144]{2,1,0:T(8,128)(2,1)}), bf16[8,16,6144]{2,1,0:T(8,128)(2,1)S(1)}, u32[]{:S(2)}, u32[]{:S(2)}) async-start(bf16[8,16,6144]{2,1,0:T(8,128)(2,1)} %bitcast.100), calls=%async_computation | async-start | bytes 3145728 | tf_op jit(solution)/shard_map/all_to_all | solution.py:142
  17.5 0.7 copy.59
  18.2 1.2 copy.54
  19.4 0.9 copy.55
  20.3 1.9 %copy.56 = bf16[1,256,768]{1,2,0:T(8,128)(2,1)} copy(bf16[1,256,768]{2,1,0:T(8,128)(2,1)} %param.14) | data formatting | bytes 786432 | tf_op args[3]
  22.2 1.2 %copy.57 = bf16[1,6,256,128]{3,2,1,0:T(8,128)(2,1)S(1)} copy(bf16[1,6,256,128]{2,3,1,0:T(8,128)(2,1)} %bitcast.105) | data formatting | bytes 786432 | tf_op jit(solution)/shard_map/transpose | solution.py:89
  23.4 1.5 %bitcast_convert_fusion = f32[128,256]{0,1:T(8,128)} fusion(bf16[1,1,1,128,256]{3,4,2,1,0:T(8,128)(2,1)} %copy.59), kind=kLoop, calls=%fused_computation.47 | loop fusion | flops 32768 | bytes 196608 | tf_op jit(solution)/shard_map/convert_element_type | solution.py:146
  25.0 1.4 %fusion.5 = f32[256,1536]{1,0:T(8,128)S(1)} fusion(bf16[1536,128]{1,0:T(8,128)(2,1)} %bitcast.96, f32[1536]{0:T(1024)S(1)} %sub.50, bf16[2,256,128]{2,1,0:T(8,128)(2,1)} %collective-permute-done), kind=kOutput, calls=%fused_computation.10 | convolution fusion | flops 101449728 | bytes 2037760 | tf_op jit(solution)/shard_map/kqd,kud->kqu/dot_general | solution.py:32
  26.4 1.3 %fusion.7 = bf16[256,1536]{1,0:T(8,128)(2,1)S(1)} fusion(f32[256,1536]{1,0:T(8,128)S(1)} %fusion.5, bf16[1536,128]{1,0:T(8,128)(2,1)S(1)} %bitcast.92, f32[1536]{0:T(1024)S(1)} %sub.53, bf16[2,256,128]{2,1,0:T(8,128)(2,1)} %collective-permute-done), kind=kOutput, calls=%fused_computation.12 | convolution fusion | flops 101842944 | bytes 2824192 | tf_op jit(solution)/shard_map/kqd,kud->kqu/dot_general | solution.py:37
  27.7 0.4 fusion.16
  28.0 0.4 convolution_bitcast_fusion.1
  28.4 0.7 fusion.20
  29.1 3.2 %collective-permute-start.2 = (bf16[2,1,256,128]{3,2,1,0:T(8,128)(2,1)}, bf16[2,1,256,128]{3,2,1,0:T(8,128)(2,1)}, u32[]{:S(2)}, u32[]{:S(2)}) collective-permute-start(bf16[2,1,256,128]{3,2,1,0:T(8,128)(2,1)} %fusion.20), channel_id=1, source_target_pairs={{992,0},{0,32},{32,64},{64,96},{96,128},{128,160},{160,192},{192,2... | collective-permute-start | bytes 393224 | tf_op jit(solution)/shard_map/ppermute | solution.py:22
  32.3 2.2 %collective-permute-start.1 = (bf16[2,256,128]{2,1,0:T(8,128)(2,1)}, bf16[2,256,128]{2,1,0:T(8,128)(2,1)S(1)}, u32[]{:S(2)}, u32[]{:S(2)}) collective-permute-start(bf16[2,256,128]{2,1,0:T(8,128)(2,1)} %collective-permute-done), channel_id=1, source_target_pairs={{0,32},{32,64},{64,96},{96,128},{128,160},{160,192},{192,224},{224... | collective-permute-start | bytes 393224 | tf_op jit(solution)/shard_map/ppermute | solution.py:16
  34.5 1.3 %convolution_multiply_fusion.4 = f32[1536,128]{1,0:T(8,128)S(1)} fusion(bf16[256,1536]{1,0:T(8,128)(2,1)S(1)} %fusion.7, f32[]{:T(128)S(6)} %mul.165, bf16[2,256,128]{2,1,0:T(8,128)(2,1)} %collective-permute-done), kind=kOutput, calls=%fused_computation.15 | convolution fusion | flops 100859904 | bytes 1638404 | tf_op jit(solution)/shard_map/kqu,kud->kqd/dot_general | solution.py:42
  35.8 5.1 %collective-permute-done.1 = bf16[2,256,128]{2,1,0:T(8,128)(2,1)S(1)} collective-permute-done((bf16[2,256,128]{2,1,0:T(8,128)(2,1)}, bf16[2,256,128]{2,1,0:T(8,128)(2,1)S(1)}, u32[]{:S(2)}, u32[]{:S(2)}) %collective-permute-start.1) | collective-permute-done | bytes 131104 | tf_op jit(solution)/shard_map/ppermute | solution.py:16
  40.9 0.4 fusion.6
  41.3 0.4 fusion.8
  41.7 1.0 copy-done.4
  42.7 1.2 fusion.10
  43.8 1.9 %copy.58 = bf16[1,6,256,128]{2,3,1,0:T(8,128)(2,1)} copy(bf16[1,6,256,128]{3,2,1,0:T(8,128)(2,1)} %bitcast.103) | data formatting | bytes 786432 | tf_op jit(solution)/shard_map/convert_element_type | solution.py:116
  45.8 1.9 %convolution_bitcast_fusion = f32[1,1,256,128]{3,2,1,0:T(8,128)S(1)} fusion(bf16[1536,128]{1,0:T(8,128)(2,1)S(1)} %bitcast.95, f32[256,1536]{1,0:T(8,128)} %copy-done.1), kind=kOutput, calls=%fused_computation.24 | convolution fusion | flops 101056512 | bytes 2097152 | tf_op jit(solution)/shard_map/kqu,kqd->kud/dot_general | solution.py:49
  47.6 0.4 fusion.15
  48.0 0.9 fusion.22
  49.0 0.7 slice_bitcast_fusion
  49.6 9.2 %all-to-all-done = bf16[8,16,6144]{2,1,0:T(8,128)(2,1)S(1)} async-done(((bf16[8,16,6144]{2,1,0:T(8,128)(2,1)}), bf16[8,16,6144]{2,1,0:T(8,128)(2,1)S(1)}, u32[]{:S(2)}, u32[]{:S(2)}) %all-to-all-start) | async-done | bytes 1572896 | tf_op jit(solution)/shard_map/all_to_all | solution.py:142
  58.8 0.6 fusion.25
  59.4 0.3 constant_dynamic-slice_fusion
  59.8 0.1 copy.72
  59.9 2.0 %collective-permute-start.3 = (f32[4,4,4,48,128]{4,3,2,1,0:T(8,128)S(1)}, f32[4,4,4,48,128]{4,3,2,1,0:T(8,128)S(1)}, u32[]{:S(2)}, u32[]{:S(2)}) collective-permute-start(f32[4,4,4,48,128]{4,3,2,1,0:T(8,128)S(1)} %bitcast.101), channel_id=1, source_target_pairs={{0,32},{32,0},{1,33},{33,1},{2,34},{34,2},{3,35},{35,3},{4,36},{36... | collective-permute-start | bytes 4718600 | tf_op jit(solution)/shard_map/ppermute | solution.py:63
  62.0 3.3 %collective-permute-done.3 = f32[4,4,4,48,128]{4,3,2,1,0:T(8,128)S(1)} collective-permute-done((f32[4,4,4,48,128]{4,3,2,1,0:T(8,128)S(1)}, f32[4,4,4,48,128]{4,3,2,1,0:T(8,128)S(1)}, u32[]{:S(2)}, u32[]{:S(2)}) %collective-permute-start.3) | collective-permute-done | bytes 1572896 | tf_op jit(solution)/shard_map/ppermute | solution.py:63
  65.2 0.2 fusion.12
  65.4 17.0 %all_to_all.22 = bf16[4,4,4,48,128]{4,3,2,1,0:T(8,128)(2,1)} all-to-all(bf16[4,4,4,48,128]{4,3,2,1,0:T(8,128)(2,1)S(1)} %fusion.12), channel_id=1, replica_groups=mesh['zl'=4,'xx'=4,'core'=2,'exp'=8,'dp'=4] {'xx'}, dimensions={0} | all-to-all | bytes 1572864 | tf_op jit(solution)/shard_map/all_to_all | solution.py:64
  82.4 2.0 %reduce_sum.44 = bf16[4,4,48,128]{3,2,1,0:T(8,128)(2,1)} reduce(bf16[4,4,4,48,128]{4,3,2,1,0:T(8,128)(2,1)} %all_to_all.22, bf16[]{:T(256)} %constant.52.clone.1), dimensions={0}, to_apply=%region_4.5 | reduce | flops 294912 | bytes 983042 | tf_op jit(solution)/shard_map/reduce_sum | solution.py:65
  84.4 18.4 %all-to-all-start.2 = ((bf16[16,48,128]{2,1,0:T(8,128)(2,1)}), bf16[16,48,128]{2,1,0:T(8,128)(2,1)}, u32[]{:S(2)}, u32[]{:S(2)}) async-start(bf16[16,48,128]{2,1,0:T(8,128)(2,1)} %bitcast.106), calls=%async_computation.2 | async-start | bytes 393216 | tf_op jit(solution)/shard_map/all_to_all | solution.py:66
  102.8 0.9 copy.62
  103.8 1.4 %fusion.28 = (bf16[1,1,1,128,128]{3,4,2,1,0:T(8,128)(2,1)S(1)}, bf16[1,1,1,128,128]{3,4,2,1,0:T(8,128)(2,1)S(1)}) fusion(f32[128,256]{0,1:T(8,128)} %bitcast_convert_fusion, bf16[128,6144]{1,0:T(8,128)(2,1)S(1)} %bitcast.91, bf16[1,128,6144]{2,1,0:T(8,128)(2,1)S(1)} %copy-done), kind=kOutput, calls=%fused_computation.62 | convolution fusion | flops 201539584 | bytes 3342336 | tf_op jit(solution)/shard_map/rd,fd->rf/dot_general | solution.py:153
  105.2 0.7 copy.63
  106.0 13.1 %all-to-all-done.2 = bf16[16,48,128]{2,1,0:T(8,128)(2,1)} async-done(((bf16[16,48,128]{2,1,0:T(8,128)(2,1)}), bf16[16,48,128]{2,1,0:T(8,128)(2,1)}, u32[]{:S(2)}, u32[]{:S(2)}) %all-to-all-start.2) | async-done | bytes 196640 | tf_op jit(solution)/shard_map/all_to_all | solution.py:66
  119.1 1.0 convert_reduce_fusion
  120.1 0.6 multiply_bitcast_fusion
  (37 shorter events, 0.8 us)
Async XLA Ops:
  0.6 103.1 %copy-start = (bf16[1,128,6144]{2,1,0:T(8,128)(2,1)S(1)}, bf16[1,128,6144]{2,1,0:T(8,128)(2,1)}, u32[]{:S(2)}) copy-start(bf16[1,128,6144]{2,1,0:T(8,128)(2,1)} %param.21) | copy-start | bytes 4718596
  2.3 22.7 %collective-permute-start = (bf16[2,256,128]{2,1,0:T(8,128)(2,1)}, bf16[2,256,128]{2,1,0:T(8,128)(2,1)}, u32[]{:S(2)}, u32[]{:S(2)}) collective-permute-start(bf16[2,256,128]{2,1,0:T(8,128)(2,1)} %pad_maximum_fusion), channel_id=1, source_target_pairs={{0,32},{32,64},{64,96},{96,128},{128,160},{160,192},{192,224},{224... | collective-permute-start | bytes 393224 | tf_op jit(solution)/shard_map/ppermute | solution.py:16
  10.2 7.2 %copy-start.9 = (f32[1,6,256]{2,0,1:T(1,128)S(1)}, f32[1,6,256]{2,0,1:T(1,128)}, u32[]{:S(2)}) copy-start(f32[1,6,256]{2,0,1:T(1,128)} %param.15) | copy-start | bytes 18436
  10.2 7.3 %copy-start.10 = (f32[1,6,256]{2,0,1:T(1,128)S(1)}, f32[1,6,256]{2,0,1:T(1,128)}, u32[]{:S(2)}) copy-start(f32[1,6,256]{2,0,1:T(1,128)} %param.16) | copy-start | bytes 18436
  10.2 7.3 %copy-start.8 = (bf16[1,1,1,128,256]{4,3,2,1,0:T(8,128)(2,1)S(1)}, bf16[1,1,1,128,256]{4,3,2,1,0:T(8,128)(2,1)}, u32[]{:S(2)}) copy-start(bf16[1,1,1,128,256]{4,3,2,1,0:T(8,128)(2,1)} %param.20) | copy-start | bytes 196612
  10.2 48.6 %all-to-all-start = ((bf16[8,16,6144]{2,1,0:T(8,128)(2,1)}), bf16[8,16,6144]{2,1,0:T(8,128)(2,1)S(1)}, u32[]{:S(2)}, u32[]{:S(2)}) async-start(bf16[8,16,6144]{2,1,0:T(8,128)(2,1)} %bitcast.100), calls=%async_computation | async-start | bytes 3145728 | tf_op jit(solution)/shard_map/all_to_all | solution.py:142
  26.4 1.3 %copy-start.2 = (bf16[1,6,256,128]{3,2,1,0:T(8,128)(2,1)S(1)}, bf16[1,6,256,128]{3,2,1,0:T(8,128)(2,1)}, u32[]{:S(2)}) copy-start(bf16[1,6,256,128]{3,2,1,0:T(8,128)(2,1)} %copy.55) | copy-start | bytes 1179652
  29.1 18.9 %collective-permute-start.2 = (bf16[2,1,256,128]{3,2,1,0:T(8,128)(2,1)}, bf16[2,1,256,128]{3,2,1,0:T(8,128)(2,1)}, u32[]{:S(2)}, u32[]{:S(2)}) collective-permute-start(bf16[2,1,256,128]{3,2,1,0:T(8,128)(2,1)} %fusion.20), channel_id=1, source_target_pairs={{992,0},{0,32},{32,64},{64,96},{96,128},{128,160},{160,192},{192,2... | collective-permute-start | bytes 393224 | tf_op jit(solution)/shard_map/ppermute | solution.py:22
  32.3 8.6 %collective-permute-start.1 = (bf16[2,256,128]{2,1,0:T(8,128)(2,1)}, bf16[2,256,128]{2,1,0:T(8,128)(2,1)S(1)}, u32[]{:S(2)}, u32[]{:S(2)}) collective-permute-start(bf16[2,256,128]{2,1,0:T(8,128)(2,1)} %collective-permute-done), channel_id=1, source_target_pairs={{0,32},{32,64},{64,96},{96,128},{128,160},{160,192},{192,224},{224... | collective-permute-start | bytes 393224 | tf_op jit(solution)/shard_map/ppermute | solution.py:16
  41.3 2.6 %copy-start.1 = (f32[256,1536]{1,0:T(8,128)}, f32[256,1536]{1,0:T(8,128)S(1)}, u32[]{:S(2)}) copy-start(f32[256,1536]{1,0:T(8,128)S(1)} %fusion.6) | copy-start | bytes 4718596
  41.7 1.0 copy-start.4
  45.8 1.9 %copy-start.3 = (bf16[1,6,256,128]{3,2,1,0:T(8,128)(2,1)S(1)}, bf16[1,6,256,128]{3,2,1,0:T(8,128)(2,1)}, u32[]{:S(2)}) copy-start(bf16[1,6,256,128]{3,2,1,0:T(8,128)(2,1)} %copy.55) | copy-start | bytes 1179652
  45.8 1.9 %copy-start.5 = (bf16[256,1536]{1,0:T(8,128)(2,1)S(1)}, bf16[256,1536]{1,0:T(8,128)(2,1)}, u32[]{:S(2)}) copy-start(bf16[256,1536]{1,0:T(8,128)(2,1)} %copy-done.4) | copy-start | bytes 2359300
  47.6 11.2 %copy-start.7 = (f32[128,256]{0,1:T(8,128)S(1)}, f32[128,256]{0,1:T(8,128)}, u32[]{:S(2)}) copy-start(f32[128,256]{0,1:T(8,128)} %bitcast_convert_fusion) | copy-start | bytes 393220
  59.9 5.3 %collective-permute-start.3 = (f32[4,4,4,48,128]{4,3,2,1,0:T(8,128)S(1)}, f32[4,4,4,48,128]{4,3,2,1,0:T(8,128)S(1)}, u32[]{:S(2)}, u32[]{:S(2)}) collective-permute-start(f32[4,4,4,48,128]{4,3,2,1,0:T(8,128)S(1)} %bitcast.101), channel_id=1, source_target_pairs={{0,32},{32,0},{1,33},{33,1},{2,34},{34,2},{3,35},{35,3},{4,36},{36... | collective-permute-start | bytes 4718600 | tf_op jit(solution)/shard_map/ppermute | solution.py:63
  65.4 37.4 %copy-start.6 = (bf16[1,6,256,128]{2,3,1,0:T(8,128)(2,1)S(1)}, bf16[1,6,256,128]{2,3,1,0:T(8,128)(2,1)}, u32[]{:S(2)}) copy-start(bf16[1,6,256,128]{2,3,1,0:T(8,128)(2,1)} %copy.58) | copy-start | bytes 1179652
  84.4 34.7 %all-to-all-start.2 = ((bf16[16,48,128]{2,1,0:T(8,128)(2,1)}), bf16[16,48,128]{2,1,0:T(8,128)(2,1)}, u32[]{:S(2)}, u32[]{:S(2)}) async-start(bf16[16,48,128]{2,1,0:T(8,128)(2,1)} %bitcast.106), calls=%async_computation.2 | async-start | bytes 393216 | tf_op jit(solution)/shard_map/all_to_all | solution.py:66

commit v8 on v7

--- a/solution.py
+++ b/solution.py
@@ -80,6 +80,27 @@
     saved_pre,
     w_down,
 ):
+    expert_count = lax.axis_size("exp")
+    capacity = saved_pre.shape[3] // expert_count
+    model_width = tok_grad.shape[2]
+    pair_count = tok_grad.shape[1] * 2
+    flat_ids = expert_ids[0].reshape(pair_count)
+    matches = (flat_ids[:, None] == jnp.arange(expert_count, dtype=jnp.int32)[None, :]).astype(
+        jnp.int32
+    )
+    earlier = jnp.cumsum(matches, axis=0) - matches
+    place = jnp.sum(earlier * matches, axis=1)
+    slot_index = flat_ids * capacity + place
+    hit = jnp.arange(expert_count * capacity, dtype=jnp.int32)[:, None] == slot_index[None, :]
+    token_table = hit.reshape(expert_count * capacity, pair_count // 2, 2).any(axis=2)
+    slot_prob = jnp.sum(jnp.where(hit, router_prob[0].reshape(pair_count)[None, :], 0.0), axis=1)
+    picked = jnp.dot(
+        token_table.astype(jnp.bfloat16), tok_grad[0], preferred_element_type=jnp.float32
+    )
+    outbound = (slot_prob[:, None] * picked).astype(jnp.bfloat16)
+    outbound, queries, key_rows, value_rows, out_grad, log_norm, row_delta = lax.optimization_barrier(
+        (outbound, queries, key_rows, value_rows, out_grad, log_norm, row_delta)
+    )
     length = queries.shape[1]
     head_sets = key_rows.shape[2] // HEAD_DIM
     group_size = HEADS // KV_HEADS
@@ -121,24 +142,6 @@
     )
     key_grad = both_total[0].transpose(1, 0, 2).reshape(1, length, head_sets * HEAD_DIM)
     value_grad = both_total[1].transpose(1, 0, 2).reshape(1, length, head_sets * HEAD_DIM)
-    expert_count = lax.axis_size("exp")
-    capacity = saved_pre.shape[3] // expert_count
-    model_width = tok_grad.shape[2]
-    pair_count = tok_grad.shape[1] * 2
-    flat_ids = expert_ids[0].reshape(pair_count)
-    matches = (flat_ids[:, None] == jnp.arange(expert_count, dtype=jnp.int32)[None, :]).astype(
-        jnp.int32
-    )
-    earlier = jnp.cumsum(matches, axis=0) - matches
-    place = jnp.sum(earlier * matches, axis=1)
-    slot_index = flat_ids * capacity + place
-    hit = jnp.arange(expert_count * capacity, dtype=jnp.int32)[:, None] == slot_index[None, :]
-    token_table = hit.reshape(expert_count * capacity, pair_count // 2, 2).any(axis=2)
-    slot_prob = jnp.sum(jnp.where(hit, router_prob[0].reshape(pair_count)[None, :], 0.0), axis=1)
-    picked = jnp.dot(
-        token_table.astype(jnp.bfloat16), tok_grad[0], preferred_element_type=jnp.float32
-    )
-    outbound = (slot_prob[:, None] * picked).astype(jnp.bfloat16)
     incoming_block = lax.all_to_all(outbound, "exp", split_axis=0, concat_axis=0, tiled=True)
     incoming_block, query_grad, key_grad, value_grad = lax.optimization_barrier(
         (incoming_block, query_grad, key_grad, value_grad)

time: 122 us -> 117 us (0.959)
  waiting for transfers between devices: 30.7 us -> 26.6 us
    all_to_all x1, waiting for transfers between devices: 9.16 us -> 4.59 us  [body(): lax.all_to_all(outbound, 'exp', split_axis=0, concat_axis=0, tiled=True)]
    optimization_barrier x0 -> x2, local copies, waits for them, and re-layouts: none -> 3.07 us  [body(): lax.optimization_barrier((outbound, queries, key_rows, value_rows, out_gr...]
    unnamed x30 -> x32, local copies, waits for them, and re-layouts: 8.19 us -> 5.23 us
  transfers between devices with their start and end apart: 6 -> 6, of which waited for: 4 -> 4; matrix products, arithmetic and copies ran while one was open for 24% -> 21% of each run, Pallas kernels for 0% -> 0%
where the time goes in v8:
time: 117 us; the launch traced here: 116 us
  starting transfers between devices  34.9 us (30%)
  waiting for transfers between devices  26.6 us (23%)
  blocking collectives  16.9 us (14%)
  matrix products  13.8 us (12%)
  local copies, waits for them, and re-layouts  13.7 us (12%)
  other arithmetic  8.87 us (8%)
    all_to_all x1, starting transfers between devices, staged_reduce_scatter(): lax.all_to_all(pieces.astype(jnp.bfloat16), ('zl', 'dp'), 0, 0, tiled=True)  18.4 us
    all_to_all x1, blocking collectives, staged_reduce_scatter(): pieces = lax.all_to_all(pieces.astype(jnp.bfloat16), 'xx', 0, 0, tiled=True)  16.9 us
    all_to_all x1, waiting for transfers between devices, staged_reduce_scatter(): lax.all_to_all(pieces.astype(jnp.bfloat16), ('zl', 'dp'), 0, 0, tiled=True)  13.1 us
    all_to_all x1, starting transfers between devices, body(): lax.all_to_all(outbound, 'exp', split_axis=0, concat_axis=0, tiled=True)  7.24 us
    ppermute x2, waiting for transfers between devices, passed_along(): return lax.ppermute(value, axis, pairs)  5.46 us
    unnamed x32, local copies, waits for them, and re-layouts  5.23 us
    all_to_all x1, waiting for transfers between devices, body(): lax.all_to_all(outbound, 'exp', split_axis=0, concat_axis=0, tiled=True)  4.59 us
    ppermute x2, starting transfers between devices, passed_along(): return lax.ppermute(value, axis, pairs)  3.83 us
  transfers between devices with their start and end apart: 6, of which 4 were waited for; matrix products, arithmetic and copies ran while one was open for 21% of the time, Pallas kernels for 0%

profile of v8, /device:TPU:64, one launch (start us, length us, event | category | flops | bytes accessed | tf_op | source)
XLA Modules:
  0.0 115.7 jit_solution(5495946198068392164)
XLA Ops:
  0.6 0.9 copy.51
  1.8 0.2 select_reduce_fusion.1
  2.1 0.8 copy.52
  3.1 0.7 bitcast_add_fusion
  3.9 2.8 %fusion = bf16[128,6144]{1,0:T(8,128)(2,1)} fusion(pred[128,32]{0,1:T(8,128)(4,1)S(1)} %fusion.27, f32[128]{0:T(128)S(1)} %select_reduce_fusion, bf16[1,32,6144]{2,1,0:T(8,128)(2,1)} %param.17), kind=kOutput, calls=%fused_computation.1 | convolution fusion | flops 51904512 | bytes 1970688 | tf_op jit(solution)/shard_map/dot_general | solution.py:97
  6.7 7.2 %all-to-all-start = ((bf16[8,16,6144]{2,1,0:T(8,128)(2,1)}), bf16[8,16,6144]{2,1,0:T(8,128)(2,1)S(1)}, u32[]{:S(2)}, u32[]{:S(2)}) async-start(bf16[8,16,6144]{2,1,0:T(8,128)(2,1)} %bitcast.100), calls=%async_computation | async-start | bytes 3145728 | tf_op jit(solution)/shard_map/all_to_all | solution.py:145
  14.0 0.7 pad_maximum_fusion
  14.7 1.9 %collective-permute-start = (bf16[2,256,128]{2,1,0:T(8,128)(2,1)}, bf16[2,256,128]{2,1,0:T(8,128)(2,1)}, u32[]{:S(2)}, u32[]{:S(2)}) collective-permute-start(bf16[2,256,128]{2,1,0:T(8,128)(2,1)} %pad_maximum_fusion), channel_id=1, source_target_pairs={{0,32},{32,64},{64,96},{96,128},{128,160},{160,192},{192,224},{224... | collective-permute-start | bytes 393224 | tf_op jit(solution)/shard_map/ppermute | solution.py:16
  16.6 0.7 copy.59
  17.4 1.2 %copy.54 = bf16[1,256,768]{1,2,0:T(8,128)(2,1)S(1)} copy(bf16[1,256,768]{2,1,0:T(8,128)(2,1)} %param.11) | data formatting | bytes 786432 | tf_op jit(solution)/shard_map/optimization_barrier | solution.py:101
  18.6 0.9 copy.55
  19.5 1.9 %copy.56 = bf16[1,256,768]{1,2,0:T(8,128)(2,1)} copy(bf16[1,256,768]{2,1,0:T(8,128)(2,1)} %param.14) | data formatting | bytes 786432 | tf_op jit(solution)/shard_map/optimization_barrier | solution.py:101
  21.4 1.2 %copy.57 = bf16[1,6,256,128]{3,2,1,0:T(8,128)(2,1)S(1)} copy(bf16[1,6,256,128]{2,3,1,0:T(8,128)(2,1)} %bitcast.105) | data formatting | bytes 786432 | tf_op jit(solution)/shard_map/transpose | solution.py:110
  22.7 1.5 %bitcast_convert_fusion = f32[128,256]{0,1:T(8,128)} fusion(bf16[1,1,1,128,256]{3,4,2,1,0:T(8,128)(2,1)} %copy.59), kind=kLoop, calls=%fused_computation.47 | loop fusion | flops 32768 | bytes 196608 | tf_op jit(solution)/shard_map/convert_element_type | solution.py:149
  24.2 1.4 %fusion.5 = f32[1536,256]{1,0:T(8,128)S(1)} fusion(bf16[1536,128]{1,0:T(8,128)(2,1)} %bitcast.96, f32[1536]{0:T(1024)S(1)} %sub.46, bf16[2,256,128]{2,1,0:T(8,128)(2,1)} %collective-permute-done), kind=kOutput, calls=%fused_computation.10 | convolution fusion | flops 101449728 | bytes 2037760 | tf_op jit(solution)/shard_map/kqd,kud->kqu/dot_general | solution.py:32
  25.6 1.3 %fusion.7 = bf16[1536,256]{1,0:T(8,128)(2,1)S(1)} fusion(f32[1536,256]{1,0:T(8,128)S(1)} %fusion.5, bf16[1536,128]{1,0:T(8,128)(2,1)S(1)} %bitcast.92, f32[1536]{0:T(1024)S(1)} %sub.49, bf16[2,256,128]{2,1,0:T(8,128)(2,1)} %collective-permute-done), kind=kOutput, calls=%fused_computation.12 | convolution fusion | flops 101842944 | bytes 2824192 | tf_op jit(solution)/shard_map/kqd,kud->kqu/dot_general | solution.py:37
  26.9 0.4 fusion.16
  27.3 0.4 convolution_bitcast_fusion.1
  27.7 0.7 fusion.20
  28.4 3.5 %collective-permute-start.2 = (bf16[2,1,256,128]{3,2,1,0:T(8,128)(2,1)}, bf16[2,1,256,128]{3,2,1,0:T(8,128)(2,1)}, u32[]{:S(2)}, u32[]{:S(2)}) collective-permute-start(bf16[2,1,256,128]{3,2,1,0:T(8,128)(2,1)} %fusion.20), channel_id=1, source_target_pairs={{992,0},{0,32},{32,64},{64,96},{96,128},{128,160},{160,192},{192,2... | collective-permute-start | bytes 393224 | tf_op jit(solution)/shard_map/ppermute | solution.py:22
  31.9 1.9 %collective-permute-start.1 = (bf16[2,256,128]{2,1,0:T(8,128)(2,1)}, bf16[2,256,128]{2,1,0:T(8,128)(2,1)S(1)}, u32[]{:S(2)}, u32[]{:S(2)}) collective-permute-start(bf16[2,256,128]{2,1,0:T(8,128)(2,1)} %collective-permute-done), channel_id=1, source_target_pairs={{0,32},{32,64},{64,96},{96,128},{128,160},{160,192},{192,224},{224... | collective-permute-start | bytes 393224 | tf_op jit(solution)/shard_map/ppermute | solution.py:16
  33.8 1.2 %convolution_multiply_fusion.4 = f32[1536,128]{1,0:T(8,128)S(1)} fusion(bf16[1536,256]{1,0:T(8,128)(2,1)S(1)} %fusion.7, f32[]{:T(128)S(6)} %mul.156, bf16[2,256,128]{2,1,0:T(8,128)(2,1)} %collective-permute-done), kind=kOutput, calls=%fused_computation.15 | convolution fusion | flops 100859904 | bytes 1638404 | tf_op jit(solution)/shard_map/kqu,kud->kqd/dot_general | solution.py:42
  35.1 5.5 %collective-permute-done.1 = bf16[2,256,128]{2,1,0:T(8,128)(2,1)S(1)} collective-permute-done((bf16[2,256,128]{2,1,0:T(8,128)(2,1)}, bf16[2,256,128]{2,1,0:T(8,128)(2,1)S(1)}, u32[]{:S(2)}, u32[]{:S(2)}) %collective-permute-start.1) | collective-permute-done | bytes 131104 | tf_op jit(solution)/shard_map/ppermute | solution.py:16
  40.5 0.4 fusion.6
  40.9 0.4 fusion.8
  41.3 1.0 copy-done.4
  42.3 1.1 fusion.10
  43.4 1.9 %copy.58 = bf16[1,6,256,128]{2,3,1,0:T(8,128)(2,1)} copy(bf16[1,6,256,128]{3,2,1,0:T(8,128)(2,1)} %bitcast.103) | data formatting | bytes 786432 | tf_op jit(solution)/shard_map/convert_element_type | solution.py:137
  45.4 1.9 %convolution_bitcast_fusion = f32[1,1,256,128]{3,2,1,0:T(8,128)S(1)} fusion(bf16[1536,128]{1,0:T(8,128)(2,1)S(1)} %bitcast.95, f32[1536,256]{1,0:T(8,128)} %copy-done.1), kind=kOutput, calls=%fused_computation.24 | convolution fusion | flops 101056512 | bytes 2097152 | tf_op jit(solution)/shard_map/kqu,kqd->kud/dot_general | solution.py:49
  47.3 0.4 fusion.15
  47.7 0.9 fusion.22
  48.7 0.7 slice_bitcast_fusion
  49.3 4.6 %all-to-all-done = bf16[8,16,6144]{2,1,0:T(8,128)(2,1)S(1)} async-done(((bf16[8,16,6144]{2,1,0:T(8,128)(2,1)}), bf16[8,16,6144]{2,1,0:T(8,128)(2,1)S(1)}, u32[]{:S(2)}, u32[]{:S(2)}) %all-to-all-start) | async-done | bytes 1572896 | tf_op jit(solution)/shard_map/all_to_all | solution.py:145
  53.9 0.6 fusion.25
  54.6 0.3 constant_dynamic-slice_fusion
  54.9 0.1 copy.72
  55.1 1.9 %collective-permute-start.3 = (f32[4,4,4,48,128]{4,3,2,1,0:T(8,128)S(1)}, f32[4,4,4,48,128]{4,3,2,1,0:T(8,128)S(1)}, u32[]{:S(2)}, u32[]{:S(2)}) collective-permute-start(f32[4,4,4,48,128]{4,3,2,1,0:T(8,128)S(1)} %bitcast.101), channel_id=1, source_target_pairs={{0,32},{32,0},{1,33},{33,1},{2,34},{34,2},{3,35},{35,3},{4,36},{36... | collective-permute-start | bytes 4718600 | tf_op jit(solution)/shard_map/ppermute | solution.py:63
  57.0 3.4 %collective-permute-done.3 = f32[4,4,4,48,128]{4,3,2,1,0:T(8,128)S(1)} collective-permute-done((f32[4,4,4,48,128]{4,3,2,1,0:T(8,128)S(1)}, f32[4,4,4,48,128]{4,3,2,1,0:T(8,128)S(1)}, u32[]{:S(2)}, u32[]{:S(2)}) %collective-permute-start.3) | collective-permute-done | bytes 1572896 | tf_op jit(solution)/shard_map/ppermute | solution.py:63
  60.4 0.2 fusion.12
  60.6 16.9 %all_to_all.22 = bf16[4,4,4,48,128]{4,3,2,1,0:T(8,128)(2,1)} all-to-all(bf16[4,4,4,48,128]{4,3,2,1,0:T(8,128)(2,1)S(1)} %fusion.12), channel_id=1, replica_groups=mesh['zl'=4,'xx'=4,'core'=2,'exp'=8,'dp'=4] {'xx'}, dimensions={0} | all-to-all | bytes 1572864 | tf_op jit(solution)/shard_map/all_to_all | solution.py:64
  77.5 2.0 %reduce_sum.44 = bf16[4,4,48,128]{3,2,1,0:T(8,128)(2,1)} reduce(bf16[4,4,4,48,128]{4,3,2,1,0:T(8,128)(2,1)} %all_to_all.22, bf16[]{:T(256)} %constant.52.clone.1), dimensions={0}, to_apply=%region_4.5 | reduce | flops 294912 | bytes 983042 | tf_op jit(solution)/shard_map/reduce_sum | solution.py:65
  79.5 18.4 %all-to-all-start.2 = ((bf16[16,48,128]{2,1,0:T(8,128)(2,1)}), bf16[16,48,128]{2,1,0:T(8,128)(2,1)}, u32[]{:S(2)}, u32[]{:S(2)}) async-start(bf16[16,48,128]{2,1,0:T(8,128)(2,1)} %bitcast.106), calls=%async_computation.2 | async-start | bytes 393216 | tf_op jit(solution)/shard_map/all_to_all | solution.py:66
  97.9 0.9 copy.62
  98.8 1.4 %fusion.28 = (bf16[1,1,1,128,128]{3,4,2,1,0:T(8,128)(2,1)S(1)}, bf16[1,1,1,128,128]{3,4,2,1,0:T(8,128)(2,1)S(1)}) fusion(f32[128,256]{0,1:T(8,128)} %bitcast_convert_fusion, bf16[128,6144]{1,0:T(8,128)(2,1)S(1)} %bitcast.91, bf16[1,128,6144]{2,1,0:T(8,128)(2,1)S(1)} %copy-done), kind=kOutput, calls=%fused_computation.62 | convolution fusion | flops 201539584 | bytes 3342336 | tf_op jit(solution)/shard_map/rd,fd->rf/dot_general | solution.py:156
  100.3 0.7 copy.63
  101.0 13.1 %all-to-all-done.2 = bf16[16,48,128]{2,1,0:T(8,128)(2,1)} async-done(((bf16[16,48,128]{2,1,0:T(8,128)(2,1)}), bf16[16,48,128]{2,1,0:T(8,128)(2,1)}, u32[]{:S(2)}, u32[]{:S(2)}) %all-to-all-start.2) | async-done | bytes 196640 | tf_op jit(solution)/shard_map/all_to_all | solution.py:66
  114.2 1.0 convert_reduce_fusion
  115.1 0.6 multiply_bitcast_fusion
  (41 shorter events, 0.9 us)
Async XLA Ops:
  0.6 98.2 %copy-start = (bf16[1,128,6144]{2,1,0:T(8,128)(2,1)S(1)}, bf16[1,128,6144]{2,1,0:T(8,128)(2,1)}, u32[]{:S(2)}) copy-start(bf16[1,128,6144]{2,1,0:T(8,128)(2,1)} %param.21) | copy-start | bytes 4718596
  6.7 7.3 %copy-start.9 = (bf16[1,256,128]{2,1,0:T(8,128)(2,1)S(1)}, bf16[1,256,128]{2,1,0:T(8,128)(2,1)}, u32[]{:S(2)}) copy-start(bf16[1,256,128]{2,1,0:T(8,128)(2,1)} %param.13) | copy-start | bytes 196612
  6.7 7.3 %copy-start.10 = (bf16[1,256,128]{2,1,0:T(8,128)(2,1)S(1)}, bf16[1,256,128]{2,1,0:T(8,128)(2,1)}, u32[]{:S(2)}) copy-start(bf16[1,256,128]{2,1,0:T(8,128)(2,1)} %param.12) | copy-start | bytes 196612
  6.7 9.9 %copy-start.8 = (bf16[1,1,1,128,256]{4,3,2,1,0:T(8,128)(2,1)S(1)}, bf16[1,1,1,128,256]{4,3,2,1,0:T(8,128)(2,1)}, u32[]{:S(2)}) copy-start(bf16[1,1,1,128,256]{4,3,2,1,0:T(8,128)(2,1)} %param.20) | copy-start | bytes 196612
  6.7 10.6 %copy-start.11 = (f32[1,6,256]{2,0,1:T(1,128)S(1)}, f32[1,6,256]{2,0,1:T(1,128)}, u32[]{:S(2)}) copy-start(f32[1,6,256]{2,0,1:T(1,128)} %param.15) | copy-start | bytes 18436
  6.7 10.7 %copy-start.12 = (f32[1,6,256]{2,0,1:T(1,128)S(1)}, f32[1,6,256]{2,0,1:T(1,128)}, u32[]{:S(2)}) copy-start(f32[1,6,256]{2,0,1:T(1,128)} %param.16) | copy-start | bytes 18436
  6.7 47.2 %all-to-all-start = ((bf16[8,16,6144]{2,1,0:T(8,128)(2,1)}), bf16[8,16,6144]{2,1,0:T(8,128)(2,1)S(1)}, u32[]{:S(2)}, u32[]{:S(2)}) async-start(bf16[8,16,6144]{2,1,0:T(8,128)(2,1)} %bitcast.100), calls=%async_computation | async-start | bytes 3145728 | tf_op jit(solution)/shard_map/all_to_all | solution.py:145
  14.7 9.5 %collective-permute-start = (bf16[2,256,128]{2,1,0:T(8,128)(2,1)}, bf16[2,256,128]{2,1,0:T(8,128)(2,1)}, u32[]{:S(2)}, u32[]{:S(2)}) collective-permute-start(bf16[2,256,128]{2,1,0:T(8,128)(2,1)} %pad_maximum_fusion), channel_id=1, source_target_pairs={{0,32},{32,64},{64,96},{96,128},{128,160},{160,192},{192,224},{224... | collective-permute-start | bytes 393224 | tf_op jit(solution)/shard_map/ppermute | solution.py:16
  25.6 1.3 %copy-start.2 = (bf16[1,6,256,128]{3,2,1,0:T(8,128)(2,1)S(1)}, bf16[1,6,256,128]{3,2,1,0:T(8,128)(2,1)}, u32[]{:S(2)}) copy-start(bf16[1,6,256,128]{3,2,1,0:T(8,128)(2,1)} %copy.55) | copy-start | bytes 1179652
  28.4 19.3 %collective-permute-start.2 = (bf16[2,1,256,128]{3,2,1,0:T(8,128)(2,1)}, bf16[2,1,256,128]{3,2,1,0:T(8,128)(2,1)}, u32[]{:S(2)}, u32[]{:S(2)}) collective-permute-start(bf16[2,1,256,128]{3,2,1,0:T(8,128)(2,1)} %fusion.20), channel_id=1, source_target_pairs={{992,0},{0,32},{32,64},{64,96},{96,128},{128,160},{160,192},{192,2... | collective-permute-start | bytes 393224 | tf_op jit(solution)/shard_map/ppermute | solution.py:22
  31.9 8.6 %collective-permute-start.1 = (bf16[2,256,128]{2,1,0:T(8,128)(2,1)}, bf16[2,256,128]{2,1,0:T(8,128)(2,1)S(1)}, u32[]{:S(2)}, u32[]{:S(2)}) collective-permute-start(bf16[2,256,128]{2,1,0:T(8,128)(2,1)} %collective-permute-done), channel_id=1, source_target_pairs={{0,32},{32,64},{64,96},{96,128},{128,160},{160,192},{192,224},{224... | collective-permute-start | bytes 393224 | tf_op jit(solution)/shard_map/ppermute | solution.py:16
  40.9 2.5 %copy-start.1 = (f32[1536,256]{1,0:T(8,128)}, f32[1536,256]{1,0:T(8,128)S(1)}, u32[]{:S(2)}) copy-start(f32[1536,256]{1,0:T(8,128)S(1)} %fusion.6) | copy-start | bytes 4718596
  41.3 1.0 copy-start.4
  45.4 1.9 %copy-start.3 = (bf16[1,6,256,128]{3,2,1,0:T(8,128)(2,1)S(1)}, bf16[1,6,256,128]{3,2,1,0:T(8,128)(2,1)}, u32[]{:S(2)}) copy-start(bf16[1,6,256,128]{3,2,1,0:T(8,128)(2,1)} %copy.55) | copy-start | bytes 1179652
  45.4 1.9 %copy-start.5 = (bf16[1536,256]{1,0:T(8,128)(2,1)S(1)}, bf16[1536,256]{1,0:T(8,128)(2,1)}, u32[]{:S(2)}) copy-start(bf16[1536,256]{1,0:T(8,128)(2,1)} %copy-done.4) | copy-start | bytes 2359300
  47.3 6.6 %copy-start.7 = (f32[128,256]{0,1:T(8,128)S(1)}, f32[128,256]{0,1:T(8,128)}, u32[]{:S(2)}) copy-start(f32[128,256]{0,1:T(8,128)} %bitcast_convert_fusion) | copy-start | bytes 393220
  55.1 5.3 %collective-permute-start.3 = (f32[4,4,4,48,128]{4,3,2,1,0:T(8,128)S(1)}, f32[4,4,4,48,128]{4,3,2,1,0:T(8,128)S(1)}, u32[]{:S(2)}, u32[]{:S(2)}) collective-permute-start(f32[4,4,4,48,128]{4,3,2,1,0:T(8,128)S(1)} %bitcast.101), channel_id=1, source_target_pairs={{0,32},{32,0},{1,33},{33,1},{2,34},{34,2},{3,35},{35,3},{4,36},{36... | collective-permute-start | bytes 4718600 | tf_op jit(solution)/shard_map/ppermute | solution.py:63
  60.6 37.3 %copy-start.6 = (bf16[1,6,256,128]{2,3,1,0:T(8,128)(2,1)S(1)}, bf16[1,6,256,128]{2,3,1,0:T(8,128)(2,1)}, u32[]{:S(2)}) copy-start(bf16[1,6,256,128]{2,3,1,0:T(8,128)(2,1)} %copy.58) | copy-start | bytes 1179652
  79.5 34.7 %all-to-all-start.2 = ((bf16[16,48,128]{2,1,0:T(8,128)(2,1)}), bf16[16,48,128]{2,1,0:T(8,128)(2,1)}, u32[]{:S(2)}, u32[]{:S(2)}) async-start(bf16[16,48,128]{2,1,0:T(8,128)(2,1)} %bitcast.106), calls=%async_computation.2 | async-start | bytes 393216 | tf_op jit(solution)/shard_map/all_to_all | solution.py:66
